TPU v7x, 512 devices: a whole 4x4x16 slice. The times are simulated.
512 devices in a mesh: tok: 16 (over z), head: 32 (over y, x, core).
Axes of the slice: x: 4, y: 4, z: 16, core: 2. Of those that a mesh axis runs over, the one named last changes fastest.
Arguments:
- tokens: bfloat16 [3072, 4096], P(('tok', 'head')), may hold values from -6 to 6
- ln1_gain: float32 [4096], replicated, may hold values from 0.25 to 1.75
- ln1_bias: float32 [4096], replicated, may hold values from -1.75 to 1.75
- ln2_gain: float32 [4096], replicated, may hold values from 0.25 to 1.75
- ln2_bias: float32 [4096], replicated, may hold values from -1.75 to 1.75
- w_qkv: bfloat16 [4096, 12288], P('tok', 'head'), may hold values from -0.09375 to 0.09375
- b_qkv: float32 [12288], P('head'), may hold values from -3 to 3
- w_dense: bfloat16 [4096, 4096], P('head', 'tok'), may hold values from -0.09375 to 0.09375
- b_dense: float32 [4096], replicated, may hold values from -1.75 to 1.75
- w_up: bfloat16 [4096, 16384], P('tok', 'head'), may hold values from -0.09375 to 0.09375
- b_up: float32 [16384], P('head'), may hold values from -3 to 3
- w_down: bfloat16 [16384, 4096], P('head', 'tok'), may hold values from -0.046875 to 0.046875
- b_down: float32 [4096], replicated, may hold values from -1.75 to 1.75
- k_cache: bfloat16 [98304, 4096], P('tok', 'head'), may hold values from -610 to 610
- v_cache: bfloat16 [98304, 4096], P('tok', 'head'), may hold values from -6 to 6
- cache_lengths: int32 [16, 33], P('tok'), may hold values from 1 to 4096, 6144 in all within a row
Outputs:
- mixed: bfloat16 [3072, 4096], P(('tok', 'head'))
Inputs may be any that keep to these rules, and one draw needn't show every extreme that they name: `cache_lengths`: row g lists the cache lengths of group g's 33 requests in the order in which their caches lie in the group's 6144 cache rows; every row sums to 6144. Request 0 of a group is the one whose 160 new tokens are prefilled, the others decode one token each.
All inputs are finite; a program needn't handle non-finite values.
Results may differ from a plain program's by a relative error of at most 0.02.
Values may be sent and summed in bfloat16 or wider, within the bound.
No kernel may reach another device: no remote copies, remote signals or barrier semaphores. Data moves between devices by JAX's collectives and lax.ppermute only.
A program may use at most 64 MiB of HBM per device.

v0:
```python
import jax
import jax.numpy as jnp
from jax import lax
from jax.sharding import PartitionSpec as P

HD = 128
ROT = 32
WINDOW = 2048
SINKS = 4


epsilon = 1e-05


def layer_norm(values, gain, shift):
    values = values.astype(jnp.float32)
    center = jnp.mean(values, axis=-1, keepdims=True)
    spread = jnp.mean(jnp.square(values - center), axis=-1, keepdims=True)
    return (values - center) * lax.rsqrt(spread + epsilon) * gain + shift


def rotate(values, positions):
    half = ROT // 2
    inverse = jnp.power(jnp.float32(10000.0), -jnp.arange(half, dtype=jnp.float32) * (2.0 / ROT))
    angles = (
        positions.astype(jnp.float32).reshape(positions.shape + (1,) * (values.ndim - 1)) * inverse
    )
    cosine = jnp.cos(angles)
    sine = jnp.sin(angles)
    first = values[..., :half]
    second = values[..., half:ROT]
    rest = values[..., ROT:]
    return jnp.concatenate(
        [first * cosine - second * sine, second * cosine + first * sine, rest], axis=-1
    )


def token_layout(lengths_row, group_rows):
    requests_count = lengths_row.shape[0]
    count_pre = group_rows - (requests_count - 1)
    index = jnp.arange(group_rows, dtype=jnp.int32)
    owner = jnp.maximum(index - (count_pre - 1), 0)
    table = owner[:, None] == jnp.arange(requests_count, dtype=jnp.int32)[None, :]
    start = jnp.sum(jnp.where(table, lengths_row[None, :], 0), axis=1)
    place = start + jnp.where(owner == 0, index, 0)
    return (owner, place)


def slot_layout(lengths_row, slots):
    starts = jnp.cumsum(lengths_row) - lengths_row
    index = jnp.arange(slots, dtype=jnp.int32)
    inside = index[:, None] >= starts[None, :]
    owner = jnp.sum(inside.astype(jnp.int32), axis=1) - 1
    begin = jnp.max(jnp.where(inside, starts[None, :], 0), axis=1)
    return (owner, index - begin)


def visible(query_owner, query_place, key_owner, key_place):
    same = query_owner[:, None] == key_owner[None, :]
    before = key_place[None, :] <= query_place[:, None]
    near = (key_place[None, :] < SINKS) | (query_place[:, None] - key_place[None, :] < WINDOW)
    return same & before & near


def stage_pairs(size, stride, shift, total):
    pairs = []
    for index in range(total):
        sub = (index // stride) % size
        pairs.append((index, index + ((sub + shift) % size - sub) * stride))
    return pairs


def gather_stage(stacked, size, stride):
    total = lax.axis_size("head")
    sub = (lax.axis_index("head") // stride) % size
    received = [stacked] + [
        lax.ppermute(stacked, "head", stage_pairs(size, stride, shift, total))
        for shift in range(1, size)
    ]
    return jnp.take(jnp.stack(received), (sub - jnp.arange(size)) % size, axis=0)


def head_gather(block):
    by_y = gather_stage(block, 4, 8)
    by_x = gather_stage(by_y, 4, 2)
    by_core = gather_stage(by_x, 2, 1)
    ordered = by_core.transpose((2, 1, 0) + tuple(range(3, by_core.ndim)))
    return ordered.reshape((-1,) + block.shape[1:])


def scatter_stage(chunks, size, stride):
    total = lax.axis_size("head")
    sub = (lax.axis_index("head") // stride) % size
    summed = lax.dynamic_index_in_dim(chunks, sub, 0, keepdims=False)
    for shift in range(1, size):
        outgoing = lax.dynamic_index_in_dim(chunks, (sub + shift) % size, 0, keepdims=False)
        summed = summed + lax.ppermute(
            outgoing.astype(jnp.bfloat16), "head", stage_pairs(size, stride, shift, total)
        ).astype(jnp.float32)
    return summed


def head_reduce_scatter(partial, rows):
    blocks = partial.reshape((4, 4, 2, rows) + partial.shape[1:])
    by_core = scatter_stage(jnp.moveaxis(blocks, 2, 0), 2, 1)
    by_x = scatter_stage(jnp.moveaxis(by_core, 1, 0), 4, 2)
    return scatter_stage(by_x, 4, 8)


def body(
    tokens,
    ln1_gain,
    ln1_bias,
    ln2_gain,
    ln2_bias,
    w_qkv,
    b_qkv,
    w_dense,
    b_dense,
    w_up,
    b_up,
    w_down,
    b_down,
    k_cache,
    v_cache,
    cache_lengths,
):
    scale = HD ** (-0.5)
    width_qkv = w_qkv.shape[1]
    width_up = w_up.shape[1]
    width_dense = w_dense.shape[0]
    first = lax.all_gather(jnp.concatenate([w_qkv, w_up], axis=1), "tok", axis=0, tiled=False)
    second = lax.all_gather(
        jnp.concatenate([w_dense, w_down], axis=0), "tok", axis=0, tiled=False
    )
    parts = first.shape[0] * first.shape[1]
    qkv_full = first[:, :, :width_qkv].reshape(parts, width_qkv)
    up_full = first[:, :, width_qkv:].reshape(parts, width_up)
    dense_parts = second[:, :width_dense, :]
    down_parts = second[:, width_dense:, :]
    whole = head_gather(tokens)
    normed_one = layer_norm(whole, ln1_gain, ln1_bias).astype(jnp.bfloat16)
    normed_two = layer_norm(whole, ln2_gain, ln2_bias).astype(jnp.bfloat16)
    rows_total = whole.shape[0]
    projected = jnp.dot(normed_one, qkv_full, preferred_element_type=jnp.float32) + b_qkv
    upward = jnp.dot(normed_two, up_full, preferred_element_type=jnp.float32)
    lengths_row = cache_lengths[0]
    query_owner, query_place = token_layout(lengths_row, rows_total)
    queries = rotate(projected[:, :HD], query_place).astype(jnp.bfloat16)
    new_keys = rotate(projected[:, HD : 2 * HD], query_place).astype(jnp.bfloat16)
    new_values = projected[:, 2 * HD :].astype(jnp.bfloat16)
    hidden = jax.nn.gelu(upward + b_up, approximate=False).astype(jnp.bfloat16)
    slots = k_cache.shape[0]
    slot_owner, slot_place = slot_layout(lengths_row, slots)
    cache_scores = jnp.dot(queries, k_cache.T, preferred_element_type=jnp.float32) * scale
    cache_scores = jnp.where(
        visible(query_owner, query_place, slot_owner, slot_place), cache_scores, -jnp.inf
    )
    new_scores = jnp.dot(queries, new_keys.T, preferred_element_type=jnp.float32) * scale
    new_scores = jnp.where(
        visible(query_owner, query_place, query_owner, query_place), new_scores, -jnp.inf
    )
    top = jnp.maximum(jnp.max(cache_scores, axis=1), jnp.max(new_scores, axis=1))
    cache_weights = jnp.exp(cache_scores - top[:, None])
    new_weights = jnp.exp(new_scores - top[:, None])
    total = jnp.sum(cache_weights, axis=1) + jnp.sum(new_weights, axis=1)
    summed = jnp.dot(
        cache_weights.astype(jnp.bfloat16), v_cache, preferred_element_type=jnp.float32
    ) + jnp.dot(new_weights.astype(jnp.bfloat16), new_values, preferred_element_type=jnp.float32)
    attention = (summed / total[:, None]).astype(jnp.bfloat16)
    contract = (((1,), (1,)), ((), ()))
    partial = lax.dot_general(
        attention, dense_parts, contract, preferred_element_type=jnp.float32
    ) + lax.dot_general(hidden, down_parts, contract, preferred_element_type=jnp.float32)
    partial = partial.reshape(rows_total, -1)
    partial_value = head_reduce_scatter(partial, tokens.shape[0])
    mixed = tokens.astype(jnp.float32) + partial_value + b_dense + b_down
    return mixed.astype(jnp.bfloat16)


def solution(mesh):
    placed = (
        P(("tok", "head"), None),
        P(),
        P(),
        P(),
        P(),
        P("tok", "head"),
        P("head"),
        P("head", "tok"),
        P(),
        P("tok", "head"),
        P("head"),
        P("head", "tok"),
        P(),
        P("tok", "head"),
        P("tok", "head"),
        P("tok", None),
    )
    return jax.shard_map(
        body, mesh=mesh, in_specs=placed, out_specs=P(("tok", "head"), None), check_vma=False
    )
```

profile of v0, /device:TPU:1, one launch (start us, length us, event | category | flops | bytes accessed | tf_op | source)
XLA Modules:
  0.0 266.3 jit_solution(9896899705459566519)
XLA Ops:
  8.5 5.5 %collective-permute-start.2 = (bf16[6,4096]{1,0:T(8,128)(2,1)}, bf16[6,4096]{1,0:T(8,128)(2,1)S(1)}, u32[]{:S(2)}, u32[]{:S(2)}) collective-permute-start(bf16[6,4096]{1,0:T(8,128)(2,1)} %param.16), channel_id=1, source_target_pairs={{0,24},{1,25},{2,26},{3,27},{4,28},{5,29},{6,30},{7,31},{8,0},{9,1... | collective-permute-start | bytes 147464 | tf_op jit(solution)/shard_map/ppermute | solution.py:77
  14.0 2.3 collective-permute-start.1
  16.3 2.6 collective-permute-start
  25.2 4.4 %collective-permute-start.5 = (bf16[4,6,4096]{2,1,0:T(8,128)(2,1)S(1)}, bf16[4,6,4096]{2,1,0:T(8,128)(2,1)S(1)}, u32[]{:S(2)}, u32[]{:S(2)}) collective-permute-start(bf16[4,6,4096]{2,1,0:T(8,128)(2,1)S(1)} %broadcast_select_fusion.2), channel_id=1, source_target_pairs={{0,6},{1,7},{2,0},{3,1},{4,2},{5,3},{6,4},{7,5},{8,14},{9,15},{10,... | collective-permute-start | bytes 589832 | tf_op jit(solution)/shard_map/ppermute | solution.py:77
  29.6 2.4 collective-permute-start.4
  32.0 2.5 collective-permute-start.3
  34.7 3.9 %collective-permute-done.4 = bf16[4,6,4096]{2,1,0:T(8,128)(2,1)S(1)} collective-permute-done((bf16[4,6,4096]{2,1,0:T(8,128)(2,1)S(1)}, bf16[4,6,4096]{2,1,0:T(8,128)(2,1)S(1)}, u32[]{:S(2)}, u32[]{:S(2)}) %collective-permute-start.4) | collective-permute-done | bytes 196640 | tf_op jit(solution)/shard_map/ppermute | solution.py:77
  38.5 7.0 %collective-permute-done.3 = bf16[4,6,4096]{2,1,0:T(8,128)(2,1)S(1)} collective-permute-done((bf16[4,6,4096]{2,1,0:T(8,128)(2,1)S(1)}, bf16[4,6,4096]{2,1,0:T(8,128)(2,1)S(1)}, u32[]{:S(2)}, u32[]{:S(2)}) %collective-permute-start.3) | collective-permute-done | bytes 196640 | tf_op jit(solution)/shard_map/ppermute | solution.py:77
  48.0 3.9 %collective-permute-start.6 = (bf16[4,4,6,4096]{3,1,2,0:T(4,128)(2,1)S(1)}, bf16[4,4,6,4096]{3,1,2,0:T(4,128)(2,1)S(1)}, u32[]{:S(2)}, u32[]{:S(2)}) collective-permute-start(bf16[4,4,6,4096]{3,1,2,0:T(4,128)(2,1)S(1)} %broadcast_select_fusion.1), channel_id=1, source_target_pairs={{0,1},{1,0},{2,3},{3,2},{4,5},{5,4},{6,7},{7,6},{8,9},{9,8},{10,11... | collective-permute-start | bytes 2359304 | tf_op jit(solution)/shard_map/ppermute | solution.py:77
  54.8 3.0 %gather_fusion.2 = bf16[2,4,4,6,4096]{4,2,3,1,0:T(4,128)(2,1)} fusion(bf16[2,4,4,6,4096]{4,2,3,1,0:T(4,128)(2,1)S(1)} %pad_maximum_fusion, s32[1024]{0:T(1024)S(1)} %pad_clamp_fusion), kind=kCustom, calls=%fused_computation.2 | custom fusion | bytes 3145736 | tf_op jit(solution)/shard_map/jit(_take)/gather | solution.py:80
  57.8 3.2 %bitcast_reduce_fusion = (f32[4,4,2,6]{0,3,1,2:T(8,128)S(1)}, bf16[2,4,4,6,4096]{4,2,3,1,0:T(4,128)(2,1)S(1)}) fusion(bf16[2,4,4,6,4096]{4,2,3,1,0:T(4,128)(2,1)} %gather_fusion.2, pred[2]{0:T(512)(128)(4,1)S(1)} %compare_and_fusion.2), kind=kLoop, calls=%fused_computation.14 | loop fusion | flops 2359104 | bytes 3146498 | tf_op jit(solution)/shard_map/reduce_sum | solution.py:17
  64.3 2.2 copy.104
  66.5 3.7 %convert_element_type.123 = bf16[192,4096]{1,0:T(8,128)(2,1)} reshape(bf16[4,4,2,6,4096]{4,3,2,1,0:T(8,128)(2,1)} %copy.104) | data formatting | bytes 3145728 | tf_op jit(solution)/shard_map/convert_element_type | solution.py:142
  72.4 2.8 %convert_element_type.129 = bf16[192,4096]{1,0:T(8,128)(2,1)S(1)} reshape(bf16[4,4,2,6,4096]{4,3,2,1,0:T(8,128)(2,1)} %copy.106) | data formatting | bytes 3145728 | tf_op jit(solution)/shard_map/convert_element_type | solution.py:143
  75.2 35.0 %all-gather.5.cloned.1.call-done = bf16[4096,896]{1,0:T(8,128)(2,1)} async-done(((bf16[256,896]{1,0:T(8,128)(2,1)}), bf16[4096,896]{1,0:T(8,128)(2,1)}) %all-gather.5.cloned.1.call-update) | async-done | bytes 7340048 | tf_op jit(solution)/shard_map/all_gather | solution.py:132
  110.2 2.3 slice.61
  112.5 4.6 %slice.70 = bf16[16,256,512]{2,1,0:T(8,128)(2,1)} slice(bf16[16,256,896]{2,1,0:T(8,128)(2,1)} %bitcast.103), slice={[0:16], [0:256], [384:896]} | slice | bytes 8388608 | tf_op jit(solution)/shard_map/slice | solution.py:138
  118.9 2.7 %fusion.165 = (f32[192]{0:T(256)S(1)}, f32[192,6144]{1,0:T(8,128)S(1)}) fusion(bf16[6144,128]{1,0:T(8,128)(2,1)S(1)} %copy-done, bf16[192,96]{0,1:T(8,128)(2,1)S(1)} %get-tuple-element.21, bf16[192,16]{0,1:T(8,128)(2,1)S(1)} %get-tuple-element.17, bf16[192,16]{0,1:T(8,128)(2,1)S(1)} %get-tuple-element.14, pred[6144]{0:T(1024)(128)(4,1)S(1)} %broadcast_compare_fusion, ...), kind=kOutput, calls=%fused_computation.250 | convolution fusion | flops 313933632 | bytes 6398208 | tf_op jit(solution)/shard_map/dot_general | solution.py:155
  124.8 60.1 %all-gather.7.cloned.1.call-done = bf16[10240,256]{1,0:T(8,128)(2,1)} async-done(((bf16[640,256]{1,0:T(8,128)(2,1)}), bf16[10240,256]{1,0:T(8,128)(2,1)}) %all-gather.7.cloned.1.call-update) | async-done | bytes 5242896 | tf_op jit(solution)/shard_map/all_gather | solution.py:133
  184.8 5.7 %fusion.36 = f32[192,16,256]{2,0,1:T(8,128)} fusion(f32[192,128]{1,0:T(8,128)S(1)} %fusion.94, bf16[6144,128]{1,0:T(8,128)(2,1)S(1)} %copy-done.4, f32[192,6144]{1,0:T(8,128)} %copy-done.2, f32[192]{0:T(256)S(1)} %max.37, bf16[16,640,256]{2,1,0:T(8,128)(2,1)} %bitcast.111, f32[192]{0:T(256)S(1)} %add.354), kind=kOutput, calls=%fused_computation.39 | convolution fusion | flops 505749504 | bytes 10585600 | tf_op jit(solution)/shard_map/dot_general | solution.py:172
  190.5 8.8 %fusion.19 = f32[192,16,256]{2,0,1:T(8,128)} fusion(f32[192,16,256]{2,0,1:T(8,128)} %fusion.36, bf16[16,640,256]{2,1,0:T(8,128)(2,1)} %bitcast.112, bf16[192,4096]{1,0:T(8,128)(2,1)S(1)} %convert_element_type.129, bf16[4096,512]{1,0:T(8,128)(2,1)} %bitcast.104, f32[512]{0:T(512)S(1)} %copy-done.13), kind=kOutput, calls=%fused_computation.27 | convolution fusion | flops 1617887232 | bytes 16254976 | tf_op jit(solution)/shard_map/dot_general | solution.py:174
  199.3 5.4 %copy.107 = f32[192,16,256]{2,1,0:T(8,128)} copy(f32[192,16,256]{2,0,1:T(8,128)} %fusion.19) | data formatting | bytes 6291456 | tf_op jit(solution)/shard_map/add | solution.py:172
  204.7 4.9 %reshape_reshape.3 = f32[4,4,2,6,4096]{4,3,2,1,0:T(8,128)} reshape(f32[192,16,256]{2,1,0:T(8,128)} %copy.107) | data formatting | bytes 6291456 | tf_op jit(solution)/shard_map/reshape;reshape | solution.py:104
  212.0 8.9 %collective-permute-start.7 = (bf16[4,4,6,4096]{3,1,2,0:T(4,128)(2,1)S(1)}, bf16[4,4,6,4096]{3,1,2,0:T(4,128)(2,1)S(1)}, u32[]{:S(2)}, u32[]{:S(2)}) collective-permute-start(bf16[4,4,6,4096]{3,1,2,0:T(4,128)(2,1)S(1)} %copy.109), channel_id=1, source_target_pairs={{0,1},{1,0},{2,3},{3,2},{4,5},{5,4},{6,7},{7,6},{8,9},{9,8},{10,11... | collective-permute-start | bytes 2359304 | tf_op jit(solution)/shard_map/ppermute | solution.py:97
  225.7 4.5 %collective-permute-start.10 = (bf16[4,6,4096]{2,0,1:T(4,128)(2,1)S(1)}, bf16[4,6,4096]{2,0,1:T(4,128)(2,1)S(1)}, u32[]{:S(2)}, u32[]{:S(2)}) collective-permute-start(bf16[4,6,4096]{2,0,1:T(4,128)(2,1)S(1)} %bitcast.113), channel_id=1, source_target_pairs={{0,6},{1,7},{2,0},{3,1},{4,2},{5,3},{6,4},{7,5},{8,14},{9,15},{10,... | collective-permute-start | bytes 589832 | tf_op jit(solution)/shard_map/ppermute | solution.py:97
  230.4 2.6 collective-permute-start.9
  233.3 2.3 collective-permute-start.8
  236.1 3.5 %collective-permute-done.9 = bf16[4,6,4096]{2,0,1:T(4,128)(2,1)S(1)} collective-permute-done((bf16[4,6,4096]{2,0,1:T(4,128)(2,1)S(1)}, bf16[4,6,4096]{2,0,1:T(4,128)(2,1)S(1)}, u32[]{:S(2)}, u32[]{:S(2)}) %collective-permute-start.9) | collective-permute-done | bytes 196640 | tf_op jit(solution)/shard_map/ppermute | solution.py:97
  239.6 4.8 %collective-permute-done.8 = bf16[4,6,4096]{2,0,1:T(4,128)(2,1)S(1)} collective-permute-done((bf16[4,6,4096]{2,0,1:T(4,128)(2,1)S(1)}, bf16[4,6,4096]{2,0,1:T(4,128)(2,1)S(1)}, u32[]{:S(2)}, u32[]{:S(2)}) %collective-permute-start.8) | collective-permute-done | bytes 196640 | tf_op jit(solution)/shard_map/ppermute | solution.py:97
  245.2 4.7 %collective-permute-start.13 = (bf16[6,4096]{1,0:T(8,128)(2,1)S(1)}, bf16[6,4096]{1,0:T(8,128)(2,1)S(1)}, u32[]{:S(2)}, u32[]{:S(2)}) collective-permute-start(bf16[6,4096]{1,0:T(8,128)(2,1)S(1)} %bitcast.116), channel_id=1, source_target_pairs={{0,24},{1,25},{2,26},{3,27},{4,28},{5,29},{6,30},{7,31},{8,0},{9,1... | collective-permute-start | bytes 147464 | tf_op jit(solution)/shard_map/ppermute | solution.py:97
  252.1 2.8 %collective-permute-start.11 = (bf16[6,4096]{1,0:T(8,128)(2,1)S(1)}, bf16[6,4096]{1,0:T(8,128)(2,1)S(1)}, u32[]{:S(2)}, u32[]{:S(2)}) collective-permute-start(bf16[6,4096]{1,0:T(8,128)(2,1)S(1)} %bitcast.118), channel_id=1, source_target_pairs={{0,8},{1,9},{2,10},{3,11},{4,12},{5,13},{6,14},{7,15},{8,16},{9,17... | collective-permute-start | bytes 147464 | tf_op jit(solution)/shard_map/ppermute | solution.py:97
  256.5 2.2 collective-permute-done.11
  (102 shorter events, 37.2 us)
Async XLA Ops:
  6.5 112.4 %copy-start = (bf16[6144,128]{1,0:T(8,128)(2,1)S(1)}, bf16[6144,128]{1,0:T(8,128)(2,1)}, u32[]{:S(2)}) copy-start(bf16[6144,128]{1,0:T(8,128)(2,1)} %param.29) | copy-start | bytes 4718596
  6.5 103.6 %all-gather.5.cloned.1.call-start = ((), (), s32[]{:S(2)}) async-start(), calls=%async_computation | async-start | bytes 7798784 | tf_op jit(solution)/shard_map/all_gather | solution.py:132
  8.5 176.3 %all-gather.7.cloned.1.call-start = ((), (), s32[]{:S(2)}) async-start(), calls=%async_computation.1 | async-start | bytes 5570560 | tf_op jit(solution)/shard_map/all_gather | solution.py:133
  8.5 15.0 %collective-permute-start.2 = (bf16[6,4096]{1,0:T(8,128)(2,1)}, bf16[6,4096]{1,0:T(8,128)(2,1)S(1)}, u32[]{:S(2)}, u32[]{:S(2)}) collective-permute-start(bf16[6,4096]{1,0:T(8,128)(2,1)} %param.16), channel_id=1, source_target_pairs={{0,24},{1,25},{2,26},{3,27},{4,28},{5,29},{6,30},{7,31},{8,0},{9,1... | collective-permute-start | bytes 147464 | tf_op jit(solution)/shard_map/ppermute | solution.py:77
  14.0 9.6 %collective-permute-start.1 = (bf16[6,4096]{1,0:T(8,128)(2,1)}, bf16[6,4096]{1,0:T(8,128)(2,1)S(1)}, u32[]{:S(2)}, u32[]{:S(2)}) collective-permute-start(bf16[6,4096]{1,0:T(8,128)(2,1)} %param.16), channel_id=1, source_target_pairs={{0,16},{1,17},{2,18},{3,19},{4,20},{5,21},{6,22},{7,23},{8,24},{9,... | collective-permute-start | bytes 147464 | tf_op jit(solution)/shard_map/ppermute | solution.py:77
  16.3 7.3 %collective-permute-start = (bf16[6,4096]{1,0:T(8,128)(2,1)}, bf16[6,4096]{1,0:T(8,128)(2,1)S(1)}, u32[]{:S(2)}, u32[]{:S(2)}) collective-permute-start(bf16[6,4096]{1,0:T(8,128)(2,1)} %param.16), channel_id=1, source_target_pairs={{0,8},{1,9},{2,10},{3,11},{4,12},{5,13},{6,14},{7,15},{8,16},{9,17... | collective-permute-start | bytes 147464 | tf_op jit(solution)/shard_map/ppermute | solution.py:77
  25.2 9.5 %collective-permute-start.5 = (bf16[4,6,4096]{2,1,0:T(8,128)(2,1)S(1)}, bf16[4,6,4096]{2,1,0:T(8,128)(2,1)S(1)}, u32[]{:S(2)}, u32[]{:S(2)}) collective-permute-start(bf16[4,6,4096]{2,1,0:T(8,128)(2,1)S(1)} %broadcast_select_fusion.2), channel_id=1, source_target_pairs={{0,6},{1,7},{2,0},{3,1},{4,2},{5,3},{6,4},{7,5},{8,14},{9,15},{10,... | collective-permute-start | bytes 589832 | tf_op jit(solution)/shard_map/ppermute | solution.py:77
  29.6 8.9 %collective-permute-start.4 = (bf16[4,6,4096]{2,1,0:T(8,128)(2,1)S(1)}, bf16[4,6,4096]{2,1,0:T(8,128)(2,1)S(1)}, u32[]{:S(2)}, u32[]{:S(2)}) collective-permute-start(bf16[4,6,4096]{2,1,0:T(8,128)(2,1)S(1)} %broadcast_select_fusion.2), channel_id=1, source_target_pairs={{0,4},{1,5},{2,6},{3,7},{4,0},{5,1},{6,2},{7,3},{8,12},{9,13},{10,... | collective-permute-start | bytes 589832 | tf_op jit(solution)/shard_map/ppermute | solution.py:77
  32.0 13.5 %collective-permute-start.3 = (bf16[4,6,4096]{2,1,0:T(8,128)(2,1)S(1)}, bf16[4,6,4096]{2,1,0:T(8,128)(2,1)S(1)}, u32[]{:S(2)}, u32[]{:S(2)}) collective-permute-start(bf16[4,6,4096]{2,1,0:T(8,128)(2,1)S(1)} %broadcast_select_fusion.2), channel_id=1, source_target_pairs={{0,2},{1,3},{2,4},{3,5},{4,6},{5,7},{6,0},{7,1},{8,10},{9,11},{10,... | collective-permute-start | bytes 589832 | tf_op jit(solution)/shard_map/ppermute | solution.py:77
  48.0 5.6 %collective-permute-start.6 = (bf16[4,4,6,4096]{3,1,2,0:T(4,128)(2,1)S(1)}, bf16[4,4,6,4096]{3,1,2,0:T(4,128)(2,1)S(1)}, u32[]{:S(2)}, u32[]{:S(2)}) collective-permute-start(bf16[4,4,6,4096]{3,1,2,0:T(4,128)(2,1)S(1)} %broadcast_select_fusion.1), channel_id=1, source_target_pairs={{0,1},{1,0},{2,3},{3,2},{4,5},{5,4},{6,7},{7,6},{8,9},{9,8},{10,11... | collective-permute-start | bytes 2359304 | tf_op jit(solution)/shard_map/ppermute | solution.py:77
  57.8 4.4 %copy-start.6 = (f32[4096]{0:T(1024)S(1)}, f32[4096]{0:T(1024)}, u32[]{:S(2)}) copy-start(f32[4096]{0:T(1024)} %param.20) | copy-start | bytes 49156
  57.8 4.4 %copy-start.7 = (f32[4096]{0:T(1024)S(1)}, f32[4096]{0:T(1024)}, u32[]{:S(2)}) copy-start(f32[4096]{0:T(1024)} %param.19) | copy-start | bytes 49156
  57.8 4.4 %copy-start.8 = (f32[4096]{0:T(1024)S(1)}, f32[4096]{0:T(1024)}, u32[]{:S(2)}) copy-start(f32[4096]{0:T(1024)} %param.18) | copy-start | bytes 49156
  57.8 4.4 %copy-start.9 = (f32[4096]{0:T(1024)S(1)}, f32[4096]{0:T(1024)}, u32[]{:S(2)}) copy-start(f32[4096]{0:T(1024)} %param.17) | copy-start | bytes 49156
  112.4 4.6 %copy-start.3 = (bf16[192,4096]{1,0:T(8,128)(2,1)S(1)}, bf16[192,4096]{1,0:T(8,128)(2,1)}, u32[]{:S(2)}) copy-start(bf16[192,4096]{1,0:T(8,128)(2,1)} %convert_element_type.123) | copy-start | bytes 4718596
  112.5 4.6 %copy-start.12 = (f32[384]{0:T(512)S(1)}, f32[384]{0:T(512)}, u32[]{:S(2)}) copy-start(f32[384]{0:T(512)} %param.22) | copy-start | bytes 4612
  121.6 2.1 copy-start.2
  121.6 63.2 %copy-start.4 = (bf16[6144,128]{1,0:T(8,128)(2,1)S(1)}, bf16[6144,128]{1,0:T(8,128)(2,1)}, u32[]{:S(2)}) copy-start(bf16[6144,128]{1,0:T(8,128)(2,1)} %param.30) | copy-start | bytes 4718596
  184.8 5.7 %copy-start.13 = (f32[512]{0:T(512)S(1)}, f32[512]{0:T(512)}, u32[]{:S(2)}) copy-start(f32[512]{0:T(512)} %param.26) | copy-start | bytes 6148
  212.0 10.8 %collective-permute-start.7 = (bf16[4,4,6,4096]{3,1,2,0:T(4,128)(2,1)S(1)}, bf16[4,4,6,4096]{3,1,2,0:T(4,128)(2,1)S(1)}, u32[]{:S(2)}, u32[]{:S(2)}) collective-permute-start(bf16[4,4,6,4096]{3,1,2,0:T(4,128)(2,1)S(1)} %copy.109), channel_id=1, source_target_pairs={{0,1},{1,0},{2,3},{3,2},{4,5},{5,4},{6,7},{7,6},{8,9},{9,8},{10,11... | collective-permute-start | bytes 2359304 | tf_op jit(solution)/shard_map/ppermute | solution.py:97
  224.1 35.4 %copy-start.1 = (bf16[6144,128]{1,0:T(8,128)(2,1)S(1)}, bf16[6144,128]{1,0:T(8,128)(2,1)}, u32[]{:S(2)}) copy-start(bf16[6144,128]{1,0:T(8,128)(2,1)} %param.29) | copy-start | bytes 4718596
  225.4 33.4 %copy-start.5 = (bf16[6,4096]{1,0:T(8,128)(2,1)S(1)}, bf16[6,4096]{1,0:T(8,128)(2,1)}, u32[]{:S(2)}) copy-start(bf16[6,4096]{1,0:T(8,128)(2,1)} %param.16) | copy-start | bytes 147460
  225.4 33.3 %copy-start.10 = (f32[4096]{0:T(1024)S(1)}, f32[4096]{0:T(1024)}, u32[]{:S(2)}) copy-start(f32[4096]{0:T(1024)} %param.28) | copy-start | bytes 49156
  225.4 33.3 %copy-start.11 = (f32[4096]{0:T(1024)S(1)}, f32[4096]{0:T(1024)}, u32[]{:S(2)}) copy-start(f32[4096]{0:T(1024)} %param.24) | copy-start | bytes 49156
  225.7 10.4 %collective-permute-start.10 = (bf16[4,6,4096]{2,0,1:T(4,128)(2,1)S(1)}, bf16[4,6,4096]{2,0,1:T(4,128)(2,1)S(1)}, u32[]{:S(2)}, u32[]{:S(2)}) collective-permute-start(bf16[4,6,4096]{2,0,1:T(4,128)(2,1)S(1)} %bitcast.113), channel_id=1, source_target_pairs={{0,6},{1,7},{2,0},{3,1},{4,2},{5,3},{6,4},{7,5},{8,14},{9,15},{10,... | collective-permute-start | bytes 589832 | tf_op jit(solution)/shard_map/ppermute | solution.py:97
  230.4 9.2 %collective-permute-start.9 = (bf16[4,6,4096]{2,0,1:T(4,128)(2,1)S(1)}, bf16[4,6,4096]{2,0,1:T(4,128)(2,1)S(1)}, u32[]{:S(2)}, u32[]{:S(2)}) collective-permute-start(bf16[4,6,4096]{2,0,1:T(4,128)(2,1)S(1)} %bitcast.114), channel_id=1, source_target_pairs={{0,4},{1,5},{2,6},{3,7},{4,0},{5,1},{6,2},{7,3},{8,12},{9,13},{10,... | collective-permute-start | bytes 589832 | tf_op jit(solution)/shard_map/ppermute | solution.py:97
  233.3 11.1 %collective-permute-start.8 = (bf16[4,6,4096]{2,0,1:T(4,128)(2,1)S(1)}, bf16[4,6,4096]{2,0,1:T(4,128)(2,1)S(1)}, u32[]{:S(2)}, u32[]{:S(2)}) collective-permute-start(bf16[4,6,4096]{2,0,1:T(4,128)(2,1)S(1)} %bitcast.115), channel_id=1, source_target_pairs={{0,2},{1,3},{2,4},{3,5},{4,6},{5,7},{6,0},{7,1},{8,10},{9,11},{10,... | collective-permute-start | bytes 589832 | tf_op jit(solution)/shard_map/ppermute | solution.py:97
  245.2 9.8 %collective-permute-start.13 = (bf16[6,4096]{1,0:T(8,128)(2,1)S(1)}, bf16[6,4096]{1,0:T(8,128)(2,1)S(1)}, u32[]{:S(2)}, u32[]{:S(2)}) collective-permute-start(bf16[6,4096]{1,0:T(8,128)(2,1)S(1)} %bitcast.116), channel_id=1, source_target_pairs={{0,24},{1,25},{2,26},{3,27},{4,28},{5,29},{6,30},{7,31},{8,0},{9,1... | collective-permute-start | bytes 147464 | tf_op jit(solution)/shard_map/ppermute | solution.py:97
  250.0 6.5 %collective-permute-start.12 = (bf16[6,4096]{1,0:T(8,128)(2,1)S(1)}, bf16[6,4096]{1,0:T(8,128)(2,1)S(1)}, u32[]{:S(2)}, u32[]{:S(2)}) collective-permute-start(bf16[6,4096]{1,0:T(8,128)(2,1)S(1)} %bitcast.117), channel_id=1, source_target_pairs={{0,16},{1,17},{2,18},{3,19},{4,20},{5,21},{6,22},{7,23},{8,24},{9,... | collective-permute-start | bytes 147464 | tf_op jit(solution)/shard_map/ppermute | solution.py:97
  252.1 6.6 %collective-permute-start.11 = (bf16[6,4096]{1,0:T(8,128)(2,1)S(1)}, bf16[6,4096]{1,0:T(8,128)(2,1)S(1)}, u32[]{:S(2)}, u32[]{:S(2)}) collective-permute-start(bf16[6,4096]{1,0:T(8,128)(2,1)S(1)} %bitcast.118), channel_id=1, source_target_pairs={{0,8},{1,9},{2,10},{3,11},{4,12},{5,13},{6,14},{7,15},{8,16},{9,17... | collective-permute-start | bytes 147464 | tf_op jit(solution)/shard_map/ppermute | solution.py:97
Sparse Core Ops, SparseCore 0:
  9.4 100.7 all-gather.4
  112.3 72.5 all-gather.6
where the time goes:
time: 267 us; the launch traced here: 266 us
  waiting for transfers between devices  119 us (45%)
  starting transfers between devices  51.5 us (19%)
  local copies, waits for them, and re-layouts  42.8 us (16%)
  other arithmetic  19.6 us (7%)
  matrix products  19 us (7%)
  between operations  14.2 us (5%)
    all_gather x1, waiting for transfers between devices, body(): lax.all_gather(jnp.concatenate([w_dense, w_down], axis=0), 'tok', axis=0,...  60.1 us
    all_gather x1, waiting for transfers between devices, body(): lax.all_gather(jnp.concatenate([w_qkv, w_up], axis=1), 'tok', axis=0, til...  35 us
    ppermute x7, starting transfers between devices, scatter_stage(): lax.ppermute(outgoing.astype(jnp.bfloat16), 'head', stage_pairs(size, str...  27.9 us
    ppermute x7, starting transfers between devices, gather_stage(): lax.ppermute(stacked, 'head', stage_pairs(size, stride, shift, total))  23.6 us
    ppermute x7, waiting for transfers between devices, gather_stage(): lax.ppermute(stacked, 'head', stage_pairs(size, stride, shift, total))  12.1 us
    ppermute x7, waiting for transfers between devices, scatter_stage(): lax.ppermute(outgoing.astype(jnp.bfloat16), 'head', stage_pairs(size, str...  12 us
    dot_general x1, matrix products, body(): lax.dot_general(hidden, down_parts, contract, preferred_element_type=jnp....  8.76 us
    convert_element_type x2, local copies, waits for them, and re-layouts, body(): normed_one = layer_norm(whole, ln1_gain, ln1_bias).astype(jnp.bfloat16)  5.94 us
  transfers between devices with their start and end apart: 16, of which 9 were waited for; matrix products, arithmetic and copies ran while one was open for 17% of the time, Pallas kernels for 0%

commit v1 on v0

--- a/solution.py
+++ b/solution.py
@@ -173,7 +173,10 @@
         attention, dense_parts, contract, preferred_element_type=jnp.float32
     ) + lax.dot_general(hidden, down_parts, contract, preferred_element_type=jnp.float32)
     partial = partial.reshape(rows_total, -1)
-    partial_value = head_reduce_scatter(partial, tokens.shape[0])
+    heads = lax.axis_size("head")
+    blocks = partial.astype(jnp.bfloat16).reshape(heads, tokens.shape[0], -1)
+    exchanged = lax.all_to_all(blocks, "head", 0, 0, tiled=True)
+    partial_value = jnp.sum(exchanged.astype(jnp.float32), axis=0)
     mixed = tokens.astype(jnp.float32) + partial_value + b_dense + b_down
     return mixed.astype(jnp.bfloat16)
 

time: 267 us -> 255 us (0.955)
  blocking collectives: 0 us -> 42.5 us
  starting transfers between devices: 51.5 us -> 27.2 us
  waiting for transfers between devices: 119 us -> 104 us
  local copies, waits for them, and re-layouts: 42.8 us -> 30.3 us
    all_to_all x0 -> x1, blocking collectives: none -> 42.5 us  [body(): exchanged = lax.all_to_all(blocks, 'head', 0, 0, tiled=True)]
    ppermute x7 -> x0, starting transfers between devices: 27.9 us -> none  [scatter_stage(): lax.ppermute(outgoing.astype(jnp.bfloat16), 'head', stage_pairs(size, str...]
    ppermute x7 -> x0, waiting for transfers between devices: 12 us -> none  [scatter_stage(): lax.ppermute(outgoing.astype(jnp.bfloat16), 'head', stage_pairs(size, str...]
    another operation x3 -> x0, local copies, waits for them, and re-layouts: 7.1 us -> none  [the longest x1 4.94 us: head_reduce_scatter(): blocks = partial.reshape((4, 4, 2, rows) + partial.shape[1:])]
    add x1 -> x0, local copies, waits for them, and re-layouts: 5.41 us -> none  [body(): lax.dot_general(attention, dense_parts, contract, preferred_element_type=...]
    ppermute x7, starting transfers between devices: 23.6 us -> 27.2 us  [gather_stage(): lax.ppermute(stacked, 'head', stage_pairs(size, stride, shift, total))]
    ppermute x7, waiting for transfers between devices: 12.1 us -> 9.45 us  [gather_stage(): lax.ppermute(stacked, 'head', stage_pairs(size, stride, shift, total))]
  transfers between devices with their start and end apart: 16 -> 9, of which waited for: 9 -> 5; matrix products, arithmetic and copies ran while one was open for 17% -> 17% of each run, Pallas kernels for 0% -> 0%
where the time goes in v1:
time: 255 us
  waiting for transfers between devices  104 us (41%)
  blocking collectives  42.5 us (17%)
  local copies, waits for them, and re-layouts  30.3 us (12%)
  starting transfers between devices  27.2 us (11%)
  matrix products  19 us (7%)
  other arithmetic  18.3 us (7%)
  between operations  13.9 us (5%)
    all_gather x1, waiting for transfers between devices, body(): lax.all_gather(jnp.concatenate([w_dense, w_down], axis=0), 'tok', axis=0,...  60.1 us
    all_to_all x1, blocking collectives, body(): exchanged = lax.all_to_all(blocks, 'head', 0, 0, tiled=True)  42.5 us
    all_gather x1, waiting for transfers between devices, body(): lax.all_gather(jnp.concatenate([w_qkv, w_up], axis=1), 'tok', axis=0, til...  34 us
    ppermute x7, starting transfers between devices, gather_stage(): lax.ppermute(stacked, 'head', stage_pairs(size, stride, shift, total))  27.2 us
    ppermute x7, waiting for transfers between devices, gather_stage(): lax.ppermute(stacked, 'head', stage_pairs(size, stride, shift, total))  9.45 us
    dot_general x1, matrix products, body(): lax.dot_general(hidden, down_parts, contract, preferred_element_type=jnp....  8.29 us
    dot_general x1, matrix products, body(): lax.dot_general(attention, dense_parts, contract, preferred_element_type=...  6.15 us
    convert_element_type x2, local copies, waits for them, and re-layouts, body(): normed_one = layer_norm(whole, ln1_gain, ln1_bias).astype(jnp.bfloat16)  5.89 us
  transfers between devices with their start and end apart: 9, of which 5 were waited for; matrix products, arithmetic and copies ran while one was open for 17% of the time, Pallas kernels for 0%

profile of v1, /device:TPU:1, one launch (start us, length us, event | category | flops | bytes accessed | tf_op | source)
XLA Modules:
  0.0 254.8 jit_solution(97385241001620581)
XLA Ops:
  6.5 2.0 pad_maximum_fusion.2
  8.6 4.0 %collective-permute-start = (bf16[6,4096]{1,0:T(8,128)(2,1)}, bf16[6,4096]{1,0:T(8,128)(2,1)S(1)}, u32[]{:S(2)}, u32[]{:S(2)}) collective-permute-start(bf16[6,4096]{1,0:T(8,128)(2,1)} %param.16), channel_id=1, source_target_pairs={{0,8},{1,9},{2,10},{3,11},{4,12},{5,13},{6,14},{7,15},{8,16},{9,17... | collective-permute-start | bytes 147464 | tf_op jit(solution)/shard_map/ppermute | solution.py:77
  12.6 4.5 %collective-permute-start.1 = (bf16[6,4096]{1,0:T(8,128)(2,1)}, bf16[6,4096]{1,0:T(8,128)(2,1)S(1)}, u32[]{:S(2)}, u32[]{:S(2)}) collective-permute-start(bf16[6,4096]{1,0:T(8,128)(2,1)} %param.16), channel_id=1, source_target_pairs={{0,16},{1,17},{2,18},{3,19},{4,20},{5,21},{6,22},{7,23},{8,24},{9,... | collective-permute-start | bytes 147464 | tf_op jit(solution)/shard_map/ppermute | solution.py:77
  17.2 3.0 %collective-permute-start.2 = (bf16[6,4096]{1,0:T(8,128)(2,1)}, bf16[6,4096]{1,0:T(8,128)(2,1)S(1)}, u32[]{:S(2)}, u32[]{:S(2)}) collective-permute-start(bf16[6,4096]{1,0:T(8,128)(2,1)} %param.16), channel_id=1, source_target_pairs={{0,24},{1,25},{2,26},{3,27},{4,28},{5,29},{6,30},{7,31},{8,0},{9,1... | collective-permute-start | bytes 147464 | tf_op jit(solution)/shard_map/ppermute | solution.py:77
  20.2 1.7 pad_maximum_fusion.3
  26.4 4.4 %collective-permute-start.5 = (bf16[4,6,4096]{2,1,0:T(8,128)(2,1)S(1)}, bf16[4,6,4096]{2,1,0:T(8,128)(2,1)S(1)}, u32[]{:S(2)}, u32[]{:S(2)}) collective-permute-start(bf16[4,6,4096]{2,1,0:T(8,128)(2,1)S(1)} %broadcast_select_fusion.2), channel_id=1, source_target_pairs={{0,6},{1,7},{2,0},{3,1},{4,2},{5,3},{6,4},{7,5},{8,14},{9,15},{10,... | collective-permute-start | bytes 589832 | tf_op jit(solution)/shard_map/ppermute | solution.py:77
  30.8 1.9 collective-permute-start.3
  32.8 3.6 %collective-permute-start.4 = (bf16[4,6,4096]{2,1,0:T(8,128)(2,1)S(1)}, bf16[4,6,4096]{2,1,0:T(8,128)(2,1)S(1)}, u32[]{:S(2)}, u32[]{:S(2)}) collective-permute-start(bf16[4,6,4096]{2,1,0:T(8,128)(2,1)S(1)} %broadcast_select_fusion.2), channel_id=1, source_target_pairs={{0,4},{1,5},{2,6},{3,7},{4,0},{5,1},{6,2},{7,3},{8,12},{9,13},{10,... | collective-permute-start | bytes 589832 | tf_op jit(solution)/shard_map/ppermute | solution.py:77
  36.5 4.4 %collective-permute-done.3 = bf16[4,6,4096]{2,1,0:T(8,128)(2,1)S(1)} collective-permute-done((bf16[4,6,4096]{2,1,0:T(8,128)(2,1)S(1)}, bf16[4,6,4096]{2,1,0:T(8,128)(2,1)S(1)}, u32[]{:S(2)}, u32[]{:S(2)}) %collective-permute-start.3) | collective-permute-done | bytes 196640 | tf_op jit(solution)/shard_map/ppermute | solution.py:77
  40.9 3.8 %collective-permute-done.4 = bf16[4,6,4096]{2,1,0:T(8,128)(2,1)S(1)} collective-permute-done((bf16[4,6,4096]{2,1,0:T(8,128)(2,1)S(1)}, bf16[4,6,4096]{2,1,0:T(8,128)(2,1)S(1)}, u32[]{:S(2)}, u32[]{:S(2)}) %collective-permute-start.4) | collective-permute-done | bytes 196640 | tf_op jit(solution)/shard_map/ppermute | solution.py:77
  45.6 1.2 gather_fusion.1
  47.2 5.7 %collective-permute-start.6 = (bf16[4,4,6,4096]{3,1,2,0:T(4,128)(2,1)S(1)}, bf16[4,4,6,4096]{3,1,2,0:T(4,128)(2,1)S(1)}, u32[]{:S(2)}, u32[]{:S(2)}) collective-permute-start(bf16[4,4,6,4096]{3,1,2,0:T(4,128)(2,1)S(1)} %broadcast_select_fusion.1), channel_id=1, source_target_pairs={{0,1},{1,0},{2,3},{3,2},{4,5},{5,4},{6,7},{7,6},{8,9},{9,8},{10,11... | collective-permute-start | bytes 2359304 | tf_op jit(solution)/shard_map/ppermute | solution.py:77
  53.3 1.3 collective-permute-done.6
  55.7 3.0 %gather_fusion.2 = bf16[2,4,4,6,4096]{4,2,3,1,0:T(4,128)(2,1)} fusion(bf16[2,4,4,6,4096]{4,2,3,1,0:T(4,128)(2,1)S(1)} %pad_maximum_fusion, s32[1024]{0:T(1024)S(1)} %pad_clamp_fusion), kind=kCustom, calls=%fused_computation.2 | custom fusion | bytes 3145736 | tf_op jit(solution)/shard_map/jit(_take)/gather | solution.py:80
  58.8 3.2 %bitcast_reduce_fusion = (f32[4,4,2,6]{0,3,1,2:T(8,128)S(1)}, bf16[2,4,4,6,4096]{4,2,3,1,0:T(4,128)(2,1)S(1)}) fusion(bf16[2,4,4,6,4096]{4,2,3,1,0:T(4,128)(2,1)} %gather_fusion.2, pred[2]{0:T(512)(128)(4,1)S(1)} %compare_and_fusion.2), kind=kLoop, calls=%fused_computation.15 | loop fusion | flops 2359104 | bytes 3146498 | tf_op jit(solution)/shard_map/reduce_sum | solution.py:17
  63.2 2.1 fusion.14
  65.2 2.2 copy.35
  67.5 3.7 %convert_element_type.70 = bf16[192,4096]{1,0:T(8,128)(2,1)} reshape(bf16[4,4,2,6,4096]{4,3,2,1,0:T(8,128)(2,1)} %copy.35) | data formatting | bytes 3145728 | tf_op jit(solution)/shard_map/convert_element_type | solution.py:142
  71.1 2.2 copy.37
  73.4 2.8 %convert_element_type.76 = bf16[192,4096]{1,0:T(8,128)(2,1)S(1)} reshape(bf16[4,4,2,6,4096]{4,3,2,1,0:T(8,128)(2,1)} %copy.37) | data formatting | bytes 3145728 | tf_op jit(solution)/shard_map/convert_element_type | solution.py:143
  76.1 34.0 %all-gather.5.cloned.1.call-done = bf16[4096,896]{1,0:T(8,128)(2,1)} async-done(((bf16[256,896]{1,0:T(8,128)(2,1)}), bf16[4096,896]{1,0:T(8,128)(2,1)}) %all-gather.5.cloned.1.call-update) | async-done | bytes 7340048 | tf_op jit(solution)/shard_map/all_gather | solution.py:132
  110.2 2.3 slice.61
  112.5 4.6 %slice.70 = bf16[16,256,512]{2,1,0:T(8,128)(2,1)} slice(bf16[16,256,896]{2,1,0:T(8,128)(2,1)} %bitcast.61), slice={[0:16], [0:256], [384:896]} | slice | bytes 8388608 | tf_op jit(solution)/shard_map/slice | solution.py:138
  117.1 1.4 fusion.154
  119.0 2.7 %fusion.155 = (f32[192]{0:T(256)S(1)}, f32[192,6144]{1,0:T(8,128)S(1)}) fusion(bf16[6144,128]{1,0:T(8,128)(2,1)S(1)} %copy-done, bf16[192,96]{0,1:T(8,128)(2,1)S(1)} %get-tuple-element.15, bf16[192,16]{0,1:T(8,128)(2,1)S(1)} %get-tuple-element.14, bf16[192,16]{0,1:T(8,128)(2,1)S(1)} %get-tuple-element.11, pred[6144]{0:T(1024)(128)(4,1)S(1)} %broadcast_compare_fusion, ...), kind=kOutput, calls=%fused_computation.224 | convolution fusion | flops 313933632 | bytes 6398208 | tf_op jit(solution)/shard_map/dot_general | solution.py:155
  121.7 2.0 copy-done.1
  124.8 60.1 %all-gather.7.cloned.1.call-done = bf16[10240,256]{1,0:T(8,128)(2,1)} async-done(((bf16[640,256]{1,0:T(8,128)(2,1)}), bf16[10240,256]{1,0:T(8,128)(2,1)}) %all-gather.7.cloned.1.call-update) | async-done | bytes 5242896 | tf_op jit(solution)/shard_map/all_gather | solution.py:133
  184.8 6.2 %fusion.35 = f32[192,16,256]{2,0,1:T(8,128)} fusion(f32[192,128]{1,0:T(8,128)S(1)} %fusion.84, bf16[6144,128]{1,0:T(8,128)(2,1)} %param.30, f32[192,6144]{1,0:T(8,128)} %copy-done.1, f32[192]{0:T(256)S(1)} %max.37, bf16[16,640,256]{2,1,0:T(8,128)(2,1)} %bitcast.69, f32[192]{0:T(256)S(1)} %add.255), kind=kOutput, calls=%fused_computation.38 | convolution fusion | flops 505749504 | bytes 10585600 | tf_op jit(solution)/shard_map/dot_general | solution.py:172
  191.0 8.3 %add_convert_fusion = bf16[192,16,256]{2,0,1:T(8,128)(2,1)} fusion(f32[192,16,256]{2,0,1:T(8,128)} %fusion.35, bf16[16,640,256]{2,1,0:T(8,128)(2,1)} %bitcast.70, bf16[192,4096]{1,0:T(8,128)(2,1)S(1)} %convert_element_type.76, bf16[4096,512]{1,0:T(8,128)(2,1)} %bitcast.62, f32[512]{0:T(512)S(1)} %copy-done.11), kind=kOutput, calls=%fused_computation.25 | convolution fusion | flops 1618673664 | bytes 14682112 | tf_op jit(solution)/shard_map/dot_general | solution.py:174
  199.3 2.3 copy.38
  201.6 2.7 %convert_element_type.79 = bf16[32,6,4096]{2,1,0:T(8,128)(2,1)} reshape(bf16[192,16,256]{2,1,0:T(8,128)(2,1)S(1)} %copy.38) | data formatting | bytes 3145728 | tf_op jit(solution)/shard_map/convert_element_type | solution.py:177
  204.3 42.5 %all_to_all.5 = bf16[32,6,4096]{2,1,0:T(8,128)(2,1)S(1)} all-to-all(bf16[32,6,4096]{2,1,0:T(8,128)(2,1)} %convert_element_type.79), channel_id=1, replica_groups=mesh['tok'=16,'head'=32] {'head'}, dimensions={0} | all-to-all | bytes 3145728 | tf_op jit(solution)/shard_map/all_to_all | solution.py:178
  (72 shorter events, 11.2 us)
Async XLA Ops:
  6.5 112.4 %copy-start = (bf16[6144,128]{1,0:T(8,128)(2,1)S(1)}, bf16[6144,128]{1,0:T(8,128)(2,1)}, u32[]{:S(2)}) copy-start(bf16[6144,128]{1,0:T(8,128)(2,1)} %param.29) | copy-start | bytes 4718596
  6.5 103.6 %all-gather.5.cloned.1.call-start = ((), (), s32[]{:S(2)}) async-start(), calls=%async_computation.1 | async-start | bytes 7798784 | tf_op jit(solution)/shard_map/all_gather | solution.py:132
  8.5 176.3 %all-gather.7.cloned.1.call-start = ((), (), s32[]{:S(2)}) async-start(), calls=%async_computation.2 | async-start | bytes 5570560 | tf_op jit(solution)/shard_map/all_gather | solution.py:133
  8.6 16.2 %collective-permute-start = (bf16[6,4096]{1,0:T(8,128)(2,1)}, bf16[6,4096]{1,0:T(8,128)(2,1)S(1)}, u32[]{:S(2)}, u32[]{:S(2)}) collective-permute-start(bf16[6,4096]{1,0:T(8,128)(2,1)} %param.16), channel_id=1, source_target_pairs={{0,8},{1,9},{2,10},{3,11},{4,12},{5,13},{6,14},{7,15},{8,16},{9,17... | collective-permute-start | bytes 147464 | tf_op jit(solution)/shard_map/ppermute | solution.py:77
  12.6 12.2 %collective-permute-start.1 = (bf16[6,4096]{1,0:T(8,128)(2,1)}, bf16[6,4096]{1,0:T(8,128)(2,1)S(1)}, u32[]{:S(2)}, u32[]{:S(2)}) collective-permute-start(bf16[6,4096]{1,0:T(8,128)(2,1)} %param.16), channel_id=1, source_target_pairs={{0,16},{1,17},{2,18},{3,19},{4,20},{5,21},{6,22},{7,23},{8,24},{9,... | collective-permute-start | bytes 147464 | tf_op jit(solution)/shard_map/ppermute | solution.py:77
  17.2 7.7 %collective-permute-start.2 = (bf16[6,4096]{1,0:T(8,128)(2,1)}, bf16[6,4096]{1,0:T(8,128)(2,1)S(1)}, u32[]{:S(2)}, u32[]{:S(2)}) collective-permute-start(bf16[6,4096]{1,0:T(8,128)(2,1)} %param.16), channel_id=1, source_target_pairs={{0,24},{1,25},{2,26},{3,27},{4,28},{5,29},{6,30},{7,31},{8,0},{9,1... | collective-permute-start | bytes 147464 | tf_op jit(solution)/shard_map/ppermute | solution.py:77
  26.4 10.1 %collective-permute-start.5 = (bf16[4,6,4096]{2,1,0:T(8,128)(2,1)S(1)}, bf16[4,6,4096]{2,1,0:T(8,128)(2,1)S(1)}, u32[]{:S(2)}, u32[]{:S(2)}) collective-permute-start(bf16[4,6,4096]{2,1,0:T(8,128)(2,1)S(1)} %broadcast_select_fusion.2), channel_id=1, source_target_pairs={{0,6},{1,7},{2,0},{3,1},{4,2},{5,3},{6,4},{7,5},{8,14},{9,15},{10,... | collective-permute-start | bytes 589832 | tf_op jit(solution)/shard_map/ppermute | solution.py:77
  30.8 10.0 %collective-permute-start.3 = (bf16[4,6,4096]{2,1,0:T(8,128)(2,1)S(1)}, bf16[4,6,4096]{2,1,0:T(8,128)(2,1)S(1)}, u32[]{:S(2)}, u32[]{:S(2)}) collective-permute-start(bf16[4,6,4096]{2,1,0:T(8,128)(2,1)S(1)} %broadcast_select_fusion.2), channel_id=1, source_target_pairs={{0,2},{1,3},{2,4},{3,5},{4,6},{5,7},{6,0},{7,1},{8,10},{9,11},{10,... | collective-permute-start | bytes 589832 | tf_op jit(solution)/shard_map/ppermute | solution.py:77
  32.8 11.9 %collective-permute-start.4 = (bf16[4,6,4096]{2,1,0:T(8,128)(2,1)S(1)}, bf16[4,6,4096]{2,1,0:T(8,128)(2,1)S(1)}, u32[]{:S(2)}, u32[]{:S(2)}) collective-permute-start(bf16[4,6,4096]{2,1,0:T(8,128)(2,1)S(1)} %broadcast_select_fusion.2), channel_id=1, source_target_pairs={{0,4},{1,5},{2,6},{3,7},{4,0},{5,1},{6,2},{7,3},{8,12},{9,13},{10,... | collective-permute-start | bytes 589832 | tf_op jit(solution)/shard_map/ppermute | solution.py:77
  47.2 7.4 %collective-permute-start.6 = (bf16[4,4,6,4096]{3,1,2,0:T(4,128)(2,1)S(1)}, bf16[4,4,6,4096]{3,1,2,0:T(4,128)(2,1)S(1)}, u32[]{:S(2)}, u32[]{:S(2)}) collective-permute-start(bf16[4,4,6,4096]{3,1,2,0:T(4,128)(2,1)S(1)} %broadcast_select_fusion.1), channel_id=1, source_target_pairs={{0,1},{1,0},{2,3},{3,2},{4,5},{5,4},{6,7},{7,6},{8,9},{9,8},{10,11... | collective-permute-start | bytes 2359304 | tf_op jit(solution)/shard_map/ppermute | solution.py:77
  58.8 4.4 %copy-start.4 = (f32[4096]{0:T(1024)S(1)}, f32[4096]{0:T(1024)}, u32[]{:S(2)}) copy-start(f32[4096]{0:T(1024)} %param.20) | copy-start | bytes 49156
  58.8 4.4 %copy-start.5 = (f32[4096]{0:T(1024)S(1)}, f32[4096]{0:T(1024)}, u32[]{:S(2)}) copy-start(f32[4096]{0:T(1024)} %param.19) | copy-start | bytes 49156
  58.8 4.4 %copy-start.6 = (f32[4096]{0:T(1024)S(1)}, f32[4096]{0:T(1024)}, u32[]{:S(2)}) copy-start(f32[4096]{0:T(1024)} %param.18) | copy-start | bytes 49156
  58.8 4.4 %copy-start.7 = (f32[4096]{0:T(1024)S(1)}, f32[4096]{0:T(1024)}, u32[]{:S(2)}) copy-start(f32[4096]{0:T(1024)} %param.17) | copy-start | bytes 49156
  112.4 4.6 %copy-start.2 = (bf16[192,4096]{1,0:T(8,128)(2,1)S(1)}, bf16[192,4096]{1,0:T(8,128)(2,1)}, u32[]{:S(2)}) copy-start(bf16[192,4096]{1,0:T(8,128)(2,1)} %convert_element_type.70) | copy-start | bytes 4718596
  112.5 4.6 %copy-start.10 = (f32[384]{0:T(512)S(1)}, f32[384]{0:T(512)}, u32[]{:S(2)}) copy-start(f32[384]{0:T(512)} %param.22) | copy-start | bytes 4612
  121.6 2.1 copy-start.1
  184.8 6.2 %copy-start.11 = (f32[512]{0:T(512)S(1)}, f32[512]{0:T(512)}, u32[]{:S(2)}) copy-start(f32[512]{0:T(512)} %param.26) | copy-start | bytes 6148
  204.3 43.0 %copy-start.3 = (bf16[6,4096]{1,0:T(8,128)(2,1)S(1)}, bf16[6,4096]{1,0:T(8,128)(2,1)}, u32[]{:S(2)}) copy-start(bf16[6,4096]{1,0:T(8,128)(2,1)} %param.16) | copy-start | bytes 147460
  204.3 43.0 %copy-start.8 = (f32[4096]{0:T(1024)S(1)}, f32[4096]{0:T(1024)}, u32[]{:S(2)}) copy-start(f32[4096]{0:T(1024)} %param.28) | copy-start | bytes 49156
  204.3 43.0 %copy-start.9 = (f32[4096]{0:T(1024)S(1)}, f32[4096]{0:T(1024)}, u32[]{:S(2)}) copy-start(f32[4096]{0:T(1024)} %param.24) | copy-start | bytes 49156
Sparse Core Ops, SparseCore 0:
  9.4 100.7 all-gather.4
  112.3 72.5 all-gather.6

commit v2 on v0

--- a/solution.py
+++ b/solution.py
@@ -130,14 +130,15 @@
     width_up = w_up.shape[1]
     width_dense = w_dense.shape[0]
     first = lax.all_gather(jnp.concatenate([w_qkv, w_up], axis=1), "tok", axis=0, tiled=False)
-    second = lax.all_gather(
-        jnp.concatenate([w_dense, w_down], axis=0), "tok", axis=0, tiled=False
-    )
+    outgoing = jnp.concatenate([w_dense, w_down], axis=0)
+    half = outgoing.shape[1] // 2
+    seconds = [
+        lax.all_gather(outgoing[:, :half], "tok", axis=0, tiled=False),
+        lax.all_gather(outgoing[:, half:], "tok", axis=0, tiled=False),
+    ]
     parts = first.shape[0] * first.shape[1]
     qkv_full = first[:, :, :width_qkv].reshape(parts, width_qkv)
     up_full = first[:, :, width_qkv:].reshape(parts, width_up)
-    dense_parts = second[:, :width_dense, :]
-    down_parts = second[:, width_dense:, :]
     whole = head_gather(tokens)
     normed_one = layer_norm(whole, ln1_gain, ln1_bias).astype(jnp.bfloat16)
     normed_two = layer_norm(whole, ln2_gain, ln2_bias).astype(jnp.bfloat16)
@@ -169,11 +170,19 @@
     ) + jnp.dot(new_weights.astype(jnp.bfloat16), new_values, preferred_element_type=jnp.float32)
     attention = (summed / total[:, None]).astype(jnp.bfloat16)
     contract = (((1,), (1,)), ((), ()))
-    partial = lax.dot_general(
-        attention, dense_parts, contract, preferred_element_type=jnp.float32
-    ) + lax.dot_general(hidden, down_parts, contract, preferred_element_type=jnp.float32)
-    partial = partial.reshape(rows_total, -1)
-    partial_value = head_reduce_scatter(partial, tokens.shape[0])
+    heads = lax.axis_size("head")
+    halves = []
+    for second in seconds:
+        partial = lax.dot_general(
+            attention, second[:, :width_dense, :], contract, preferred_element_type=jnp.float32
+        ) + lax.dot_general(
+            hidden, second[:, width_dense:, :], contract, preferred_element_type=jnp.float32
+        )
+        blocks = partial.astype(jnp.bfloat16).reshape(heads, tokens.shape[0], -1)
+        exchanged = lax.all_to_all(blocks, "head", 0, 0, tiled=True)
+        summed = jnp.sum(exchanged.astype(jnp.float32), axis=0)
+        halves.append(summed.reshape(tokens.shape[0], -1, half))
+    partial_value = jnp.concatenate(halves, axis=2).reshape(tokens.shape)
     mixed = tokens.astype(jnp.float32) + partial_value + b_dense + b_down
     return mixed.astype(jnp.bfloat16)
 

time: 267 us -> 300 us (1.12)
  waiting for transfers between devices: 119 us -> 163 us
  local copies, waits for them, and re-layouts: 42.8 us -> 31.3 us
  starting transfers between devices: 51.5 us -> 60.2 us
  other arithmetic: 19.6 us -> 15 us
  matrix products: 19 us -> 15.2 us
    all_gather x1 -> x2, waiting for transfers between devices: 60.1 us -> 101 us  [the longest x1 52.1 us: body(): lax.all_gather(outgoing[:, :half], 'tok', axis=0, tiled=False)]
    all_to_all x0 -> x2, starting transfers between devices: none -> 33 us  [body(): exchanged = lax.all_to_all(blocks, 'head', 0, 0, tiled=True)]
    ppermute x7 -> x0, starting transfers between devices: 27.9 us -> none  [scatter_stage(): lax.ppermute(outgoing.astype(jnp.bfloat16), 'head', stage_pairs(size, str...]
    all_to_all x0 -> x2, waiting for transfers between devices: none -> 17 us  [body(): exchanged = lax.all_to_all(blocks, 'head', 0, 0, tiled=True)]
    ppermute x7 -> x0, waiting for transfers between devices: 12 us -> none  [scatter_stage(): lax.ppermute(outgoing.astype(jnp.bfloat16), 'head', stage_pairs(size, str...]
    another operation x3 -> x0, local copies, waits for them, and re-layouts: 7.1 us -> none  [the longest x1 4.94 us: head_reduce_scatter(): blocks = partial.reshape((4, 4, 2, rows) + partial.shape[1:])]
    add x1 -> x0, local copies, waits for them, and re-layouts: 5.41 us -> none  [body(): lax.dot_general(attention, dense_parts, contract, preferred_element_type=...]
    dot_general x2 -> x6, matrix products: 14.5 us -> 10.7 us  [the longest x1 4.12 us: body(): upward = jnp.dot(normed_two, up_full, preferred_element_type=jnp.float32)]
  transfers between devices with their start and end apart: 16 -> 12, of which waited for: 9 -> 8; matrix products, arithmetic and copies ran while one was open for 17% -> 19% of each run, Pallas kernels for 0% -> 0%
where the time goes in v2:
time: 300 us; the launch traced here: 299 us
  waiting for transfers between devices  163 us (54%)
  starting transfers between devices  60.2 us (20%)
  local copies, waits for them, and re-layouts  31.3 us (10%)
  matrix products  15.2 us (5%)
  other arithmetic  15 us (5%)
  between operations  13.7 us (5%)
    all_gather x1, waiting for transfers between devices, body(): lax.all_gather(outgoing[:, :half], 'tok', axis=0, tiled=False)  52.1 us
    all_gather x1, waiting for transfers between devices, body(): lax.all_gather(outgoing[:, half:], 'tok', axis=0, tiled=False)  48.8 us
    all_gather x1, waiting for transfers between devices, body(): lax.all_gather(jnp.concatenate([w_qkv, w_up], axis=1), 'tok', axis=0, til...  34.7 us
    all_to_all x2, starting transfers between devices, body(): exchanged = lax.all_to_all(blocks, 'head', 0, 0, tiled=True)  33 us
    ppermute x7, starting transfers between devices, gather_stage(): lax.ppermute(stacked, 'head', stage_pairs(size, stride, shift, total))  27.1 us
    all_to_all x2, waiting for transfers between devices, body(): exchanged = lax.all_to_all(blocks, 'head', 0, 0, tiled=True)  17 us
    ppermute x7, waiting for transfers between devices, gather_stage(): lax.ppermute(stacked, 'head', stage_pairs(size, stride, shift, total))  10.5 us
    convert_element_type x2, local copies, waits for them, and re-layouts, body(): normed_one = layer_norm(whole, ln1_gain, ln1_bias).astype(jnp.bfloat16)  6.01 us
  transfers between devices with their start and end apart: 12, of which 8 were waited for; matrix products, arithmetic and copies ran while one was open for 19% of the time, Pallas kernels for 0%

profile of v2, /device:TPU:1, one launch (start us, length us, event | category | flops | bytes accessed | tf_op | source)
XLA Modules:
  0.0 298.6 jit_solution(14638721693284110222)
XLA Ops:
  6.5 1.9 pad_maximum_fusion.2
  11.2 4.0 %collective-permute-start = (bf16[6,4096]{1,0:T(8,128)(2,1)S(1)}, bf16[6,4096]{1,0:T(8,128)(2,1)S(1)}, u32[]{:S(2)}, u32[]{:S(2)}) collective-permute-start(bf16[6,4096]{1,0:T(8,128)(2,1)S(1)} %copy-done.4), channel_id=1, source_target_pairs={{0,8},{1,9},{2,10},{3,11},{4,12},{5,13},{6,14},{7,15},{8,16},{9,17... | collective-permute-start | bytes 147464 | tf_op jit(solution)/shard_map/ppermute | solution.py:77
  15.2 4.5 %collective-permute-start.1 = (bf16[6,4096]{1,0:T(8,128)(2,1)S(1)}, bf16[6,4096]{1,0:T(8,128)(2,1)S(1)}, u32[]{:S(2)}, u32[]{:S(2)}) collective-permute-start(bf16[6,4096]{1,0:T(8,128)(2,1)S(1)} %copy-done.4), channel_id=1, source_target_pairs={{0,16},{1,17},{2,18},{3,19},{4,20},{5,21},{6,22},{7,23},{8,24},{9,... | collective-permute-start | bytes 147464 | tf_op jit(solution)/shard_map/ppermute | solution.py:77
  19.8 3.0 collective-permute-start.2
  25.8 4.1 %collective-permute-start.5 = (bf16[4,6,4096]{2,1,0:T(8,128)(2,1)S(1)}, bf16[4,6,4096]{2,1,0:T(8,128)(2,1)S(1)}, u32[]{:S(2)}, u32[]{:S(2)}) collective-permute-start(bf16[4,6,4096]{2,1,0:T(8,128)(2,1)S(1)} %broadcast_select_fusion.2), channel_id=1, source_target_pairs={{0,6},{1,7},{2,0},{3,1},{4,2},{5,3},{6,4},{7,5},{8,14},{9,15},{10,... | collective-permute-start | bytes 589832 | tf_op jit(solution)/shard_map/ppermute | solution.py:77
  29.9 1.9 collective-permute-start.3
  31.9 3.6 %collective-permute-start.4 = (bf16[4,6,4096]{2,1,0:T(8,128)(2,1)S(1)}, bf16[4,6,4096]{2,1,0:T(8,128)(2,1)S(1)}, u32[]{:S(2)}, u32[]{:S(2)}) collective-permute-start(bf16[4,6,4096]{2,1,0:T(8,128)(2,1)S(1)} %broadcast_select_fusion.2), channel_id=1, source_target_pairs={{0,4},{1,5},{2,6},{3,7},{4,0},{5,1},{6,2},{7,3},{8,12},{9,13},{10,... | collective-permute-start | bytes 589832 | tf_op jit(solution)/shard_map/ppermute | solution.py:77
  35.6 3.6 %collective-permute-done.3 = bf16[4,6,4096]{2,1,0:T(8,128)(2,1)S(1)} collective-permute-done((bf16[4,6,4096]{2,1,0:T(8,128)(2,1)S(1)}, bf16[4,6,4096]{2,1,0:T(8,128)(2,1)S(1)}, u32[]{:S(2)}, u32[]{:S(2)}) %collective-permute-start.3) | collective-permute-done | bytes 196640 | tf_op jit(solution)/shard_map/ppermute | solution.py:77
  39.2 4.3 %collective-permute-done.4 = bf16[4,6,4096]{2,1,0:T(8,128)(2,1)S(1)} collective-permute-done((bf16[4,6,4096]{2,1,0:T(8,128)(2,1)S(1)}, bf16[4,6,4096]{2,1,0:T(8,128)(2,1)S(1)}, u32[]{:S(2)}, u32[]{:S(2)}) %collective-permute-start.4) | collective-permute-done | bytes 196640 | tf_op jit(solution)/shard_map/ppermute | solution.py:77
  46.1 5.9 %collective-permute-start.6 = (bf16[4,4,6,4096]{3,1,2,0:T(4,128)(2,1)S(1)}, bf16[4,4,6,4096]{3,1,2,0:T(4,128)(2,1)S(1)}, u32[]{:S(2)}, u32[]{:S(2)}) collective-permute-start(bf16[4,4,6,4096]{3,1,2,0:T(4,128)(2,1)S(1)} %broadcast_select_fusion.1), channel_id=1, source_target_pairs={{0,1},{1,0},{2,3},{3,2},{4,5},{5,4},{6,7},{7,6},{8,9},{9,8},{10,11... | collective-permute-start | bytes 2359304 | tf_op jit(solution)/shard_map/ppermute | solution.py:77
  54.8 3.1 %gather_fusion.2 = bf16[2,4,4,6,4096]{4,2,3,1,0:T(4,128)(2,1)} fusion(bf16[2,4,4,6,4096]{4,2,3,1,0:T(4,128)(2,1)S(1)} %pad_maximum_fusion, s32[1024]{0:T(1024)S(1)} %pad_clamp_fusion), kind=kCustom, calls=%fused_computation.2 | custom fusion | bytes 3145736 | tf_op jit(solution)/shard_map/jit(_take)/gather | solution.py:80
  57.9 3.2 %bitcast_reduce_fusion = (f32[4,4,2,6]{0,3,1,2:T(8,128)S(1)}, bf16[2,4,4,6,4096]{4,2,3,1,0:T(4,128)(2,1)S(1)}) fusion(bf16[2,4,4,6,4096]{4,2,3,1,0:T(4,128)(2,1)} %gather_fusion.2, pred[2]{0:T(512)(128)(4,1)S(1)} %compare_and_fusion.2), kind=kLoop, calls=%fused_computation.12 | loop fusion | flops 2359104 | bytes 3146498 | tf_op jit(solution)/shard_map/reduce_sum | solution.py:17
  62.4 2.1 fusion.12
  64.4 2.3 copy.40
  66.7 3.7 %convert_element_type.72 = bf16[192,4096]{1,0:T(8,128)(2,1)} reshape(bf16[4,4,2,6,4096]{4,3,2,1,0:T(8,128)(2,1)} %copy.40) | data formatting | bytes 3145728 | tf_op jit(solution)/shard_map/convert_element_type | solution.py:143
  70.4 2.3 copy.42
  72.7 2.8 convert_element_type.78
  75.5 34.7 %all-gather.7.cloned.1.call-done = bf16[4096,896]{1,0:T(8,128)(2,1)} async-done(((bf16[256,896]{1,0:T(8,128)(2,1)}), bf16[4096,896]{1,0:T(8,128)(2,1)}) %all-gather.7.cloned.1.call-update) | async-done | bytes 7340048 | tf_op jit(solution)/shard_map/all_gather | solution.py:132
  110.2 2.3 slice.77
  112.5 4.7 %slice.87 = bf16[16,256,512]{2,1,0:T(8,128)(2,1)} slice(bf16[16,256,896]{2,1,0:T(8,128)(2,1)} %bitcast.73), slice={[0:16], [0:256], [384:896]} | slice | bytes 8388608 | tf_op jit(solution)/shard_map/slice | solution.py:141
  117.2 1.4 fusion.97
  119.1 2.7 fusion.98
  124.2 52.1 %all-gather.9.cloned.1.call-done = bf16[10240,128]{1,0:T(8,128)(2,1)} async-done(((bf16[640,128]{1,0:T(8,128)(2,1)}), bf16[10240,128]{1,0:T(8,128)(2,1)}) %all-gather.9.cloned.1.call-update) | async-done | bytes 2621456 | tf_op jit(solution)/shard_map/all_gather | solution.py:136
  177.7 4.1 %fusion.52 = bf16[192,512,1]{1,0,2:T(8,128)(2,1)S(1)} fusion(bf16[192,4096]{1,0:T(8,128)(2,1)S(1)} %convert_element_type.78, bf16[4096,512]{1,0:T(8,128)(2,1)} %bitcast.74, f32[512]{0:T(512)S(1)} %copy-done.13), kind=kOutput, calls=%fused_computation.72 | convolution fusion | flops 811794432 | bytes 5965824 | tf_op jit(solution)/shard_map/dot_general | solution.py:147
  183.0 1.8 reshape.353
  184.7 16.5 %all-to-all-start = ((bf16[32,6,2048]{2,1,0:T(8,128)(2,1)}), bf16[32,6,2048]{2,1,0:T(8,128)(2,1)S(1)}, u32[]{:S(2)}, u32[]{:S(2)}) async-start(bf16[32,6,2048]{2,1,0:T(8,128)(2,1)} %reshape.353), calls=%async_computation | async-start | bytes 2097152 | tf_op jit(solution)/shard_map/all_to_all | solution.py:182
  201.2 48.8 %all-gather.11.cloned.1.call-done = bf16[10240,128]{1,0:T(8,128)(2,1)} async-done(((bf16[640,128]{1,0:T(8,128)(2,1)}), bf16[10240,128]{1,0:T(8,128)(2,1)}) %all-gather.11.cloned.1.call-update) | async-done | bytes 2621456 | tf_op jit(solution)/shard_map/all_gather | solution.py:137
  251.4 2.2 add_convert_fusion
  254.2 1.9 reshape.355
  256.0 16.6 %all-to-all-start.1 = ((bf16[32,6,2048]{2,1,0:T(8,128)(2,1)}), bf16[32,6,2048]{2,1,0:T(8,128)(2,1)}, u32[]{:S(2)}, u32[]{:S(2)}) async-start(bf16[32,6,2048]{2,1,0:T(8,128)(2,1)} %reshape.355), calls=%async_computation.1 | async-start | bytes 2097152 | tf_op jit(solution)/shard_map/all_to_all | solution.py:182
  272.9 17.0 %all-to-all-done.1 = bf16[32,6,2048]{2,1,0:T(8,128)(2,1)} async-done(((bf16[32,6,2048]{2,1,0:T(8,128)(2,1)}), bf16[32,6,2048]{2,1,0:T(8,128)(2,1)}, u32[]{:S(2)}, u32[]{:S(2)}) %all-to-all-start.1) | async-done | bytes 786464 | tf_op jit(solution)/shard_map/all_to_all | solution.py:182
  289.8 1.4 convert_reduce_fusion
  (95 shorter events, 20.4 us)
Async XLA Ops:
  6.5 112.5 %copy-start = (bf16[6144,128]{1,0:T(8,128)(2,1)S(1)}, bf16[6144,128]{1,0:T(8,128)(2,1)}, u32[]{:S(2)}) copy-start(bf16[6144,128]{1,0:T(8,128)(2,1)} %param.29) | copy-start | bytes 4718596
  6.5 4.7 %copy-start.4 = (bf16[6,4096]{1,0:T(8,128)(2,1)S(1)}, bf16[6,4096]{1,0:T(8,128)(2,1)}, u32[]{:S(2)}) copy-start(bf16[6,4096]{1,0:T(8,128)(2,1)} %param.16) | copy-start | bytes 147460
  6.5 16.4 %copy-start.11 = (s32[1,33]{1,0:T(1,128)S(1)}, s32[1,33]{1,0:T(1,128)}, u32[]{:S(2)}) copy-start(s32[1,33]{1,0:T(1,128)} %param.31) | copy-start | bytes 400
  6.5 103.6 %all-gather.7.cloned.1.call-start = ((), (), s32[]{:S(2)}) async-start(), calls=%async_computation.2 | async-start | bytes 7798784 | tf_op jit(solution)/shard_map/all_gather | solution.py:132
  8.5 167.7 %all-gather.9.cloned.1.call-start = ((), (), s32[]{:S(2)}) async-start(), calls=%async_computation.3 | async-start | bytes 2785280 | tf_op jit(solution)/shard_map/all_gather | solution.py:136
  11.1 238.9 %all-gather.11.cloned.1.call-start = ((), (), s32[]{:S(2)}) async-start(), calls=%async_computation.4 | async-start | bytes 2785280 | tf_op jit(solution)/shard_map/all_gather | solution.py:137
  11.2 12.6 %collective-permute-start = (bf16[6,4096]{1,0:T(8,128)(2,1)S(1)}, bf16[6,4096]{1,0:T(8,128)(2,1)S(1)}, u32[]{:S(2)}, u32[]{:S(2)}) collective-permute-start(bf16[6,4096]{1,0:T(8,128)(2,1)S(1)} %copy-done.4), channel_id=1, source_target_pairs={{0,8},{1,9},{2,10},{3,11},{4,12},{5,13},{6,14},{7,15},{8,16},{9,17... | collective-permute-start | bytes 147464 | tf_op jit(solution)/shard_map/ppermute | solution.py:77
  15.2 8.6 %collective-permute-start.1 = (bf16[6,4096]{1,0:T(8,128)(2,1)S(1)}, bf16[6,4096]{1,0:T(8,128)(2,1)S(1)}, u32[]{:S(2)}, u32[]{:S(2)}) collective-permute-start(bf16[6,4096]{1,0:T(8,128)(2,1)S(1)} %copy-done.4), channel_id=1, source_target_pairs={{0,16},{1,17},{2,18},{3,19},{4,20},{5,21},{6,22},{7,23},{8,24},{9,... | collective-permute-start | bytes 147464 | tf_op jit(solution)/shard_map/ppermute | solution.py:77
  19.8 5.3 %collective-permute-start.2 = (bf16[6,4096]{1,0:T(8,128)(2,1)S(1)}, bf16[6,4096]{1,0:T(8,128)(2,1)S(1)}, u32[]{:S(2)}, u32[]{:S(2)}) collective-permute-start(bf16[6,4096]{1,0:T(8,128)(2,1)S(1)} %copy-done.4), channel_id=1, source_target_pairs={{0,24},{1,25},{2,26},{3,27},{4,28},{5,29},{6,30},{7,31},{8,0},{9,1... | collective-permute-start | bytes 147464 | tf_op jit(solution)/shard_map/ppermute | solution.py:77
  25.8 9.8 %collective-permute-start.5 = (bf16[4,6,4096]{2,1,0:T(8,128)(2,1)S(1)}, bf16[4,6,4096]{2,1,0:T(8,128)(2,1)S(1)}, u32[]{:S(2)}, u32[]{:S(2)}) collective-permute-start(bf16[4,6,4096]{2,1,0:T(8,128)(2,1)S(1)} %broadcast_select_fusion.2), channel_id=1, source_target_pairs={{0,6},{1,7},{2,0},{3,1},{4,2},{5,3},{6,4},{7,5},{8,14},{9,15},{10,... | collective-permute-start | bytes 589832 | tf_op jit(solution)/shard_map/ppermute | solution.py:77
  29.9 9.3 %collective-permute-start.3 = (bf16[4,6,4096]{2,1,0:T(8,128)(2,1)S(1)}, bf16[4,6,4096]{2,1,0:T(8,128)(2,1)S(1)}, u32[]{:S(2)}, u32[]{:S(2)}) collective-permute-start(bf16[4,6,4096]{2,1,0:T(8,128)(2,1)S(1)} %broadcast_select_fusion.2), channel_id=1, source_target_pairs={{0,2},{1,3},{2,4},{3,5},{4,6},{5,7},{6,0},{7,1},{8,10},{9,11},{10,... | collective-permute-start | bytes 589832 | tf_op jit(solution)/shard_map/ppermute | solution.py:77
  31.9 11.7 %collective-permute-start.4 = (bf16[4,6,4096]{2,1,0:T(8,128)(2,1)S(1)}, bf16[4,6,4096]{2,1,0:T(8,128)(2,1)S(1)}, u32[]{:S(2)}, u32[]{:S(2)}) collective-permute-start(bf16[4,6,4096]{2,1,0:T(8,128)(2,1)S(1)} %broadcast_select_fusion.2), channel_id=1, source_target_pairs={{0,4},{1,5},{2,6},{3,7},{4,0},{5,1},{6,2},{7,3},{8,12},{9,13},{10,... | collective-permute-start | bytes 589832 | tf_op jit(solution)/shard_map/ppermute | solution.py:77
  46.1 7.6 %collective-permute-start.6 = (bf16[4,4,6,4096]{3,1,2,0:T(4,128)(2,1)S(1)}, bf16[4,4,6,4096]{3,1,2,0:T(4,128)(2,1)S(1)}, u32[]{:S(2)}, u32[]{:S(2)}) collective-permute-start(bf16[4,4,6,4096]{3,1,2,0:T(4,128)(2,1)S(1)} %broadcast_select_fusion.1), channel_id=1, source_target_pairs={{0,1},{1,0},{2,3},{3,2},{4,5},{5,4},{6,7},{7,6},{8,9},{9,8},{10,11... | collective-permute-start | bytes 2359304 | tf_op jit(solution)/shard_map/ppermute | solution.py:77
  57.9 4.4 %copy-start.5 = (f32[4096]{0:T(1024)S(1)}, f32[4096]{0:T(1024)}, u32[]{:S(2)}) copy-start(f32[4096]{0:T(1024)} %param.20) | copy-start | bytes 49156
  57.9 4.4 %copy-start.6 = (f32[4096]{0:T(1024)S(1)}, f32[4096]{0:T(1024)}, u32[]{:S(2)}) copy-start(f32[4096]{0:T(1024)} %param.19) | copy-start | bytes 49156
  57.9 4.4 %copy-start.7 = (f32[4096]{0:T(1024)S(1)}, f32[4096]{0:T(1024)}, u32[]{:S(2)}) copy-start(f32[4096]{0:T(1024)} %param.18) | copy-start | bytes 49156
  57.9 4.4 %copy-start.8 = (f32[4096]{0:T(1024)S(1)}, f32[4096]{0:T(1024)}, u32[]{:S(2)}) copy-start(f32[4096]{0:T(1024)} %param.17) | copy-start | bytes 49156
  112.4 4.8 %copy-start.2 = (bf16[192,4096]{1,0:T(8,128)(2,1)S(1)}, bf16[192,4096]{1,0:T(8,128)(2,1)}, u32[]{:S(2)}) copy-start(bf16[192,4096]{1,0:T(8,128)(2,1)} %convert_element_type.72) | copy-start | bytes 4718596
  112.5 4.8 %copy-start.12 = (f32[384]{0:T(512)S(1)}, f32[384]{0:T(512)}, u32[]{:S(2)}) copy-start(f32[384]{0:T(512)} %param.22) | copy-start | bytes 4612
  121.8 1.4 copy-start.3
  123.3 54.4 %copy-start.13 = (f32[512]{0:T(512)S(1)}, f32[512]{0:T(512)}, u32[]{:S(2)}) copy-start(f32[512]{0:T(512)} %param.26) | copy-start | bytes 6148
  177.7 4.1 %copy-start.1 = (bf16[10240,128]{1,0:T(8,128)(2,1)S(1)}, bf16[10240,128]{1,0:T(8,128)(2,1)}, u32[]{:S(2)}) copy-start(bf16[10240,128]{1,0:T(8,128)(2,1)} %all-gather.9.cloned.1.call-done) | copy-start | bytes 7864324
  184.7 71.3 %all-to-all-start = ((bf16[32,6,2048]{2,1,0:T(8,128)(2,1)}), bf16[32,6,2048]{2,1,0:T(8,128)(2,1)S(1)}, u32[]{:S(2)}, u32[]{:S(2)}) async-start(bf16[32,6,2048]{2,1,0:T(8,128)(2,1)} %reshape.353), calls=%async_computation | async-start | bytes 2097152 | tf_op jit(solution)/shard_map/all_to_all | solution.py:182
  256.0 35.4 %copy-start.9 = (f32[4096]{0:T(1024)S(1)}, f32[4096]{0:T(1024)}, u32[]{:S(2)}) copy-start(f32[4096]{0:T(1024)} %param.28) | copy-start | bytes 49156
  256.0 35.4 %copy-start.10 = (f32[4096]{0:T(1024)S(1)}, f32[4096]{0:T(1024)}, u32[]{:S(2)}) copy-start(f32[4096]{0:T(1024)} %param.24) | copy-start | bytes 49156
  256.0 33.8 %all-to-all-start.1 = ((bf16[32,6,2048]{2,1,0:T(8,128)(2,1)}), bf16[32,6,2048]{2,1,0:T(8,128)(2,1)}, u32[]{:S(2)}, u32[]{:S(2)}) async-start(bf16[32,6,2048]{2,1,0:T(8,128)(2,1)} %reshape.355), calls=%async_computation.1 | async-start | bytes 2097152 | tf_op jit(solution)/shard_map/all_to_all | solution.py:182
Sparse Core Ops, SparseCore 0:
  9.4 100.7 all-gather.6
  112.3 63.9 all-gather.8
  178.3 71.6 all-gather.10

commit v3 on v1

--- a/solution.py
+++ b/solution.py
@@ -105,6 +105,24 @@
     by_core = scatter_stage(jnp.moveaxis(blocks, 2, 0), 2, 1)
     by_x = scatter_stage(jnp.moveaxis(by_core, 1, 0), 4, 2)
     return scatter_stage(by_x, 4, 8)
+
+
+def tok_ring_gather(piece):
+    count = lax.axis_size("tok")
+    position = lax.axis_index("tok")
+    forward = [(index, (index + 1) % count) for index in range(count)]
+    backward = [(index, (index - 1) % count) for index in range(count)]
+    by_offset = [piece] + [None] * (count - 1)
+    ahead = piece
+    behind = piece
+    for step in range(1, count // 2 + 1):
+        ahead = lax.ppermute(ahead, "tok", forward)
+        by_offset[step] = ahead
+        if step <= (count - 1) // 2:
+            behind = lax.ppermute(behind, "tok", backward)
+            by_offset[count - step] = behind
+    stacked = jnp.stack(by_offset)
+    return jnp.take(stacked, (position - jnp.arange(count)) % count, axis=0)
 
 
 def body(
@@ -130,9 +148,7 @@
     width_up = w_up.shape[1]
     width_dense = w_dense.shape[0]
     first = lax.all_gather(jnp.concatenate([w_qkv, w_up], axis=1), "tok", axis=0, tiled=False)
-    second = lax.all_gather(
-        jnp.concatenate([w_dense, w_down], axis=0), "tok", axis=0, tiled=False
-    )
+    second = tok_ring_gather(jnp.concatenate([w_dense, w_down], axis=0))
     parts = first.shape[0] * first.shape[1]
     qkv_full = first[:, :, :width_qkv].reshape(parts, width_qkv)
     up_full = first[:, :, width_qkv:].reshape(parts, width_up)

time: 255 us -> 293 us (1.15)
  starting transfers between devices: 27.2 us -> 80 us
  waiting for transfers between devices: 104 us -> 57.8 us
  local copies, waits for them, and re-layouts: 30.3 us -> 57.4 us
  other arithmetic: 18.3 us -> 26.3 us
  blocking collectives: 42.5 us -> 36.5 us
    all_gather x1 -> x0, waiting for transfers between devices: 60.1 us -> none  [body(): lax.all_gather(jnp.concatenate([w_dense, w_down], axis=0), 'tok', axis=0,...]
    ppermute x0 -> x15, starting transfers between devices: none -> 56.4 us  [the longest x7 40.9 us: tok_ring_gather(): behind = lax.ppermute(behind, 'tok', backward)]
    ppermute x0 -> x15, waiting for transfers between devices: none -> 46.4 us  [the longest x8 24.2 us: tok_ring_gather(): ahead = lax.ppermute(ahead, 'tok', forward)]
    all_gather x1, waiting for transfers between devices: 34 us -> 0.01 us  [body(): lax.all_gather(jnp.concatenate([w_qkv, w_up], axis=1), 'tok', axis=0, til...]
    unnamed x24 -> x60, local copies, waits for them, and re-layouts: 2.09 us -> 20.9 us
    all_to_all x1, blocking collectives: 42.5 us -> 36.5 us  [body(): exchanged = lax.all_to_all(blocks, 'head', 0, 0, tiled=True)]
    gather x0 -> x1, local copies, waits for them, and re-layouts: none -> 5.77 us  [tok_ring_gather(): return jnp.take(stacked, (position - jnp.arange(count)) % count, axis=0)]
    select_n x0 -> x2, other arithmetic: none -> 5.34 us  [tok_ring_gather(): return jnp.take(stacked, (position - jnp.arange(count)) % count, axis=0)]
  transfers between devices with their start and end apart: 9 -> 23, of which waited for: 5 -> 8; matrix products, arithmetic and copies ran while one was open for 17% -> 23% of each run, Pallas kernels for 0% -> 0%
where the time goes in v3:
time: 293 us; the launch traced here: 291 us
  starting transfers between devices  80 us (27%)
  waiting for transfers between devices  57.8 us (20%)
  local copies, waits for them, and re-layouts  57.4 us (20%)
  blocking collectives  36.5 us (12%)
  other arithmetic  26.3 us (9%)
  matrix products  19.1 us (7%)
  between operations  14.1 us (5%)
    ppermute x7, starting transfers between devices, tok_ring_gather(): behind = lax.ppermute(behind, 'tok', backward)  40.9 us
    all_to_all x1, blocking collectives, body(): exchanged = lax.all_to_all(blocks, 'head', 0, 0, tiled=True)  36.5 us
    ppermute x8, waiting for transfers between devices, tok_ring_gather(): ahead = lax.ppermute(ahead, 'tok', forward)  24.2 us
    ppermute x7, starting transfers between devices, gather_stage(): lax.ppermute(stacked, 'head', stage_pairs(size, stride, shift, total))  23.6 us
    ppermute x7, waiting for transfers between devices, tok_ring_gather(): behind = lax.ppermute(behind, 'tok', backward)  22.2 us
    unnamed x60, local copies, waits for them, and re-layouts  20.9 us
    ppermute x8, starting transfers between devices, tok_ring_gather(): ahead = lax.ppermute(ahead, 'tok', forward)  15.5 us
    ppermute x7, waiting for transfers between devices, gather_stage(): lax.ppermute(stacked, 'head', stage_pairs(size, stride, shift, total))  11.4 us
  transfers between devices with their start and end apart: 23, of which 8 were waited for; matrix products, arithmetic and copies ran while one was open for 23% of the time, Pallas kernels for 0%

profile of v3, /device:TPU:1, one launch (start us, length us, event | category | flops | bytes accessed | tf_op | source)
XLA Modules:
  0.0 291.3 jit_solution(14004757992774287644)
XLA Ops:
  6.5 4.2 %collective-permute-start = (bf16[6,4096]{1,0:T(8,128)(2,1)}, bf16[6,4096]{1,0:T(8,128)(2,1)S(1)}, u32[]{:S(2)}, u32[]{:S(2)}) collective-permute-start(bf16[6,4096]{1,0:T(8,128)(2,1)} %param.16), channel_id=1, source_target_pairs={{0,8},{1,9},{2,10},{3,11},{4,12},{5,13},{6,14},{7,15},{8,16},{9,17... | collective-permute-start | bytes 147464 | tf_op jit(solution)/shard_map/ppermute | solution.py:77
  10.7 3.4 %collective-permute-start.2 = (bf16[6,4096]{1,0:T(8,128)(2,1)}, bf16[6,4096]{1,0:T(8,128)(2,1)S(1)}, u32[]{:S(2)}, u32[]{:S(2)}) collective-permute-start(bf16[6,4096]{1,0:T(8,128)(2,1)} %param.16), channel_id=1, source_target_pairs={{0,24},{1,25},{2,26},{3,27},{4,28},{5,29},{6,30},{7,31},{8,0},{9,1... | collective-permute-start | bytes 147464 | tf_op jit(solution)/shard_map/ppermute | solution.py:77
  14.1 3.5 %collective-permute-start.1 = (bf16[6,4096]{1,0:T(8,128)(2,1)}, bf16[6,4096]{1,0:T(8,128)(2,1)S(1)}, u32[]{:S(2)}, u32[]{:S(2)}) collective-permute-start(bf16[6,4096]{1,0:T(8,128)(2,1)} %param.16), channel_id=1, source_target_pairs={{0,16},{1,17},{2,18},{3,19},{4,20},{5,21},{6,22},{7,23},{8,24},{9,... | collective-permute-start | bytes 147464 | tf_op jit(solution)/shard_map/ppermute | solution.py:77
  19.4 11.1 %collective-permute-start.15 = (bf16[640,256]{1,0:T(8,128)(2,1)S(1)}, bf16[640,256]{1,0:T(8,128)(2,1)}, u32[]{:S(2)}, u32[]{:S(2)}) collective-permute-start(bf16[640,256]{1,0:T(8,128)(2,1)S(1)} %constant_dynamic-update-slice_fusion), channel_id=1, source_target_pairs={{0,480},{32,0},{64,32},{96,64},{128,96},{160,128},{192,160},{224,1... | collective-permute-start | bytes 983048 | tf_op jit(solution)/shard_map/ppermute | solution.py:122
  44.2 4.4 %collective-permute-start.5 = (bf16[4,6,4096]{2,1,0:T(8,128)(2,1)S(1)}, bf16[4,6,4096]{2,1,0:T(8,128)(2,1)S(1)}, u32[]{:S(2)}, u32[]{:S(2)}) collective-permute-start(bf16[4,6,4096]{2,1,0:T(8,128)(2,1)S(1)} %broadcast_select_fusion.3), channel_id=1, source_target_pairs={{0,6},{1,7},{2,0},{3,1},{4,2},{5,3},{6,4},{7,5},{8,14},{9,15},{10,... | collective-permute-start | bytes 589832 | tf_op jit(solution)/shard_map/ppermute | solution.py:77
  51.0 2.5 collective-permute-start.3
  53.6 4.0 %collective-permute-done.4 = bf16[4,6,4096]{2,1,0:T(8,128)(2,1)S(1)} collective-permute-done((bf16[4,6,4096]{2,1,0:T(8,128)(2,1)S(1)}, bf16[4,6,4096]{2,1,0:T(8,128)(2,1)S(1)}, u32[]{:S(2)}, u32[]{:S(2)}) %collective-permute-start.4) | collective-permute-done | bytes 196640 | tf_op jit(solution)/shard_map/ppermute | solution.py:77
  57.7 7.3 %collective-permute-done.3 = bf16[4,6,4096]{2,1,0:T(8,128)(2,1)S(1)} collective-permute-done((bf16[4,6,4096]{2,1,0:T(8,128)(2,1)S(1)}, bf16[4,6,4096]{2,1,0:T(8,128)(2,1)S(1)}, u32[]{:S(2)}, u32[]{:S(2)}) %collective-permute-start.3) | collective-permute-done | bytes 196640 | tf_op jit(solution)/shard_map/ppermute | solution.py:77
  67.5 3.2 %collective-permute-start.6 = (bf16[4,4,6,4096]{3,1,2,0:T(4,128)(2,1)S(1)}, bf16[4,4,6,4096]{3,1,2,0:T(4,128)(2,1)S(1)}, u32[]{:S(2)}, u32[]{:S(2)}) collective-permute-start(bf16[4,4,6,4096]{3,1,2,0:T(4,128)(2,1)S(1)} %broadcast_select_fusion.2), channel_id=1, source_target_pairs={{0,1},{1,0},{2,3},{3,2},{4,5},{5,4},{6,7},{7,6},{8,9},{9,8},{10,11... | collective-permute-start | bytes 2359304 | tf_op jit(solution)/shard_map/ppermute | solution.py:77
  70.8 4.6 %collective-permute-start.16 = (bf16[640,256]{1,0:T(8,128)(2,1)}, bf16[640,256]{1,0:T(8,128)(2,1)S(1)}, u32[]{:S(2)}, u32[]{:S(2)}) collective-permute-start(bf16[640,256]{1,0:T(8,128)(2,1)} %collective-permute-done.15), channel_id=1, source_target_pairs={{0,480},{32,0},{64,32},{96,64},{128,96},{160,128},{192,160},{224,1... | collective-permute-start | bytes 983048 | tf_op jit(solution)/shard_map/ppermute | solution.py:122
  77.7 12.2 %collective-permute-done.16 = bf16[640,256]{1,0:T(8,128)(2,1)S(1)} collective-permute-done((bf16[640,256]{1,0:T(8,128)(2,1)}, bf16[640,256]{1,0:T(8,128)(2,1)S(1)}, u32[]{:S(2)}, u32[]{:S(2)}) %collective-permute-start.16) | collective-permute-done | bytes 327712 | tf_op jit(solution)/shard_map/ppermute | solution.py:122
  89.9 5.3 %collective-permute-start.17 = (bf16[640,256]{1,0:T(8,128)(2,1)S(1)}, bf16[640,256]{1,0:T(8,128)(2,1)S(1)}, u32[]{:S(2)}, u32[]{:S(2)}) collective-permute-start(bf16[640,256]{1,0:T(8,128)(2,1)S(1)} %collective-permute-done.16), channel_id=1, source_target_pairs={{0,480},{32,0},{64,32},{96,64},{128,96},{160,128},{192,160},{224,1... | collective-permute-start | bytes 983048 | tf_op jit(solution)/shard_map/ppermute | solution.py:122
  99.7 9.7 %collective-permute-done.17 = bf16[640,256]{1,0:T(8,128)(2,1)S(1)} collective-permute-done((bf16[640,256]{1,0:T(8,128)(2,1)S(1)}, bf16[640,256]{1,0:T(8,128)(2,1)S(1)}, u32[]{:S(2)}, u32[]{:S(2)}) %collective-permute-start.17) | collective-permute-done | bytes 327712 | tf_op jit(solution)/shard_map/ppermute | solution.py:122
  109.4 5.4 %collective-permute-start.18 = (bf16[640,256]{1,0:T(8,128)(2,1)S(1)}, bf16[640,256]{1,0:T(8,128)(2,1)}, u32[]{:S(2)}, u32[]{:S(2)}) collective-permute-start(bf16[640,256]{1,0:T(8,128)(2,1)S(1)} %collective-permute-done.17), channel_id=1, source_target_pairs={{0,480},{32,0},{64,32},{96,64},{128,96},{160,128},{192,160},{224,1... | collective-permute-start | bytes 983048 | tf_op jit(solution)/shard_map/ppermute | solution.py:122
  119.7 3.2 %gather_fusion.2 = bf16[2,4,4,6,4096]{4,2,3,1,0:T(4,128)(2,1)} fusion(bf16[2,4,4,6,4096]{4,2,3,1,0:T(4,128)(2,1)S(1)} %pad_maximum_fusion, s32[1024]{0:T(1024)} %pad_clamp_fusion.1), kind=kCustom, calls=%fused_computation.2 | custom fusion | bytes 3145736 | tf_op jit(solution)/shard_map/jit(_take)/gather | solution.py:80
  122.9 3.1 %bitcast_reduce_fusion = (f32[4,4,2,6]{0,3,1,2:T(8,128)S(1)}, bf16[2,4,4,6,4096]{4,2,3,1,0:T(4,128)(2,1)S(1)}) fusion(bf16[2,4,4,6,4096]{4,2,3,1,0:T(4,128)(2,1)} %gather_fusion.2, pred[2]{0:T(512)(128)(4,1)} %compare_and_fusion.3), kind=kLoop, calls=%fused_computation.17 | loop fusion | flops 2359104 | bytes 3146498 | tf_op jit(solution)/shard_map/reduce_sum | solution.py:17
  126.0 8.2 %collective-permute-done.10 = bf16[640,256]{1,0:T(8,128)(2,1)} collective-permute-done((bf16[640,256]{1,0:T(8,128)(2,1)}, bf16[640,256]{1,0:T(8,128)(2,1)}, u32[]{:S(2)}, u32[]{:S(2)}) %collective-permute-start.10) | collective-permute-done | bytes 327712 | tf_op jit(solution)/shard_map/ppermute | solution.py:119
  137.4 4.6 %collective-permute-start.19 = (bf16[640,256]{1,0:T(8,128)(2,1)}, bf16[640,256]{1,0:T(8,128)(2,1)}, u32[]{:S(2)}, u32[]{:S(2)}) collective-permute-start(bf16[640,256]{1,0:T(8,128)(2,1)} %collective-permute-done.18), channel_id=1, source_target_pairs={{0,480},{32,0},{64,32},{96,64},{128,96},{160,128},{192,160},{224,1... | collective-permute-start | bytes 983048 | tf_op jit(solution)/shard_map/ppermute | solution.py:122
  141.9 10.9 %collective-permute-done.11 = bf16[640,256]{1,0:T(8,128)(2,1)} collective-permute-done((bf16[640,256]{1,0:T(8,128)(2,1)}, bf16[640,256]{1,0:T(8,128)(2,1)}, u32[]{:S(2)}, u32[]{:S(2)}) %collective-permute-start.11) | collective-permute-done | bytes 327712 | tf_op jit(solution)/shard_map/ppermute | solution.py:119
  159.3 3.7 %convert_element_type.76 = bf16[192,4096]{1,0:T(8,128)(2,1)} reshape(bf16[4,4,2,6,4096]{4,3,2,1,0:T(8,128)(2,1)} %copy.37) | data formatting | bytes 3145728 | tf_op jit(solution)/shard_map/convert_element_type | solution.py:159
  165.3 2.5 convert_element_type.70
  167.8 4.7 %collective-permute-start.20 = (bf16[640,256]{1,0:T(8,128)(2,1)}, bf16[640,256]{1,0:T(8,128)(2,1)S(1)}, u32[]{:S(2)}, u32[]{:S(2)}) collective-permute-start(bf16[640,256]{1,0:T(8,128)(2,1)} %collective-permute-done.19), channel_id=1, source_target_pairs={{0,480},{32,0},{64,32},{96,64},{128,96},{160,128},{192,160},{224,1... | collective-permute-start | bytes 983048 | tf_op jit(solution)/shard_map/ppermute | solution.py:122
  178.2 5.2 %collective-permute-start.21 = (bf16[640,256]{1,0:T(8,128)(2,1)S(1)}, bf16[640,256]{1,0:T(8,128)(2,1)S(1)}, u32[]{:S(2)}, u32[]{:S(2)}) collective-permute-start(bf16[640,256]{1,0:T(8,128)(2,1)S(1)} %collective-permute-done.20), channel_id=1, source_target_pairs={{0,480},{32,0},{64,32},{96,64},{128,96},{160,128},{192,160},{224,1... | collective-permute-start | bytes 983048 | tf_op jit(solution)/shard_map/ppermute | solution.py:122
  187.8 5.0 %collective-permute-done.14 = bf16[640,256]{1,0:T(8,128)(2,1)S(1)} collective-permute-done((bf16[640,256]{1,0:T(8,128)(2,1)S(1)}, bf16[640,256]{1,0:T(8,128)(2,1)S(1)}, u32[]{:S(2)}, u32[]{:S(2)}) %collective-permute-start.14) | collective-permute-done | bytes 327712 | tf_op jit(solution)/shard_map/ppermute | solution.py:119
  201.8 5.8 %gather_fusion.3 = bf16[16,640,256]{2,1,0:T(8,128)(2,1)} fusion(bf16[16,640,256]{2,1,0:T(8,128)(2,1)} %bitcast_dynamic-update-slice_fusion, s32[1024]{0:T(1024)} %pad_clamp_fusion), kind=kCustom, calls=%fused_computation.3 | custom fusion | bytes 10485824 | tf_op jit(solution)/shard_map/jit(_take)/gather | solution.py:125
  207.6 5.3 %broadcast_select_fusion = bf16[16,640,256]{2,1,0:T(8,128)(2,1)} fusion(bf16[16,640,256]{2,1,0:T(8,128)(2,1)} %gather_fusion.3, pred[16]{0:T(512)(128)(4,1)S(1)} %copy-done.18), kind=kLoop, calls=%fused_computation.6 | loop fusion | flops 2621440 | bytes 10485776 | tf_op jit(solution)/shard_map/jit(_take)/select_n | solution.py:125
  215.2 4.5 %slice.72 = bf16[16,256,512]{2,1,0:T(8,128)(2,1)} slice(bf16[16,256,896]{2,1,0:T(8,128)(2,1)} %bitcast.94), slice={[0:16], [0:256], [384:896]} | slice | bytes 8388608 | tf_op jit(solution)/shard_map/slice | solution.py:154
  221.7 2.7 fusion.158
  227.3 6.2 %fusion.35 = f32[192,16,256]{2,0,1:T(8,128)} fusion(f32[192,128]{1,0:T(8,128)S(1)} %fusion.84, bf16[6144,128]{1,0:T(8,128)(2,1)} %param.30, f32[192,6144]{1,0:T(8,128)} %copy-done.1, f32[192]{0:T(256)S(1)} %max.37, bf16[16,640,256]{2,1,0:T(8,128)(2,1)} %broadcast_select_fusion, f32[192]{0:T(256)S(1)} %add.287), kind=kOutput, calls=%fused_computation.40 | convolution fusion | flops 505749504 | bytes 10585600 | tf_op jit(solution)/shard_map/dot_general | solution.py:188
  233.5 8.3 %add_convert_fusion = bf16[192,16,256]{2,0,1:T(8,128)(2,1)} fusion(f32[192,16,256]{2,0,1:T(8,128)} %fusion.35, bf16[16,640,256]{2,1,0:T(8,128)(2,1)} %broadcast_select_fusion, bf16[192,4096]{1,0:T(8,128)(2,1)S(1)} %copy-done.2, bf16[4096,512]{1,0:T(8,128)(2,1)} %bitcast.95, f32[512]{0:T(512)S(1)} %copy-done.20), kind=kOutput, calls=%fused_computation.27 | convolution fusion | flops 1618673664 | bytes 14682112 | tf_op jit(solution)/shard_map/dot_general | solution.py:190
  244.1 2.7 convert_element_type.79
  246.8 36.5 %all_to_all.5 = bf16[32,6,4096]{2,1,0:T(8,128)(2,1)S(1)} all-to-all(bf16[32,6,4096]{2,1,0:T(8,128)(2,1)} %convert_element_type.79), channel_id=1, replica_groups=mesh['tok'=16,'head'=32] {'head'}, dimensions={0} | all-to-all | bytes 3145728 | tf_op jit(solution)/shard_map/all_to_all | solution.py:194
  (141 shorter events, 73.1 us)
Async XLA Ops:
  6.5 215.1 %copy-start = (bf16[6144,128]{1,0:T(8,128)(2,1)S(1)}, bf16[6144,128]{1,0:T(8,128)(2,1)}, u32[]{:S(2)}) copy-start(bf16[6144,128]{1,0:T(8,128)(2,1)} %param.29) | copy-start | bytes 4718596
  6.5 206.4 %all-gather.3.cloned.1.call-start = ((), (), s32[]{:S(2)}) async-start(), calls=%async_computation.1 | async-start | bytes 7798784 | tf_op jit(solution)/shard_map/all_gather | solution.py:150
  6.5 36.0 %collective-permute-start = (bf16[6,4096]{1,0:T(8,128)(2,1)}, bf16[6,4096]{1,0:T(8,128)(2,1)S(1)}, u32[]{:S(2)}, u32[]{:S(2)}) collective-permute-start(bf16[6,4096]{1,0:T(8,128)(2,1)} %param.16), channel_id=1, source_target_pairs={{0,8},{1,9},{2,10},{3,11},{4,12},{5,13},{6,14},{7,15},{8,16},{9,17... | collective-permute-start | bytes 147464 | tf_op jit(solution)/shard_map/ppermute | solution.py:77
  10.7 31.9 %collective-permute-start.2 = (bf16[6,4096]{1,0:T(8,128)(2,1)}, bf16[6,4096]{1,0:T(8,128)(2,1)S(1)}, u32[]{:S(2)}, u32[]{:S(2)}) collective-permute-start(bf16[6,4096]{1,0:T(8,128)(2,1)} %param.16), channel_id=1, source_target_pairs={{0,24},{1,25},{2,26},{3,27},{4,28},{5,29},{6,30},{7,31},{8,0},{9,1... | collective-permute-start | bytes 147464 | tf_op jit(solution)/shard_map/ppermute | solution.py:77
  14.1 28.5 %collective-permute-start.1 = (bf16[6,4096]{1,0:T(8,128)(2,1)}, bf16[6,4096]{1,0:T(8,128)(2,1)S(1)}, u32[]{:S(2)}, u32[]{:S(2)}) collective-permute-start(bf16[6,4096]{1,0:T(8,128)(2,1)} %param.16), channel_id=1, source_target_pairs={{0,16},{1,17},{2,18},{3,19},{4,20},{5,21},{6,22},{7,23},{8,24},{9,... | collective-permute-start | bytes 147464 | tf_op jit(solution)/shard_map/ppermute | solution.py:77
  19.4 51.3 %collective-permute-start.15 = (bf16[640,256]{1,0:T(8,128)(2,1)S(1)}, bf16[640,256]{1,0:T(8,128)(2,1)}, u32[]{:S(2)}, u32[]{:S(2)}) collective-permute-start(bf16[640,256]{1,0:T(8,128)(2,1)S(1)} %constant_dynamic-update-slice_fusion), channel_id=1, source_target_pairs={{0,480},{32,0},{64,32},{96,64},{128,96},{160,128},{192,160},{224,1... | collective-permute-start | bytes 983048 | tf_op jit(solution)/shard_map/ppermute | solution.py:122
  30.6 44.8 %collective-permute-start.7 = (bf16[640,256]{1,0:T(8,128)(2,1)S(1)}, bf16[640,256]{1,0:T(8,128)(2,1)}, u32[]{:S(2)}, u32[]{:S(2)}) collective-permute-start(bf16[640,256]{1,0:T(8,128)(2,1)S(1)} %constant_dynamic-update-slice_fusion), channel_id=1, source_target_pairs={{0,32},{32,64},{64,96},{96,128},{128,160},{160,192},{192,224},{224... | collective-permute-start | bytes 983048 | tf_op jit(solution)/shard_map/ppermute | solution.py:119
  44.2 9.5 %collective-permute-start.5 = (bf16[4,6,4096]{2,1,0:T(8,128)(2,1)S(1)}, bf16[4,6,4096]{2,1,0:T(8,128)(2,1)S(1)}, u32[]{:S(2)}, u32[]{:S(2)}) collective-permute-start(bf16[4,6,4096]{2,1,0:T(8,128)(2,1)S(1)} %broadcast_select_fusion.3), channel_id=1, source_target_pairs={{0,6},{1,7},{2,0},{3,1},{4,2},{5,3},{6,4},{7,5},{8,14},{9,15},{10,... | collective-permute-start | bytes 589832 | tf_op jit(solution)/shard_map/ppermute | solution.py:77
  48.6 9.1 %collective-permute-start.4 = (bf16[4,6,4096]{2,1,0:T(8,128)(2,1)S(1)}, bf16[4,6,4096]{2,1,0:T(8,128)(2,1)S(1)}, u32[]{:S(2)}, u32[]{:S(2)}) collective-permute-start(bf16[4,6,4096]{2,1,0:T(8,128)(2,1)S(1)} %broadcast_select_fusion.3), channel_id=1, source_target_pairs={{0,4},{1,5},{2,6},{3,7},{4,0},{5,1},{6,2},{7,3},{8,12},{9,13},{10,... | collective-permute-start | bytes 589832 | tf_op jit(solution)/shard_map/ppermute | solution.py:77
  51.0 14.0 %collective-permute-start.3 = (bf16[4,6,4096]{2,1,0:T(8,128)(2,1)S(1)}, bf16[4,6,4096]{2,1,0:T(8,128)(2,1)S(1)}, u32[]{:S(2)}, u32[]{:S(2)}) collective-permute-start(bf16[4,6,4096]{2,1,0:T(8,128)(2,1)S(1)} %broadcast_select_fusion.3), channel_id=1, source_target_pairs={{0,2},{1,3},{2,4},{3,5},{4,6},{5,7},{6,0},{7,1},{8,10},{9,11},{10,... | collective-permute-start | bytes 589832 | tf_op jit(solution)/shard_map/ppermute | solution.py:77
  67.5 51.0 %collective-permute-start.6 = (bf16[4,4,6,4096]{3,1,2,0:T(4,128)(2,1)S(1)}, bf16[4,4,6,4096]{3,1,2,0:T(4,128)(2,1)S(1)}, u32[]{:S(2)}, u32[]{:S(2)}) collective-permute-start(bf16[4,4,6,4096]{3,1,2,0:T(4,128)(2,1)S(1)} %broadcast_select_fusion.2), channel_id=1, source_target_pairs={{0,1},{1,0},{2,3},{3,2},{4,5},{5,4},{6,7},{7,6},{8,9},{9,8},{10,11... | collective-permute-start | bytes 2359304 | tf_op jit(solution)/shard_map/ppermute | solution.py:77
  70.8 19.1 %collective-permute-start.16 = (bf16[640,256]{1,0:T(8,128)(2,1)}, bf16[640,256]{1,0:T(8,128)(2,1)S(1)}, u32[]{:S(2)}, u32[]{:S(2)}) collective-permute-start(bf16[640,256]{1,0:T(8,128)(2,1)} %collective-permute-done.15), channel_id=1, source_target_pairs={{0,480},{32,0},{64,32},{96,64},{128,96},{160,128},{192,160},{224,1... | collective-permute-start | bytes 983048 | tf_op jit(solution)/shard_map/ppermute | solution.py:122
  75.4 19.9 %collective-permute-start.8 = (bf16[640,256]{1,0:T(8,128)(2,1)}, bf16[640,256]{1,0:T(8,128)(2,1)S(1)}, u32[]{:S(2)}, u32[]{:S(2)}) collective-permute-start(bf16[640,256]{1,0:T(8,128)(2,1)} %collective-permute-done.7), channel_id=1, source_target_pairs={{0,32},{32,64},{64,96},{96,128},{128,160},{160,192},{192,224},{224... | collective-permute-start | bytes 983048 | tf_op jit(solution)/shard_map/ppermute | solution.py:119
  89.9 19.5 %collective-permute-start.17 = (bf16[640,256]{1,0:T(8,128)(2,1)S(1)}, bf16[640,256]{1,0:T(8,128)(2,1)S(1)}, u32[]{:S(2)}, u32[]{:S(2)}) collective-permute-start(bf16[640,256]{1,0:T(8,128)(2,1)S(1)} %collective-permute-done.16), channel_id=1, source_target_pairs={{0,480},{32,0},{64,32},{96,64},{128,96},{160,128},{192,160},{224,1... | collective-permute-start | bytes 983048 | tf_op jit(solution)/shard_map/ppermute | solution.py:122
  95.3 19.6 %collective-permute-start.9 = (bf16[640,256]{1,0:T(8,128)(2,1)S(1)}, bf16[640,256]{1,0:T(8,128)(2,1)}, u32[]{:S(2)}, u32[]{:S(2)}) collective-permute-start(bf16[640,256]{1,0:T(8,128)(2,1)S(1)} %collective-permute-done.8), channel_id=1, source_target_pairs={{0,32},{32,64},{64,96},{96,128},{128,160},{160,192},{192,224},{224... | collective-permute-start | bytes 983048 | tf_op jit(solution)/shard_map/ppermute | solution.py:119
  109.4 28.0 %collective-permute-start.18 = (bf16[640,256]{1,0:T(8,128)(2,1)S(1)}, bf16[640,256]{1,0:T(8,128)(2,1)}, u32[]{:S(2)}, u32[]{:S(2)}) collective-permute-start(bf16[640,256]{1,0:T(8,128)(2,1)S(1)} %collective-permute-done.17), channel_id=1, source_target_pairs={{0,480},{32,0},{64,32},{96,64},{128,96},{160,128},{192,160},{224,1... | collective-permute-start | bytes 983048 | tf_op jit(solution)/shard_map/ppermute | solution.py:122
  114.8 19.4 %collective-permute-start.10 = (bf16[640,256]{1,0:T(8,128)(2,1)}, bf16[640,256]{1,0:T(8,128)(2,1)}, u32[]{:S(2)}, u32[]{:S(2)}) collective-permute-start(bf16[640,256]{1,0:T(8,128)(2,1)} %collective-permute-done.9), channel_id=1, source_target_pairs={{0,32},{32,64},{64,96},{96,128},{128,160},{160,192},{192,224},{224... | collective-permute-start | bytes 983048 | tf_op jit(solution)/shard_map/ppermute | solution.py:119
  119.6 35.4 %copy-start.6 = (f32[4096]{0:T(1024)S(1)}, f32[4096]{0:T(1024)}, u32[]{:S(2)}) copy-start(f32[4096]{0:T(1024)} %param.20) | copy-start | bytes 49156
  119.6 35.4 %copy-start.7 = (f32[4096]{0:T(1024)S(1)}, f32[4096]{0:T(1024)}, u32[]{:S(2)}) copy-start(f32[4096]{0:T(1024)} %param.19) | copy-start | bytes 49156
  122.9 32.1 %copy-start.8 = (f32[4096]{0:T(1024)S(1)}, f32[4096]{0:T(1024)}, u32[]{:S(2)}) copy-start(f32[4096]{0:T(1024)} %param.18) | copy-start | bytes 49156
  122.9 32.1 %copy-start.9 = (f32[4096]{0:T(1024)S(1)}, f32[4096]{0:T(1024)}, u32[]{:S(2)}) copy-start(f32[4096]{0:T(1024)} %param.17) | copy-start | bytes 49156
  134.3 18.6 %collective-permute-start.11 = (bf16[640,256]{1,0:T(8,128)(2,1)}, bf16[640,256]{1,0:T(8,128)(2,1)}, u32[]{:S(2)}, u32[]{:S(2)}) collective-permute-start(bf16[640,256]{1,0:T(8,128)(2,1)} %collective-permute-done.10), channel_id=1, source_target_pairs={{0,32},{32,64},{64,96},{96,128},{128,160},{160,192},{192,224},{224... | collective-permute-start | bytes 983048 | tf_op jit(solution)/shard_map/ppermute | solution.py:119
  137.4 30.4 %collective-permute-start.19 = (bf16[640,256]{1,0:T(8,128)(2,1)}, bf16[640,256]{1,0:T(8,128)(2,1)}, u32[]{:S(2)}, u32[]{:S(2)}) collective-permute-start(bf16[640,256]{1,0:T(8,128)(2,1)} %collective-permute-done.18), channel_id=1, source_target_pairs={{0,480},{32,0},{64,32},{96,64},{128,96},{160,128},{192,160},{224,1... | collective-permute-start | bytes 983048 | tf_op jit(solution)/shard_map/ppermute | solution.py:122
  152.9 19.7 %collective-permute-start.12 = (bf16[640,256]{1,0:T(8,128)(2,1)}, bf16[640,256]{1,0:T(8,128)(2,1)}, u32[]{:S(2)}, u32[]{:S(2)}) collective-permute-start(bf16[640,256]{1,0:T(8,128)(2,1)} %collective-permute-done.11), channel_id=1, source_target_pairs={{0,32},{32,64},{64,96},{96,128},{128,160},{160,192},{192,224},{224... | collective-permute-start | bytes 983048 | tf_op jit(solution)/shard_map/ppermute | solution.py:119
  167.8 31.5 %copy-start.4 = (bf16[640,256]{1,0:T(8,128)(2,1)S(1)}, bf16[640,256]{1,0:T(8,128)(2,1)}, u32[]{:S(2)}) copy-start(bf16[640,256]{1,0:T(8,128)(2,1)} %copy-done.3) | copy-start | bytes 983044
  167.8 10.3 %collective-permute-start.20 = (bf16[640,256]{1,0:T(8,128)(2,1)}, bf16[640,256]{1,0:T(8,128)(2,1)S(1)}, u32[]{:S(2)}, u32[]{:S(2)}) collective-permute-start(bf16[640,256]{1,0:T(8,128)(2,1)} %collective-permute-done.19), channel_id=1, source_target_pairs={{0,480},{32,0},{64,32},{96,64},{128,96},{160,128},{192,160},{224,1... | collective-permute-start | bytes 983048 | tf_op jit(solution)/shard_map/ppermute | solution.py:122
  172.5 10.8 %collective-permute-start.13 = (bf16[640,256]{1,0:T(8,128)(2,1)}, bf16[640,256]{1,0:T(8,128)(2,1)S(1)}, u32[]{:S(2)}, u32[]{:S(2)}) collective-permute-start(bf16[640,256]{1,0:T(8,128)(2,1)} %collective-permute-done.12), channel_id=1, source_target_pairs={{0,32},{32,64},{64,96},{96,128},{128,160},{160,192},{192,224},{224... | collective-permute-start | bytes 983048 | tf_op jit(solution)/shard_map/ppermute | solution.py:119
  178.2 15.4 %collective-permute-start.21 = (bf16[640,256]{1,0:T(8,128)(2,1)S(1)}, bf16[640,256]{1,0:T(8,128)(2,1)S(1)}, u32[]{:S(2)}, u32[]{:S(2)}) collective-permute-start(bf16[640,256]{1,0:T(8,128)(2,1)S(1)} %collective-permute-done.20), channel_id=1, source_target_pairs={{0,480},{32,0},{64,32},{96,64},{128,96},{160,128},{192,160},{224,1... | collective-permute-start | bytes 983048 | tf_op jit(solution)/shard_map/ppermute | solution.py:122
  183.4 9.4 %collective-permute-start.14 = (bf16[640,256]{1,0:T(8,128)(2,1)S(1)}, bf16[640,256]{1,0:T(8,128)(2,1)S(1)}, u32[]{:S(2)}, u32[]{:S(2)}) collective-permute-start(bf16[640,256]{1,0:T(8,128)(2,1)S(1)} %collective-permute-done.13), channel_id=1, source_target_pairs={{0,32},{32,64},{64,96},{96,128},{128,160},{160,192},{192,224},{224... | collective-permute-start | bytes 983048 | tf_op jit(solution)/shard_map/ppermute | solution.py:119
  244.1 39.6 %copy-start.5 = (bf16[6,4096]{1,0:T(8,128)(2,1)S(1)}, bf16[6,4096]{1,0:T(8,128)(2,1)}, u32[]{:S(2)}) copy-start(bf16[6,4096]{1,0:T(8,128)(2,1)} %param.16) | copy-start | bytes 147460
  244.1 39.6 %copy-start.10 = (f32[4096]{0:T(1024)S(1)}, f32[4096]{0:T(1024)}, u32[]{:S(2)}) copy-start(f32[4096]{0:T(1024)} %param.28) | copy-start | bytes 49156
  244.1 39.6 %copy-start.11 = (f32[4096]{0:T(1024)S(1)}, f32[4096]{0:T(1024)}, u32[]{:S(2)}) copy-start(f32[4096]{0:T(1024)} %param.24) | copy-start | bytes 49156
  (13 other events, 68.3 us)
Sparse Core Ops, SparseCore 0:
  34.5 118.1 all-gather.2

commit v4 on v1

--- a/solution.py
+++ b/solution.py
@@ -174,8 +174,16 @@
     ) + lax.dot_general(hidden, down_parts, contract, preferred_element_type=jnp.float32)
     partial = partial.reshape(rows_total, -1)
     heads = lax.axis_size("head")
-    blocks = partial.astype(jnp.bfloat16).reshape(heads, tokens.shape[0], -1)
-    exchanged = lax.all_to_all(blocks, "head", 0, 0, tiled=True)
+    blocks = partial.reshape(heads // 2, 2, tokens.shape[0], -1)
+    core = lax.axis_index("head") % 2
+    mine = lax.dynamic_index_in_dim(blocks, core, 1, keepdims=False)
+    theirs = lax.dynamic_index_in_dim(blocks, 1 - core, 1, keepdims=False)
+    swapped = lax.ppermute(
+        theirs.astype(jnp.bfloat16), "head", [(index, index ^ 1) for index in range(heads)]
+    )
+    chip_sum = (mine + swapped.astype(jnp.float32)).astype(jnp.bfloat16)
+    groups = [list(range(side, heads, 2)) for side in range(2)]
+    exchanged = lax.all_to_all(chip_sum, "head", 0, 0, axis_index_groups=groups, tiled=True)
     partial_value = jnp.sum(exchanged.astype(jnp.float32), axis=0)
     mixed = tokens.astype(jnp.float32) + partial_value + b_dense + b_down
     return mixed.astype(jnp.bfloat16)

time: 255 us -> 255 us (level)
  blocking collectives: 42.5 us -> 22.8 us
  local copies, waits for them, and re-layouts: 30.3 us -> 39.9 us
  starting transfers between devices: 27.2 us -> 36.1 us
    all_to_all x1, blocking collectives: 42.5 us -> 22.8 us  [body(): lax.all_to_all(chip_sum, 'head', 0, 0, axis_index_groups=groups, tiled=True)]
    ppermute x0 -> x1, starting transfers between devices: none -> 8.9 us  [body(): lax.ppermute(theirs.astype(jnp.bfloat16), 'head', [(index, index ^ 1) for...]
    add x0 -> x1, local copies, waits for them, and re-layouts: none -> 5.39 us  [body(): lax.dot_general(attention, dense_parts, contract, preferred_element_type=...]
    another operation x0 -> x1, local copies, waits for them, and re-layouts: none -> 4.92 us  [body(): blocks = partial.reshape(heads // 2, 2, tokens.shape[0], -1)]
  transfers between devices with their start and end apart: 9 -> 10, of which waited for: 5 -> 6; matrix products, arithmetic and copies ran while one was open for 17% -> 18% of each run, Pallas kernels for 0% -> 0%
where the time goes in v4:
time: 255 us
  waiting for transfers between devices  104 us (41%)
  local copies, waits for them, and re-layouts  39.9 us (16%)
  starting transfers between devices  36.1 us (14%)
  blocking collectives  22.8 us (9%)
  other arithmetic  19 us (7%)
  matrix products  19 us (7%)
  between operations  14 us (5%)
    all_gather x1, waiting for transfers between devices, body(): lax.all_gather(jnp.concatenate([w_dense, w_down], axis=0), 'tok', axis=0,...  60 us
    all_gather x1, waiting for transfers between devices, body(): lax.all_gather(jnp.concatenate([w_qkv, w_up], axis=1), 'tok', axis=0, til...  34.1 us
    ppermute x7, starting transfers between devices, gather_stage(): lax.ppermute(stacked, 'head', stage_pairs(size, stride, shift, total))  27.2 us
    all_to_all x1, blocking collectives, body(): lax.all_to_all(chip_sum, 'head', 0, 0, axis_index_groups=groups, tiled=True)  22.8 us
    ppermute x7, waiting for transfers between devices, gather_stage(): lax.ppermute(stacked, 'head', stage_pairs(size, stride, shift, total))  9.45 us
    ppermute x1, starting transfers between devices, body(): lax.ppermute(theirs.astype(jnp.bfloat16), 'head', [(index, index ^ 1) for...  8.9 us
    dot_general x1, matrix products, body(): lax.dot_general(hidden, down_parts, contract, preferred_element_type=jnp....  8.76 us
    convert_element_type x2, local copies, waits for them, and re-layouts, body(): normed_one = layer_norm(whole, ln1_gain, ln1_bias).astype(jnp.bfloat16)  5.89 us
  transfers between devices with their start and end apart: 10, of which 6 were waited for; matrix products, arithmetic and copies ran while one was open for 18% of the time, Pallas kernels for 0%

profile of v4, /device:TPU:1, one launch (start us, length us, event | category | flops | bytes accessed | tf_op | source)
XLA Modules:
  0.0 254.6 jit_solution(13593964356162737391)
XLA Ops:
  6.5 2.0 pad_maximum_fusion.2
  8.6 4.0 %collective-permute-start = (bf16[6,4096]{1,0:T(8,128)(2,1)}, bf16[6,4096]{1,0:T(8,128)(2,1)S(1)}, u32[]{:S(2)}, u32[]{:S(2)}) collective-permute-start(bf16[6,4096]{1,0:T(8,128)(2,1)} %param.16), channel_id=1, source_target_pairs={{0,8},{1,9},{2,10},{3,11},{4,12},{5,13},{6,14},{7,15},{8,16},{9,17... | collective-permute-start | bytes 147464 | tf_op jit(solution)/shard_map/ppermute | solution.py:77
  12.6 4.5 %collective-permute-start.1 = (bf16[6,4096]{1,0:T(8,128)(2,1)}, bf16[6,4096]{1,0:T(8,128)(2,1)S(1)}, u32[]{:S(2)}, u32[]{:S(2)}) collective-permute-start(bf16[6,4096]{1,0:T(8,128)(2,1)} %param.16), channel_id=1, source_target_pairs={{0,16},{1,17},{2,18},{3,19},{4,20},{5,21},{6,22},{7,23},{8,24},{9,... | collective-permute-start | bytes 147464 | tf_op jit(solution)/shard_map/ppermute | solution.py:77
  17.2 3.0 %collective-permute-start.2 = (bf16[6,4096]{1,0:T(8,128)(2,1)}, bf16[6,4096]{1,0:T(8,128)(2,1)S(1)}, u32[]{:S(2)}, u32[]{:S(2)}) collective-permute-start(bf16[6,4096]{1,0:T(8,128)(2,1)} %param.16), channel_id=1, source_target_pairs={{0,24},{1,25},{2,26},{3,27},{4,28},{5,29},{6,30},{7,31},{8,0},{9,1... | collective-permute-start | bytes 147464 | tf_op jit(solution)/shard_map/ppermute | solution.py:77
  20.1 1.7 pad_maximum_fusion.3
  26.4 4.4 %collective-permute-start.5 = (bf16[4,6,4096]{2,1,0:T(8,128)(2,1)S(1)}, bf16[4,6,4096]{2,1,0:T(8,128)(2,1)S(1)}, u32[]{:S(2)}, u32[]{:S(2)}) collective-permute-start(bf16[4,6,4096]{2,1,0:T(8,128)(2,1)S(1)} %broadcast_select_fusion.2), channel_id=1, source_target_pairs={{0,6},{1,7},{2,0},{3,1},{4,2},{5,3},{6,4},{7,5},{8,14},{9,15},{10,... | collective-permute-start | bytes 589832 | tf_op jit(solution)/shard_map/ppermute | solution.py:77
  30.8 1.9 collective-permute-start.3
  32.8 3.6 %collective-permute-start.4 = (bf16[4,6,4096]{2,1,0:T(8,128)(2,1)S(1)}, bf16[4,6,4096]{2,1,0:T(8,128)(2,1)S(1)}, u32[]{:S(2)}, u32[]{:S(2)}) collective-permute-start(bf16[4,6,4096]{2,1,0:T(8,128)(2,1)S(1)} %broadcast_select_fusion.2), channel_id=1, source_target_pairs={{0,4},{1,5},{2,6},{3,7},{4,0},{5,1},{6,2},{7,3},{8,12},{9,13},{10,... | collective-permute-start | bytes 589832 | tf_op jit(solution)/shard_map/ppermute | solution.py:77
  36.5 4.4 %collective-permute-done.3 = bf16[4,6,4096]{2,1,0:T(8,128)(2,1)S(1)} collective-permute-done((bf16[4,6,4096]{2,1,0:T(8,128)(2,1)S(1)}, bf16[4,6,4096]{2,1,0:T(8,128)(2,1)S(1)}, u32[]{:S(2)}, u32[]{:S(2)}) %collective-permute-start.3) | collective-permute-done | bytes 196640 | tf_op jit(solution)/shard_map/ppermute | solution.py:77
  40.9 3.8 %collective-permute-done.4 = bf16[4,6,4096]{2,1,0:T(8,128)(2,1)S(1)} collective-permute-done((bf16[4,6,4096]{2,1,0:T(8,128)(2,1)S(1)}, bf16[4,6,4096]{2,1,0:T(8,128)(2,1)S(1)}, u32[]{:S(2)}, u32[]{:S(2)}) %collective-permute-start.4) | collective-permute-done | bytes 196640 | tf_op jit(solution)/shard_map/ppermute | solution.py:77
  47.2 5.7 %collective-permute-start.6 = (bf16[4,4,6,4096]{3,1,2,0:T(4,128)(2,1)S(1)}, bf16[4,4,6,4096]{3,1,2,0:T(4,128)(2,1)S(1)}, u32[]{:S(2)}, u32[]{:S(2)}) collective-permute-start(bf16[4,4,6,4096]{3,1,2,0:T(4,128)(2,1)S(1)} %broadcast_select_fusion.1), channel_id=1, source_target_pairs={{0,1},{1,0},{2,3},{3,2},{4,5},{5,4},{6,7},{7,6},{8,9},{9,8},{10,11... | collective-permute-start | bytes 2359304 | tf_op jit(solution)/shard_map/ppermute | solution.py:77
  55.7 3.0 %gather_fusion.2 = bf16[2,4,4,6,4096]{4,2,3,1,0:T(4,128)(2,1)} fusion(bf16[2,4,4,6,4096]{4,2,3,1,0:T(4,128)(2,1)S(1)} %pad_maximum_fusion, s32[1024]{0:T(1024)S(1)} %pad_clamp_fusion), kind=kCustom, calls=%fused_computation.2 | custom fusion | bytes 3145736 | tf_op jit(solution)/shard_map/jit(_take)/gather | solution.py:80
  58.7 3.2 %bitcast_reduce_fusion = (f32[4,4,2,6]{0,3,1,2:T(8,128)S(1)}, bf16[2,4,4,6,4096]{4,2,3,1,0:T(4,128)(2,1)S(1)}) fusion(bf16[2,4,4,6,4096]{4,2,3,1,0:T(4,128)(2,1)} %gather_fusion.2, pred[2]{0:T(512)(128)(4,1)S(1)} %compare_and_fusion.2), kind=kLoop, calls=%fused_computation.14 | loop fusion | flops 2359104 | bytes 3146498 | tf_op jit(solution)/shard_map/reduce_sum | solution.py:17
  63.2 2.1 fusion.14
  65.2 2.2 copy.50
  67.4 3.7 %convert_element_type.75 = bf16[192,4096]{1,0:T(8,128)(2,1)} reshape(bf16[4,4,2,6,4096]{4,3,2,1,0:T(8,128)(2,1)} %copy.50) | data formatting | bytes 3145728 | tf_op jit(solution)/shard_map/convert_element_type | solution.py:142
  71.1 2.2 copy.52
  73.3 2.8 %convert_element_type.81 = bf16[192,4096]{1,0:T(8,128)(2,1)S(1)} reshape(bf16[4,4,2,6,4096]{4,3,2,1,0:T(8,128)(2,1)} %copy.52) | data formatting | bytes 3145728 | tf_op jit(solution)/shard_map/convert_element_type | solution.py:143
  76.1 34.1 %all-gather.5.cloned.1.call-done = bf16[4096,896]{1,0:T(8,128)(2,1)} async-done(((bf16[256,896]{1,0:T(8,128)(2,1)}), bf16[4096,896]{1,0:T(8,128)(2,1)}) %all-gather.5.cloned.1.call-update) | async-done | bytes 7340048 | tf_op jit(solution)/shard_map/all_gather | solution.py:132
  110.2 2.3 slice.61
  112.5 4.6 %slice.70 = bf16[16,256,512]{2,1,0:T(8,128)(2,1)} slice(bf16[16,256,896]{2,1,0:T(8,128)(2,1)} %bitcast.67), slice={[0:16], [0:256], [384:896]} | slice | bytes 8388608 | tf_op jit(solution)/shard_map/slice | solution.py:138
  119.0 2.7 %fusion.158 = (f32[192]{0:T(256)S(1)}, f32[192,6144]{1,0:T(8,128)S(1)}) fusion(bf16[6144,128]{1,0:T(8,128)(2,1)S(1)} %copy-done, bf16[192,96]{0,1:T(8,128)(2,1)S(1)} %get-tuple-element.15, bf16[192,16]{0,1:T(8,128)(2,1)S(1)} %get-tuple-element.14, bf16[192,16]{0,1:T(8,128)(2,1)S(1)} %get-tuple-element.11, pred[6144]{0:T(1024)(128)(4,1)S(1)} %broadcast_compare_fusion, ...), kind=kOutput, calls=%fused_computation.229 | convolution fusion | flops 313933632 | bytes 6398208 | tf_op jit(solution)/shard_map/dot_general | solution.py:155
  121.7 2.0 copy-done.2
  124.8 60.0 %all-gather.7.cloned.1.call-done = bf16[10240,256]{1,0:T(8,128)(2,1)} async-done(((bf16[640,256]{1,0:T(8,128)(2,1)}), bf16[10240,256]{1,0:T(8,128)(2,1)}) %all-gather.7.cloned.1.call-update) | async-done | bytes 5242896 | tf_op jit(solution)/shard_map/all_gather | solution.py:133
  184.8 5.7 %fusion.37 = f32[192,16,256]{2,0,1:T(8,128)} fusion(f32[192,128]{1,0:T(8,128)S(1)} %fusion.87, bf16[6144,128]{1,0:T(8,128)(2,1)S(1)} %copy-done.4, f32[192,6144]{1,0:T(8,128)} %copy-done.2, f32[192]{0:T(256)S(1)} %max.37, bf16[16,640,256]{2,1,0:T(8,128)(2,1)} %bitcast.75, f32[192]{0:T(256)S(1)} %add.267), kind=kOutput, calls=%fused_computation.41 | convolution fusion | flops 505749504 | bytes 10585600 | tf_op jit(solution)/shard_map/dot_general | solution.py:172
  190.5 8.8 %fusion.19 = f32[192,16,256]{2,0,1:T(8,128)} fusion(f32[192,16,256]{2,0,1:T(8,128)} %fusion.37, bf16[16,640,256]{2,1,0:T(8,128)(2,1)} %bitcast.76, bf16[192,4096]{1,0:T(8,128)(2,1)S(1)} %convert_element_type.81, bf16[4096,512]{1,0:T(8,128)(2,1)} %bitcast.68, f32[512]{0:T(512)S(1)} %copy-done.13), kind=kOutput, calls=%fused_computation.28 | convolution fusion | flops 1617887232 | bytes 16254976 | tf_op jit(solution)/shard_map/dot_general | solution.py:174
  199.3 5.4 %copy.53 = f32[192,16,256]{2,1,0:T(8,128)} copy(f32[192,16,256]{2,0,1:T(8,128)} %fusion.19) | data formatting | bytes 6291456 | tf_op jit(solution)/shard_map/add | solution.py:172
  204.7 4.9 %reshape_reshape.3 = f32[16,2,6,4096]{3,2,1,0:T(8,128)} reshape(f32[192,16,256]{2,1,0:T(8,128)} %copy.53) | data formatting | bytes 6291456 | tf_op jit(solution)/shard_map/reshape;reshape | solution.py:177
  209.6 1.7 fusion.39
  211.8 8.9 %collective-permute-start.7 = (bf16[16,6,4096]{2,0,1:T(8,128)(2,1)S(1)}, bf16[16,6,4096]{2,0,1:T(8,128)(2,1)S(1)}, u32[]{:S(2)}, u32[]{:S(2)}) collective-permute-start(bf16[16,6,4096]{2,0,1:T(8,128)(2,1)S(1)} %copy.55), channel_id=1, source_target_pairs={{0,1},{1,0},{2,3},{3,2},{4,5},{5,4},{6,7},{7,6},{8,9},{9,8},{10,11... | collective-permute-start | bytes 2359304 | tf_op jit(solution)/shard_map/ppermute | solution.py:181
  220.7 1.7 constant_dynamic-slice_fusion
  224.0 22.8 %all_to_all.5 = bf16[16,6,4096]{2,1,0:T(8,128)(2,1)S(1)} all-to-all(bf16[16,6,4096]{2,1,0:T(8,128)(2,1)S(1)} %copy.56), channel_id=1, replica_groups={{0,2,4,6,8,10,12,14,16,18,20,22,24,26,28,30},{1,3,5,7,9,11,13,15,17,19,..., dimensions={0} | all-to-all | bytes 1572864 | tf_op jit(solution)/shard_map/all_to_all | solution.py:186
  (82 shorter events, 16.9 us)
Async XLA Ops:
  6.5 112.4 %copy-start = (bf16[6144,128]{1,0:T(8,128)(2,1)S(1)}, bf16[6144,128]{1,0:T(8,128)(2,1)}, u32[]{:S(2)}) copy-start(bf16[6144,128]{1,0:T(8,128)(2,1)} %param.29) | copy-start | bytes 4718596
  6.5 103.6 %all-gather.5.cloned.1.call-start = ((), (), s32[]{:S(2)}) async-start(), calls=%async_computation.1 | async-start | bytes 7798784 | tf_op jit(solution)/shard_map/all_gather | solution.py:132
  8.5 176.3 %all-gather.7.cloned.1.call-start = ((), (), s32[]{:S(2)}) async-start(), calls=%async_computation.2 | async-start | bytes 5570560 | tf_op jit(solution)/shard_map/all_gather | solution.py:133
  8.6 16.2 %collective-permute-start = (bf16[6,4096]{1,0:T(8,128)(2,1)}, bf16[6,4096]{1,0:T(8,128)(2,1)S(1)}, u32[]{:S(2)}, u32[]{:S(2)}) collective-permute-start(bf16[6,4096]{1,0:T(8,128)(2,1)} %param.16), channel_id=1, source_target_pairs={{0,8},{1,9},{2,10},{3,11},{4,12},{5,13},{6,14},{7,15},{8,16},{9,17... | collective-permute-start | bytes 147464 | tf_op jit(solution)/shard_map/ppermute | solution.py:77
  12.6 12.2 %collective-permute-start.1 = (bf16[6,4096]{1,0:T(8,128)(2,1)}, bf16[6,4096]{1,0:T(8,128)(2,1)S(1)}, u32[]{:S(2)}, u32[]{:S(2)}) collective-permute-start(bf16[6,4096]{1,0:T(8,128)(2,1)} %param.16), channel_id=1, source_target_pairs={{0,16},{1,17},{2,18},{3,19},{4,20},{5,21},{6,22},{7,23},{8,24},{9,... | collective-permute-start | bytes 147464 | tf_op jit(solution)/shard_map/ppermute | solution.py:77
  17.2 7.7 %collective-permute-start.2 = (bf16[6,4096]{1,0:T(8,128)(2,1)}, bf16[6,4096]{1,0:T(8,128)(2,1)S(1)}, u32[]{:S(2)}, u32[]{:S(2)}) collective-permute-start(bf16[6,4096]{1,0:T(8,128)(2,1)} %param.16), channel_id=1, source_target_pairs={{0,24},{1,25},{2,26},{3,27},{4,28},{5,29},{6,30},{7,31},{8,0},{9,1... | collective-permute-start | bytes 147464 | tf_op jit(solution)/shard_map/ppermute | solution.py:77
  26.4 10.1 %collective-permute-start.5 = (bf16[4,6,4096]{2,1,0:T(8,128)(2,1)S(1)}, bf16[4,6,4096]{2,1,0:T(8,128)(2,1)S(1)}, u32[]{:S(2)}, u32[]{:S(2)}) collective-permute-start(bf16[4,6,4096]{2,1,0:T(8,128)(2,1)S(1)} %broadcast_select_fusion.2), channel_id=1, source_target_pairs={{0,6},{1,7},{2,0},{3,1},{4,2},{5,3},{6,4},{7,5},{8,14},{9,15},{10,... | collective-permute-start | bytes 589832 | tf_op jit(solution)/shard_map/ppermute | solution.py:77
  30.8 10.0 %collective-permute-start.3 = (bf16[4,6,4096]{2,1,0:T(8,128)(2,1)S(1)}, bf16[4,6,4096]{2,1,0:T(8,128)(2,1)S(1)}, u32[]{:S(2)}, u32[]{:S(2)}) collective-permute-start(bf16[4,6,4096]{2,1,0:T(8,128)(2,1)S(1)} %broadcast_select_fusion.2), channel_id=1, source_target_pairs={{0,2},{1,3},{2,4},{3,5},{4,6},{5,7},{6,0},{7,1},{8,10},{9,11},{10,... | collective-permute-start | bytes 589832 | tf_op jit(solution)/shard_map/ppermute | solution.py:77
  32.8 11.9 %collective-permute-start.4 = (bf16[4,6,4096]{2,1,0:T(8,128)(2,1)S(1)}, bf16[4,6,4096]{2,1,0:T(8,128)(2,1)S(1)}, u32[]{:S(2)}, u32[]{:S(2)}) collective-permute-start(bf16[4,6,4096]{2,1,0:T(8,128)(2,1)S(1)} %broadcast_select_fusion.2), channel_id=1, source_target_pairs={{0,4},{1,5},{2,6},{3,7},{4,0},{5,1},{6,2},{7,3},{8,12},{9,13},{10,... | collective-permute-start | bytes 589832 | tf_op jit(solution)/shard_map/ppermute | solution.py:77
  47.2 7.4 %collective-permute-start.6 = (bf16[4,4,6,4096]{3,1,2,0:T(4,128)(2,1)S(1)}, bf16[4,4,6,4096]{3,1,2,0:T(4,128)(2,1)S(1)}, u32[]{:S(2)}, u32[]{:S(2)}) collective-permute-start(bf16[4,4,6,4096]{3,1,2,0:T(4,128)(2,1)S(1)} %broadcast_select_fusion.1), channel_id=1, source_target_pairs={{0,1},{1,0},{2,3},{3,2},{4,5},{5,4},{6,7},{7,6},{8,9},{9,8},{10,11... | collective-permute-start | bytes 2359304 | tf_op jit(solution)/shard_map/ppermute | solution.py:77
  58.7 4.4 %copy-start.6 = (f32[4096]{0:T(1024)S(1)}, f32[4096]{0:T(1024)}, u32[]{:S(2)}) copy-start(f32[4096]{0:T(1024)} %param.20) | copy-start | bytes 49156
  58.7 4.4 %copy-start.7 = (f32[4096]{0:T(1024)S(1)}, f32[4096]{0:T(1024)}, u32[]{:S(2)}) copy-start(f32[4096]{0:T(1024)} %param.19) | copy-start | bytes 49156
  58.7 4.4 %copy-start.8 = (f32[4096]{0:T(1024)S(1)}, f32[4096]{0:T(1024)}, u32[]{:S(2)}) copy-start(f32[4096]{0:T(1024)} %param.18) | copy-start | bytes 49156
  58.7 4.4 %copy-start.9 = (f32[4096]{0:T(1024)S(1)}, f32[4096]{0:T(1024)}, u32[]{:S(2)}) copy-start(f32[4096]{0:T(1024)} %param.17) | copy-start | bytes 49156
  112.4 4.6 %copy-start.3 = (bf16[192,4096]{1,0:T(8,128)(2,1)S(1)}, bf16[192,4096]{1,0:T(8,128)(2,1)}, u32[]{:S(2)}) copy-start(bf16[192,4096]{1,0:T(8,128)(2,1)} %convert_element_type.75) | copy-start | bytes 4718596
  112.5 4.6 %copy-start.12 = (f32[384]{0:T(512)S(1)}, f32[384]{0:T(512)}, u32[]{:S(2)}) copy-start(f32[384]{0:T(512)} %param.22) | copy-start | bytes 4612
  121.6 2.1 copy-start.2
  121.6 63.2 %copy-start.4 = (bf16[6144,128]{1,0:T(8,128)(2,1)S(1)}, bf16[6144,128]{1,0:T(8,128)(2,1)}, u32[]{:S(2)}) copy-start(bf16[6144,128]{1,0:T(8,128)(2,1)} %param.30) | copy-start | bytes 4718596
  184.8 5.7 %copy-start.13 = (f32[512]{0:T(512)S(1)}, f32[512]{0:T(512)}, u32[]{:S(2)}) copy-start(f32[512]{0:T(512)} %param.26) | copy-start | bytes 6148
  211.8 10.8 %collective-permute-start.7 = (bf16[16,6,4096]{2,0,1:T(8,128)(2,1)S(1)}, bf16[16,6,4096]{2,0,1:T(8,128)(2,1)S(1)}, u32[]{:S(2)}, u32[]{:S(2)}) collective-permute-start(bf16[16,6,4096]{2,0,1:T(8,128)(2,1)S(1)} %copy.55), channel_id=1, source_target_pairs={{0,1},{1,0},{2,3},{3,2},{4,5},{5,4},{6,7},{7,6},{8,9},{9,8},{10,11... | collective-permute-start | bytes 2359304 | tf_op jit(solution)/shard_map/ppermute | solution.py:181
  222.6 25.1 %copy-start.1 = (bf16[6144,128]{1,0:T(8,128)(2,1)S(1)}, bf16[6144,128]{1,0:T(8,128)(2,1)}, u32[]{:S(2)}) copy-start(bf16[6144,128]{1,0:T(8,128)(2,1)} %param.29) | copy-start | bytes 4718596
  223.5 23.5 %copy-start.5 = (bf16[6,4096]{1,0:T(8,128)(2,1)S(1)}, bf16[6,4096]{1,0:T(8,128)(2,1)}, u32[]{:S(2)}) copy-start(bf16[6,4096]{1,0:T(8,128)(2,1)} %param.16) | copy-start | bytes 147460
  223.5 23.5 %copy-start.10 = (f32[4096]{0:T(1024)S(1)}, f32[4096]{0:T(1024)}, u32[]{:S(2)}) copy-start(f32[4096]{0:T(1024)} %param.28) | copy-start | bytes 49156
  223.6 23.5 %copy-start.11 = (f32[4096]{0:T(1024)S(1)}, f32[4096]{0:T(1024)}, u32[]{:S(2)}) copy-start(f32[4096]{0:T(1024)} %param.24) | copy-start | bytes 49156
Sparse Core Ops, SparseCore 0:
  9.4 100.7 all-gather.4
  112.3 72.5 all-gather.6

commit v5 on v1

--- a/solution.py
+++ b/solution.py
@@ -131,13 +131,13 @@
     width_dense = w_dense.shape[0]
     first = lax.all_gather(jnp.concatenate([w_qkv, w_up], axis=1), "tok", axis=0, tiled=False)
     second = lax.all_gather(
-        jnp.concatenate([w_dense, w_down], axis=0), "tok", axis=0, tiled=False
+        jnp.concatenate([w_dense, w_down], axis=0), "tok", axis=1, tiled=True
     )
     parts = first.shape[0] * first.shape[1]
     qkv_full = first[:, :, :width_qkv].reshape(parts, width_qkv)
     up_full = first[:, :, width_qkv:].reshape(parts, width_up)
-    dense_parts = second[:, :width_dense, :]
-    down_parts = second[:, width_dense:, :]
+    dense_full = second[:width_dense]
+    down_full = second[width_dense:]
     whole = head_gather(tokens)
     normed_one = layer_norm(whole, ln1_gain, ln1_bias).astype(jnp.bfloat16)
     normed_two = layer_norm(whole, ln2_gain, ln2_bias).astype(jnp.bfloat16)
@@ -168,11 +168,9 @@
         cache_weights.astype(jnp.bfloat16), v_cache, preferred_element_type=jnp.float32
     ) + jnp.dot(new_weights.astype(jnp.bfloat16), new_values, preferred_element_type=jnp.float32)
     attention = (summed / total[:, None]).astype(jnp.bfloat16)
-    contract = (((1,), (1,)), ((), ()))
-    partial = lax.dot_general(
-        attention, dense_parts, contract, preferred_element_type=jnp.float32
-    ) + lax.dot_general(hidden, down_parts, contract, preferred_element_type=jnp.float32)
-    partial = partial.reshape(rows_total, -1)
+    partial = jnp.dot(attention, dense_full, preferred_element_type=jnp.float32) + jnp.dot(
+        hidden, down_full, preferred_element_type=jnp.float32
+    )
     heads = lax.axis_size("head")
     blocks = partial.astype(jnp.bfloat16).reshape(heads, tokens.shape[0], -1)
     exchanged = lax.all_to_all(blocks, "head", 0, 0, tiled=True)

time: 255 us -> 276 us (1.082)
  waiting for transfers between devices: 104 us -> 123 us
    all_gather x1, waiting for transfers between devices: 60.1 us -> 79 us  [body(): lax.all_gather(jnp.concatenate([w_dense, w_down], axis=0), 'tok', axis=1,...]
    convert_element_type x2 -> x0, local copies, waits for them, and re-layouts: 5 us -> none  [body(): blocks = partial.astype(jnp.bfloat16).reshape(heads, tokens.shape[0], -1)]
    reshape x0 -> x1, local copies, waits for them, and re-layouts: none -> 3.5 us  [body(): blocks = partial.astype(jnp.bfloat16).reshape(heads, tokens.shape[0], -1)]
  transfers between devices with their start and end apart: 9 -> 9, of which waited for: 5 -> 5; matrix products, arithmetic and copies ran while one was open for 17% -> 16% of each run, Pallas kernels for 0% -> 0%
where the time goes in v5:
time: 276 us; the launch traced here: 274 us
  waiting for transfers between devices  123 us (45%)
  blocking collectives  44.4 us (16%)
  local copies, waits for them, and re-layouts  28.8 us (10%)
  starting transfers between devices  27.2 us (10%)
  matrix products  18.9 us (7%)
  other arithmetic  18.3 us (7%)
  between operations  13.9 us (5%)
    all_gather x1, waiting for transfers between devices, body(): lax.all_gather(jnp.concatenate([w_dense, w_down], axis=0), 'tok', axis=1,...  79 us
    all_to_all x1, blocking collectives, body(): exchanged = lax.all_to_all(blocks, 'head', 0, 0, tiled=True)  44.4 us
    all_gather x1, waiting for transfers between devices, body(): lax.all_gather(jnp.concatenate([w_qkv, w_up], axis=1), 'tok', axis=0, til...  34 us
    ppermute x7, starting transfers between devices, gather_stage(): lax.ppermute(stacked, 'head', stage_pairs(size, stride, shift, total))  27.2 us
    ppermute x7, waiting for transfers between devices, gather_stage(): lax.ppermute(stacked, 'head', stage_pairs(size, stride, shift, total))  9.45 us
    dot_general x1, matrix products, body(): jnp.dot(hidden, down_full, preferred_element_type=jnp.float32)  8.27 us
    dot_general x1, matrix products, body(): jnp.dot(attention, dense_full, preferred_element_type=jnp.float32)  6.1 us
    convert_element_type x2, local copies, waits for them, and re-layouts, body(): normed_one = layer_norm(whole, ln1_gain, ln1_bias).astype(jnp.bfloat16)  5.89 us
  transfers between devices with their start and end apart: 9, of which 5 were waited for; matrix products, arithmetic and copies ran while one was open for 16% of the time, Pallas kernels for 0%

profile of v5, /device:TPU:1, one launch (start us, length us, event | category | flops | bytes accessed | tf_op | source)
XLA Modules:
  0.0 274.0 jit_solution(13199522684299900937)
XLA Ops:
  6.5 2.0 pad_maximum_fusion.2
  8.6 4.0 %collective-permute-start = (bf16[6,4096]{1,0:T(8,128)(2,1)}, bf16[6,4096]{1,0:T(8,128)(2,1)S(1)}, u32[]{:S(2)}, u32[]{:S(2)}) collective-permute-start(bf16[6,4096]{1,0:T(8,128)(2,1)} %param.16), channel_id=1, source_target_pairs={{0,8},{1,9},{2,10},{3,11},{4,12},{5,13},{6,14},{7,15},{8,16},{9,17... | collective-permute-start | bytes 147464 | tf_op jit(solution)/shard_map/ppermute | solution.py:77
  12.6 4.5 %collective-permute-start.1 = (bf16[6,4096]{1,0:T(8,128)(2,1)}, bf16[6,4096]{1,0:T(8,128)(2,1)S(1)}, u32[]{:S(2)}, u32[]{:S(2)}) collective-permute-start(bf16[6,4096]{1,0:T(8,128)(2,1)} %param.16), channel_id=1, source_target_pairs={{0,16},{1,17},{2,18},{3,19},{4,20},{5,21},{6,22},{7,23},{8,24},{9,... | collective-permute-start | bytes 147464 | tf_op jit(solution)/shard_map/ppermute | solution.py:77
  17.2 3.0 %collective-permute-start.2 = (bf16[6,4096]{1,0:T(8,128)(2,1)}, bf16[6,4096]{1,0:T(8,128)(2,1)S(1)}, u32[]{:S(2)}, u32[]{:S(2)}) collective-permute-start(bf16[6,4096]{1,0:T(8,128)(2,1)} %param.16), channel_id=1, source_target_pairs={{0,24},{1,25},{2,26},{3,27},{4,28},{5,29},{6,30},{7,31},{8,0},{9,1... | collective-permute-start | bytes 147464 | tf_op jit(solution)/shard_map/ppermute | solution.py:77
  20.2 1.7 pad_maximum_fusion.3
  26.4 4.4 %collective-permute-start.5 = (bf16[4,6,4096]{2,1,0:T(8,128)(2,1)S(1)}, bf16[4,6,4096]{2,1,0:T(8,128)(2,1)S(1)}, u32[]{:S(2)}, u32[]{:S(2)}) collective-permute-start(bf16[4,6,4096]{2,1,0:T(8,128)(2,1)S(1)} %broadcast_select_fusion.2), channel_id=1, source_target_pairs={{0,6},{1,7},{2,0},{3,1},{4,2},{5,3},{6,4},{7,5},{8,14},{9,15},{10,... | collective-permute-start | bytes 589832 | tf_op jit(solution)/shard_map/ppermute | solution.py:77
  30.8 1.9 collective-permute-start.3
  32.8 3.6 %collective-permute-start.4 = (bf16[4,6,4096]{2,1,0:T(8,128)(2,1)S(1)}, bf16[4,6,4096]{2,1,0:T(8,128)(2,1)S(1)}, u32[]{:S(2)}, u32[]{:S(2)}) collective-permute-start(bf16[4,6,4096]{2,1,0:T(8,128)(2,1)S(1)} %broadcast_select_fusion.2), channel_id=1, source_target_pairs={{0,4},{1,5},{2,6},{3,7},{4,0},{5,1},{6,2},{7,3},{8,12},{9,13},{10,... | collective-permute-start | bytes 589832 | tf_op jit(solution)/shard_map/ppermute | solution.py:77
  36.5 4.4 %collective-permute-done.3 = bf16[4,6,4096]{2,1,0:T(8,128)(2,1)S(1)} collective-permute-done((bf16[4,6,4096]{2,1,0:T(8,128)(2,1)S(1)}, bf16[4,6,4096]{2,1,0:T(8,128)(2,1)S(1)}, u32[]{:S(2)}, u32[]{:S(2)}) %collective-permute-start.3) | collective-permute-done | bytes 196640 | tf_op jit(solution)/shard_map/ppermute | solution.py:77
  40.9 3.8 %collective-permute-done.4 = bf16[4,6,4096]{2,1,0:T(8,128)(2,1)S(1)} collective-permute-done((bf16[4,6,4096]{2,1,0:T(8,128)(2,1)S(1)}, bf16[4,6,4096]{2,1,0:T(8,128)(2,1)S(1)}, u32[]{:S(2)}, u32[]{:S(2)}) %collective-permute-start.4) | collective-permute-done | bytes 196640 | tf_op jit(solution)/shard_map/ppermute | solution.py:77
  45.6 1.2 gather_fusion.1
  47.2 5.7 %collective-permute-start.6 = (bf16[4,4,6,4096]{3,1,2,0:T(4,128)(2,1)S(1)}, bf16[4,4,6,4096]{3,1,2,0:T(4,128)(2,1)S(1)}, u32[]{:S(2)}, u32[]{:S(2)}) collective-permute-start(bf16[4,4,6,4096]{3,1,2,0:T(4,128)(2,1)S(1)} %broadcast_select_fusion.1), channel_id=1, source_target_pairs={{0,1},{1,0},{2,3},{3,2},{4,5},{5,4},{6,7},{7,6},{8,9},{9,8},{10,11... | collective-permute-start | bytes 2359304 | tf_op jit(solution)/shard_map/ppermute | solution.py:77
  53.3 1.3 collective-permute-done.6
  55.7 3.0 %gather_fusion.2 = bf16[2,4,4,6,4096]{4,2,3,1,0:T(4,128)(2,1)} fusion(bf16[2,4,4,6,4096]{4,2,3,1,0:T(4,128)(2,1)S(1)} %pad_maximum_fusion, s32[1024]{0:T(1024)S(1)} %pad_clamp_fusion), kind=kCustom, calls=%fused_computation.2 | custom fusion | bytes 3145736 | tf_op jit(solution)/shard_map/jit(_take)/gather | solution.py:80
  58.8 3.2 %bitcast_reduce_fusion = (f32[4,4,2,6]{0,3,1,2:T(8,128)S(1)}, bf16[2,4,4,6,4096]{4,2,3,1,0:T(4,128)(2,1)S(1)}) fusion(bf16[2,4,4,6,4096]{4,2,3,1,0:T(4,128)(2,1)} %gather_fusion.2, pred[2]{0:T(512)(128)(4,1)S(1)} %compare_and_fusion.2), kind=kLoop, calls=%fused_computation.16 | loop fusion | flops 2359104 | bytes 3146498 | tf_op jit(solution)/shard_map/reduce_sum | solution.py:17
  62.0 1.2 fusion.15
  63.2 2.1 fusion.14
  65.2 2.2 copy.30
  67.5 3.7 %convert_element_type.66 = bf16[192,4096]{1,0:T(8,128)(2,1)} reshape(bf16[4,4,2,6,4096]{4,3,2,1,0:T(8,128)(2,1)} %copy.30) | data formatting | bytes 3145728 | tf_op jit(solution)/shard_map/convert_element_type | solution.py:142
  71.1 2.2 copy.32
  73.4 2.8 %convert_element_type.72 = bf16[192,4096]{1,0:T(8,128)(2,1)S(1)} reshape(bf16[4,4,2,6,4096]{4,3,2,1,0:T(8,128)(2,1)} %copy.32) | data formatting | bytes 3145728 | tf_op jit(solution)/shard_map/convert_element_type | solution.py:143
  76.1 34.0 %all-gather.6.cloned.1.call-done = bf16[4096,896]{1,0:T(8,128)(2,1)} async-done(((bf16[256,896]{1,0:T(8,128)(2,1)}), bf16[4096,896]{1,0:T(8,128)(2,1)}) %all-gather.6.cloned.1.call-update) | async-done | bytes 7340048 | tf_op jit(solution)/shard_map/all_gather | solution.py:132
  110.2 2.3 slice.61
  112.5 4.6 %slice.70 = bf16[16,256,512]{2,1,0:T(8,128)(2,1)} slice(bf16[16,256,896]{2,1,0:T(8,128)(2,1)} %bitcast.52), slice={[0:16], [0:256], [384:896]} | slice | bytes 8388608 | tf_op jit(solution)/shard_map/slice | solution.py:138
  117.1 1.4 fusion.148
  119.0 2.7 fusion.149
  121.7 2.0 copy-done.1
  124.8 79.0 %all-gather.4.cloned.1.call-done = bf16[640,4096]{1,0:T(8,128)(2,1)} async-done(((bf16[640,256]{1,0:T(8,128)(2,1)}), bf16[640,4096]{1,0:T(8,128)(2,1)}) %all-gather.4.cloned.1.call-update) | async-done | bytes 5242896 | tf_op jit(solution)/shard_map/all_gather | solution.py:133
  203.8 6.1 %fusion.30 = f32[192,4096]{1,0:T(8,128)} fusion(f32[192,128]{1,0:T(8,128)S(1)} %fusion.78, bf16[6144,128]{1,0:T(8,128)(2,1)} %param.30, f32[192,6144]{1,0:T(8,128)} %copy-done.1, f32[192]{0:T(256)S(1)} %max.37, bf16[640,4096]{1,0:T(8,128)(2,1)} %all-gather.4.cloned.1.call-done, f32[192]{0:T(256)S(1)} %add.255), kind=kOutput, calls=%fused_computation.37 | convolution fusion | flops 505749504 | bytes 10585600 | tf_op jit(solution)/shard_map/dot_general | solution.py:171
  209.8 8.3 %fusion.1 = bf16[192,4096]{1,0:T(8,128)(2,1)} fusion(f32[192,4096]{1,0:T(8,128)} %fusion.30, bf16[640,4096]{1,0:T(8,128)(2,1)} %all-gather.4.cloned.1.call-done, bf16[192,4096]{1,0:T(8,128)(2,1)S(1)} %convert_element_type.72, bf16[4096,512]{1,0:T(8,128)(2,1)} %bitcast.53, f32[512]{0:T(512)S(1)} %copy-done.11), kind=kOutput, calls=%fused_computation.6 | convolution fusion | flops 1618673664 | bytes 14682112 | tf_op jit(solution)/shard_map/dot_general | solution.py:171
  218.1 3.5 %reshape.341 = bf16[32,6,4096]{2,1,0:T(8,128)(2,1)} reshape(bf16[192,4096]{1,0:T(8,128)(2,1)} %fusion.1) | data formatting | bytes 3145728 | tf_op jit(solution)/shard_map/reshape | solution.py:175
  221.6 44.4 %all_to_all.5 = bf16[32,6,4096]{2,1,0:T(8,128)(2,1)S(1)} all-to-all(bf16[32,6,4096]{2,1,0:T(8,128)(2,1)} %reshape.341), channel_id=1, replica_groups=mesh['tok'=16,'head'=32] {'head'}, dimensions={0} | all-to-all | bytes 3145728 | tf_op jit(solution)/shard_map/all_to_all | solution.py:176
  (71 shorter events, 10.0 us)
Async XLA Ops:
  6.5 112.4 %copy-start = (bf16[6144,128]{1,0:T(8,128)(2,1)S(1)}, bf16[6144,128]{1,0:T(8,128)(2,1)}, u32[]{:S(2)}) copy-start(bf16[6144,128]{1,0:T(8,128)(2,1)} %param.29) | copy-start | bytes 4718596
  6.5 103.6 %all-gather.6.cloned.1.call-start = ((), (), s32[]{:S(2)}) async-start(), calls=%async_computation.2 | async-start | bytes 7798784 | tf_op jit(solution)/shard_map/all_gather | solution.py:132
  8.5 195.2 %all-gather.4.cloned.1.call-start = ((), (), s32[]{:S(2)}) async-start(), calls=%async_computation.1 | async-start | bytes 5570560 | tf_op jit(solution)/shard_map/all_gather | solution.py:133
  8.6 16.2 %collective-permute-start = (bf16[6,4096]{1,0:T(8,128)(2,1)}, bf16[6,4096]{1,0:T(8,128)(2,1)S(1)}, u32[]{:S(2)}, u32[]{:S(2)}) collective-permute-start(bf16[6,4096]{1,0:T(8,128)(2,1)} %param.16), channel_id=1, source_target_pairs={{0,8},{1,9},{2,10},{3,11},{4,12},{5,13},{6,14},{7,15},{8,16},{9,17... | collective-permute-start | bytes 147464 | tf_op jit(solution)/shard_map/ppermute | solution.py:77
  12.6 12.2 %collective-permute-start.1 = (bf16[6,4096]{1,0:T(8,128)(2,1)}, bf16[6,4096]{1,0:T(8,128)(2,1)S(1)}, u32[]{:S(2)}, u32[]{:S(2)}) collective-permute-start(bf16[6,4096]{1,0:T(8,128)(2,1)} %param.16), channel_id=1, source_target_pairs={{0,16},{1,17},{2,18},{3,19},{4,20},{5,21},{6,22},{7,23},{8,24},{9,... | collective-permute-start | bytes 147464 | tf_op jit(solution)/shard_map/ppermute | solution.py:77
  17.2 7.7 %collective-permute-start.2 = (bf16[6,4096]{1,0:T(8,128)(2,1)}, bf16[6,4096]{1,0:T(8,128)(2,1)S(1)}, u32[]{:S(2)}, u32[]{:S(2)}) collective-permute-start(bf16[6,4096]{1,0:T(8,128)(2,1)} %param.16), channel_id=1, source_target_pairs={{0,24},{1,25},{2,26},{3,27},{4,28},{5,29},{6,30},{7,31},{8,0},{9,1... | collective-permute-start | bytes 147464 | tf_op jit(solution)/shard_map/ppermute | solution.py:77
  26.4 10.1 %collective-permute-start.5 = (bf16[4,6,4096]{2,1,0:T(8,128)(2,1)S(1)}, bf16[4,6,4096]{2,1,0:T(8,128)(2,1)S(1)}, u32[]{:S(2)}, u32[]{:S(2)}) collective-permute-start(bf16[4,6,4096]{2,1,0:T(8,128)(2,1)S(1)} %broadcast_select_fusion.2), channel_id=1, source_target_pairs={{0,6},{1,7},{2,0},{3,1},{4,2},{5,3},{6,4},{7,5},{8,14},{9,15},{10,... | collective-permute-start | bytes 589832 | tf_op jit(solution)/shard_map/ppermute | solution.py:77
  30.8 10.0 %collective-permute-start.3 = (bf16[4,6,4096]{2,1,0:T(8,128)(2,1)S(1)}, bf16[4,6,4096]{2,1,0:T(8,128)(2,1)S(1)}, u32[]{:S(2)}, u32[]{:S(2)}) collective-permute-start(bf16[4,6,4096]{2,1,0:T(8,128)(2,1)S(1)} %broadcast_select_fusion.2), channel_id=1, source_target_pairs={{0,2},{1,3},{2,4},{3,5},{4,6},{5,7},{6,0},{7,1},{8,10},{9,11},{10,... | collective-permute-start | bytes 589832 | tf_op jit(solution)/shard_map/ppermute | solution.py:77
  32.8 11.9 %collective-permute-start.4 = (bf16[4,6,4096]{2,1,0:T(8,128)(2,1)S(1)}, bf16[4,6,4096]{2,1,0:T(8,128)(2,1)S(1)}, u32[]{:S(2)}, u32[]{:S(2)}) collective-permute-start(bf16[4,6,4096]{2,1,0:T(8,128)(2,1)S(1)} %broadcast_select_fusion.2), channel_id=1, source_target_pairs={{0,4},{1,5},{2,6},{3,7},{4,0},{5,1},{6,2},{7,3},{8,12},{9,13},{10,... | collective-permute-start | bytes 589832 | tf_op jit(solution)/shard_map/ppermute | solution.py:77
  47.2 7.4 %collective-permute-start.6 = (bf16[4,4,6,4096]{3,1,2,0:T(4,128)(2,1)S(1)}, bf16[4,4,6,4096]{3,1,2,0:T(4,128)(2,1)S(1)}, u32[]{:S(2)}, u32[]{:S(2)}) collective-permute-start(bf16[4,4,6,4096]{3,1,2,0:T(4,128)(2,1)S(1)} %broadcast_select_fusion.1), channel_id=1, source_target_pairs={{0,1},{1,0},{2,3},{3,2},{4,5},{5,4},{6,7},{7,6},{8,9},{9,8},{10,11... | collective-permute-start | bytes 2359304 | tf_op jit(solution)/shard_map/ppermute | solution.py:77
  58.8 4.4 %copy-start.4 = (f32[4096]{0:T(1024)S(1)}, f32[4096]{0:T(1024)}, u32[]{:S(2)}) copy-start(f32[4096]{0:T(1024)} %param.20) | copy-start | bytes 49156
  58.8 4.4 %copy-start.5 = (f32[4096]{0:T(1024)S(1)}, f32[4096]{0:T(1024)}, u32[]{:S(2)}) copy-start(f32[4096]{0:T(1024)} %param.19) | copy-start | bytes 49156
  58.8 4.4 %copy-start.6 = (f32[4096]{0:T(1024)S(1)}, f32[4096]{0:T(1024)}, u32[]{:S(2)}) copy-start(f32[4096]{0:T(1024)} %param.18) | copy-start | bytes 49156
  58.8 4.4 %copy-start.7 = (f32[4096]{0:T(1024)S(1)}, f32[4096]{0:T(1024)}, u32[]{:S(2)}) copy-start(f32[4096]{0:T(1024)} %param.17) | copy-start | bytes 49156
  112.4 4.6 %copy-start.2 = (bf16[192,4096]{1,0:T(8,128)(2,1)S(1)}, bf16[192,4096]{1,0:T(8,128)(2,1)}, u32[]{:S(2)}) copy-start(bf16[192,4096]{1,0:T(8,128)(2,1)} %convert_element_type.66) | copy-start | bytes 4718596
  112.5 4.6 %copy-start.10 = (f32[384]{0:T(512)S(1)}, f32[384]{0:T(512)}, u32[]{:S(2)}) copy-start(f32[384]{0:T(512)} %param.22) | copy-start | bytes 4612
  121.6 2.1 copy-start.1
  124.8 85.1 %copy-start.11 = (f32[512]{0:T(512)S(1)}, f32[512]{0:T(512)}, u32[]{:S(2)}) copy-start(f32[512]{0:T(512)} %param.26) | copy-start | bytes 6148
  221.6 44.9 %copy-start.3 = (bf16[6,4096]{1,0:T(8,128)(2,1)S(1)}, bf16[6,4096]{1,0:T(8,128)(2,1)}, u32[]{:S(2)}) copy-start(bf16[6,4096]{1,0:T(8,128)(2,1)} %param.16) | copy-start | bytes 147460
  221.6 44.9 %copy-start.8 = (f32[4096]{0:T(1024)S(1)}, f32[4096]{0:T(1024)}, u32[]{:S(2)}) copy-start(f32[4096]{0:T(1024)} %param.28) | copy-start | bytes 49156
  221.6 44.9 %copy-start.9 = (f32[4096]{0:T(1024)S(1)}, f32[4096]{0:T(1024)}, u32[]{:S(2)}) copy-start(f32[4096]{0:T(1024)} %param.24) | copy-start | bytes 49156
Sparse Core Ops, SparseCore 0:
  9.4 100.7 all-gather.5
  112.2 91.5 all-gather.3

commit v6 on v1

--- a/solution.py
+++ b/solution.py
@@ -128,7 +128,6 @@
     scale = HD ** (-0.5)
     width_qkv = w_qkv.shape[1]
     width_up = w_up.shape[1]
-    width_dense = w_dense.shape[0]
     first = lax.all_gather(jnp.concatenate([w_qkv, w_up], axis=1), "tok", axis=0, tiled=False)
     second = lax.all_gather(
         jnp.concatenate([w_dense, w_down], axis=0), "tok", axis=0, tiled=False
@@ -136,8 +135,6 @@
     parts = first.shape[0] * first.shape[1]
     qkv_full = first[:, :, :width_qkv].reshape(parts, width_qkv)
     up_full = first[:, :, width_qkv:].reshape(parts, width_up)
-    dense_parts = second[:, :width_dense, :]
-    down_parts = second[:, width_dense:, :]
     whole = head_gather(tokens)
     normed_one = layer_norm(whole, ln1_gain, ln1_bias).astype(jnp.bfloat16)
     normed_two = layer_norm(whole, ln2_gain, ln2_bias).astype(jnp.bfloat16)
@@ -169,9 +166,8 @@
     ) + jnp.dot(new_weights.astype(jnp.bfloat16), new_values, preferred_element_type=jnp.float32)
     attention = (summed / total[:, None]).astype(jnp.bfloat16)
     contract = (((1,), (1,)), ((), ()))
-    partial = lax.dot_general(
-        attention, dense_parts, contract, preferred_element_type=jnp.float32
-    ) + lax.dot_general(hidden, down_parts, contract, preferred_element_type=jnp.float32)
+    mixed_in = jnp.concatenate([attention, hidden], axis=1)
+    partial = lax.dot_general(mixed_in, second, contract, preferred_element_type=jnp.float32)
     partial = partial.reshape(rows_total, -1)
     heads = lax.axis_size("head")
     blocks = partial.astype(jnp.bfloat16).reshape(heads, tokens.shape[0], -1)

time: 255 us -> 244 us (0.957)
  matrix products: 19 us -> 11.2 us
  local copies, waits for them, and re-layouts: 30.3 us -> 25.2 us
    dot_general x2 -> x3, matrix products: 14.4 us -> 6.6 us  [the longest x1 3.88 us: body(): lax.dot_general(mixed_in, second, contract, preferred_element_type=jnp.fl...]
  transfers between devices with their start and end apart: 9 -> 9, of which waited for: 5 -> 5; matrix products, arithmetic and copies ran while one was open for 17% -> 18% of each run, Pallas kernels for 0% -> 0%
where the time goes in v6:
time: 244 us; the launch traced here: 243 us
  waiting for transfers between devices  104 us (43%)
  blocking collectives  42.5 us (17%)
  starting transfers between devices  27.2 us (11%)
  local copies, waits for them, and re-layouts  25.2 us (10%)
  other arithmetic  18.3 us (8%)
  between operations  13.9 us (6%)
  matrix products  11.2 us (5%)
    all_gather x1, waiting for transfers between devices, body(): lax.all_gather(jnp.concatenate([w_dense, w_down], axis=0), 'tok', axis=0,...  60.9 us
    all_to_all x1, blocking collectives, body(): exchanged = lax.all_to_all(blocks, 'head', 0, 0, tiled=True)  42.5 us
    all_gather x1, waiting for transfers between devices, body(): lax.all_gather(jnp.concatenate([w_qkv, w_up], axis=1), 'tok', axis=0, til...  34 us
    ppermute x7, starting transfers between devices, gather_stage(): lax.ppermute(stacked, 'head', stage_pairs(size, stride, shift, total))  27.2 us
    ppermute x7, waiting for transfers between devices, gather_stage(): lax.ppermute(stacked, 'head', stage_pairs(size, stride, shift, total))  9.45 us
    convert_element_type x2, local copies, waits for them, and re-layouts, body(): normed_one = layer_norm(whole, ln1_gain, ln1_bias).astype(jnp.bfloat16)  5.91 us
    convert_element_type x2, local copies, waits for them, and re-layouts, body(): normed_two = layer_norm(whole, ln2_gain, ln2_bias).astype(jnp.bfloat16)  4.98 us
  transfers between devices with their start and end apart: 9, of which 5 were waited for; matrix products, arithmetic and copies ran while one was open for 18% of the time, Pallas kernels for 0%

profile of v6, /device:TPU:1, one launch (start us, length us, event | category | flops | bytes accessed | tf_op | source)
XLA Modules:
  0.0 242.8 jit_solution(10816397491714344849)
XLA Ops:
  6.5 1.9 pad_maximum_fusion.2
  8.6 4.0 %collective-permute-start = (bf16[6,4096]{1,0:T(8,128)(2,1)}, bf16[6,4096]{1,0:T(8,128)(2,1)S(1)}, u32[]{:S(2)}, u32[]{:S(2)}) collective-permute-start(bf16[6,4096]{1,0:T(8,128)(2,1)} %param.16), channel_id=1, source_target_pairs={{0,8},{1,9},{2,10},{3,11},{4,12},{5,13},{6,14},{7,15},{8,16},{9,17... | collective-permute-start | bytes 147464 | tf_op jit(solution)/shard_map/ppermute | solution.py:77
  12.6 4.5 %collective-permute-start.1 = (bf16[6,4096]{1,0:T(8,128)(2,1)}, bf16[6,4096]{1,0:T(8,128)(2,1)S(1)}, u32[]{:S(2)}, u32[]{:S(2)}) collective-permute-start(bf16[6,4096]{1,0:T(8,128)(2,1)} %param.16), channel_id=1, source_target_pairs={{0,16},{1,17},{2,18},{3,19},{4,20},{5,21},{6,22},{7,23},{8,24},{9,... | collective-permute-start | bytes 147464 | tf_op jit(solution)/shard_map/ppermute | solution.py:77
  17.1 3.0 %collective-permute-start.2 = (bf16[6,4096]{1,0:T(8,128)(2,1)}, bf16[6,4096]{1,0:T(8,128)(2,1)S(1)}, u32[]{:S(2)}, u32[]{:S(2)}) collective-permute-start(bf16[6,4096]{1,0:T(8,128)(2,1)} %param.16), channel_id=1, source_target_pairs={{0,24},{1,25},{2,26},{3,27},{4,28},{5,29},{6,30},{7,31},{8,0},{9,1... | collective-permute-start | bytes 147464 | tf_op jit(solution)/shard_map/ppermute | solution.py:77
  20.1 1.7 pad_maximum_fusion.3
  26.4 4.4 %collective-permute-start.5 = (bf16[4,6,4096]{2,1,0:T(8,128)(2,1)S(1)}, bf16[4,6,4096]{2,1,0:T(8,128)(2,1)S(1)}, u32[]{:S(2)}, u32[]{:S(2)}) collective-permute-start(bf16[4,6,4096]{2,1,0:T(8,128)(2,1)S(1)} %broadcast_select_fusion.2), channel_id=1, source_target_pairs={{0,6},{1,7},{2,0},{3,1},{4,2},{5,3},{6,4},{7,5},{8,14},{9,15},{10,... | collective-permute-start | bytes 589832 | tf_op jit(solution)/shard_map/ppermute | solution.py:77
  30.8 1.9 collective-permute-start.3
  32.8 3.6 %collective-permute-start.4 = (bf16[4,6,4096]{2,1,0:T(8,128)(2,1)S(1)}, bf16[4,6,4096]{2,1,0:T(8,128)(2,1)S(1)}, u32[]{:S(2)}, u32[]{:S(2)}) collective-permute-start(bf16[4,6,4096]{2,1,0:T(8,128)(2,1)S(1)} %broadcast_select_fusion.2), channel_id=1, source_target_pairs={{0,4},{1,5},{2,6},{3,7},{4,0},{5,1},{6,2},{7,3},{8,12},{9,13},{10,... | collective-permute-start | bytes 589832 | tf_op jit(solution)/shard_map/ppermute | solution.py:77
  36.5 4.4 %collective-permute-done.3 = bf16[4,6,4096]{2,1,0:T(8,128)(2,1)S(1)} collective-permute-done((bf16[4,6,4096]{2,1,0:T(8,128)(2,1)S(1)}, bf16[4,6,4096]{2,1,0:T(8,128)(2,1)S(1)}, u32[]{:S(2)}, u32[]{:S(2)}) %collective-permute-start.3) | collective-permute-done | bytes 196640 | tf_op jit(solution)/shard_map/ppermute | solution.py:77
  40.9 3.8 %collective-permute-done.4 = bf16[4,6,4096]{2,1,0:T(8,128)(2,1)S(1)} collective-permute-done((bf16[4,6,4096]{2,1,0:T(8,128)(2,1)S(1)}, bf16[4,6,4096]{2,1,0:T(8,128)(2,1)S(1)}, u32[]{:S(2)}, u32[]{:S(2)}) %collective-permute-start.4) | collective-permute-done | bytes 196640 | tf_op jit(solution)/shard_map/ppermute | solution.py:77
  45.5 1.2 gather_fusion.1
  47.2 5.7 %collective-permute-start.6 = (bf16[4,4,6,4096]{3,1,2,0:T(4,128)(2,1)S(1)}, bf16[4,4,6,4096]{3,1,2,0:T(4,128)(2,1)S(1)}, u32[]{:S(2)}, u32[]{:S(2)}) collective-permute-start(bf16[4,4,6,4096]{3,1,2,0:T(4,128)(2,1)S(1)} %broadcast_select_fusion.1), channel_id=1, source_target_pairs={{0,1},{1,0},{2,3},{3,2},{4,5},{5,4},{6,7},{7,6},{8,9},{9,8},{10,11... | collective-permute-start | bytes 2359304 | tf_op jit(solution)/shard_map/ppermute | solution.py:77
  53.3 1.3 collective-permute-done.6
  54.6 1.1 pad_maximum_fusion
  55.7 3.0 %gather_fusion.2 = bf16[2,4,4,6,4096]{4,2,3,1,0:T(4,128)(2,1)} fusion(bf16[2,4,4,6,4096]{4,2,3,1,0:T(4,128)(2,1)S(1)} %pad_maximum_fusion, s32[1024]{0:T(1024)S(1)} %pad_clamp_fusion), kind=kCustom, calls=%fused_computation.2 | custom fusion | bytes 3145736 | tf_op jit(solution)/shard_map/jit(_take)/gather | solution.py:80
  58.8 3.2 %bitcast_reduce_fusion = (f32[4,4,2,6]{0,3,1,2:T(8,128)S(1)}, bf16[2,4,4,6,4096]{4,2,3,1,0:T(4,128)(2,1)S(1)}) fusion(bf16[2,4,4,6,4096]{4,2,3,1,0:T(4,128)(2,1)} %gather_fusion.2, pred[2]{0:T(512)(128)(4,1)S(1)} %compare_and_fusion.2), kind=kLoop, calls=%fused_computation.13 | loop fusion | flops 2359104 | bytes 3146498 | tf_op jit(solution)/shard_map/reduce_sum | solution.py:17
  61.9 1.2 fusion.13
  63.2 2.1 fusion.10
  65.2 2.2 copy.35
  67.5 3.7 %convert_element_type.70 = bf16[192,4096]{1,0:T(8,128)(2,1)} reshape(bf16[4,4,2,6,4096]{4,3,2,1,0:T(8,128)(2,1)} %copy.35) | data formatting | bytes 3145728 | tf_op jit(solution)/shard_map/convert_element_type | solution.py:139
  71.1 2.2 copy.37
  73.4 2.8 %convert_element_type.76 = bf16[192,4096]{1,0:T(8,128)(2,1)S(1)} reshape(bf16[4,4,2,6,4096]{4,3,2,1,0:T(8,128)(2,1)} %copy.37) | data formatting | bytes 3145728 | tf_op jit(solution)/shard_map/convert_element_type | solution.py:140
  76.1 34.0 %all-gather.5.cloned.1.call-done = bf16[4096,896]{1,0:T(8,128)(2,1)} async-done(((bf16[256,896]{1,0:T(8,128)(2,1)}), bf16[4096,896]{1,0:T(8,128)(2,1)}) %all-gather.5.cloned.1.call-update) | async-done | bytes 7340048 | tf_op jit(solution)/shard_map/all_gather | solution.py:131
  110.2 2.3 slice.53
  112.5 2.7 %slice.61 = bf16[16,256,512]{2,1,0:T(8,128)(2,1)S(1)} slice(bf16[16,256,896]{2,1,0:T(8,128)(2,1)} %bitcast.57), slice={[0:16], [0:256], [384:896]} | slice | bytes 8388608 | tf_op jit(solution)/shard_map/slice | solution.py:137
  115.2 1.4 fusion.83
  117.1 2.7 %fusion.84 = (f32[192]{0:T(256)S(1)}, f32[192,6144]{1,0:T(8,128)S(1)}) fusion(bf16[6144,128]{1,0:T(8,128)(2,1)S(1)} %copy-done, bf16[192,96]{0,1:T(8,128)(2,1)S(1)} %get-tuple-element.15, bf16[192,16]{0,1:T(8,128)(2,1)S(1)} %get-tuple-element.14, bf16[192,16]{0,1:T(8,128)(2,1)S(1)} %get-tuple-element.11, pred[6144]{0:T(1024)(128)(4,1)S(1)} %broadcast_compare_fusion, ...), kind=kOutput, calls=%fused_computation.160 | convolution fusion | flops 313933632 | bytes 6398208 | tf_op jit(solution)/shard_map/dot_general | solution.py:152
  122.1 1.8 fusion.29
  123.9 60.9 %all-gather.7.cloned.1.call-done = bf16[10240,256]{1,0:T(8,128)(2,1)} async-done(((bf16[640,256]{1,0:T(8,128)(2,1)}), bf16[10240,256]{1,0:T(8,128)(2,1)}) %all-gather.7.cloned.1.call-update) | async-done | bytes 5242896 | tf_op jit(solution)/shard_map/all_gather | solution.py:132
  184.8 3.9 %convolution_convert_fusion = bf16[192,16,256]{2,0,1:T(8,128)(2,1)S(1)} fusion(bf16[16,640,256]{2,1,0:T(8,128)(2,1)} %bitcast.58, bf16[192,512]{1,0:T(8,128)(2,1)S(1)} %fusion.29, bf16[192,128]{1,0:T(8,128)(2,1)S(1)} %fusion.24), kind=kOutput, calls=%fused_computation.25 | convolution fusion | flops 1007910912 | bytes 7061504 | tf_op jit(solution)/shard_map/dot_general | solution.py:170
  189.6 2.7 %convert_element_type.79 = bf16[32,6,4096]{2,1,0:T(8,128)(2,1)} reshape(bf16[192,16,256]{2,1,0:T(8,128)(2,1)S(1)} %copy.38) | data formatting | bytes 3145728 | tf_op jit(solution)/shard_map/convert_element_type | solution.py:173
  192.3 42.5 %all_to_all.5 = bf16[32,6,4096]{2,1,0:T(8,128)(2,1)S(1)} all-to-all(bf16[32,6,4096]{2,1,0:T(8,128)(2,1)} %convert_element_type.79), channel_id=1, replica_groups=mesh['tok'=16,'head'=32] {'head'}, dimensions={0} | all-to-all | bytes 3145728 | tf_op jit(solution)/shard_map/all_to_all | solution.py:174
  (73 shorter events, 11.0 us)
Async XLA Ops:
  6.5 110.5 %copy-start = (bf16[6144,128]{1,0:T(8,128)(2,1)S(1)}, bf16[6144,128]{1,0:T(8,128)(2,1)}, u32[]{:S(2)}) copy-start(bf16[6144,128]{1,0:T(8,128)(2,1)} %param.29) | copy-start | bytes 4718596
  6.5 103.6 %all-gather.5.cloned.1.call-start = ((), (), s32[]{:S(2)}) async-start(), calls=%async_computation.1 | async-start | bytes 7798784 | tf_op jit(solution)/shard_map/all_gather | solution.py:131
  8.5 176.3 %all-gather.7.cloned.1.call-start = ((), (), s32[]{:S(2)}) async-start(), calls=%async_computation.2 | async-start | bytes 5570560 | tf_op jit(solution)/shard_map/all_gather | solution.py:132
  8.6 16.2 %collective-permute-start = (bf16[6,4096]{1,0:T(8,128)(2,1)}, bf16[6,4096]{1,0:T(8,128)(2,1)S(1)}, u32[]{:S(2)}, u32[]{:S(2)}) collective-permute-start(bf16[6,4096]{1,0:T(8,128)(2,1)} %param.16), channel_id=1, source_target_pairs={{0,8},{1,9},{2,10},{3,11},{4,12},{5,13},{6,14},{7,15},{8,16},{9,17... | collective-permute-start | bytes 147464 | tf_op jit(solution)/shard_map/ppermute | solution.py:77
  12.6 12.2 %collective-permute-start.1 = (bf16[6,4096]{1,0:T(8,128)(2,1)}, bf16[6,4096]{1,0:T(8,128)(2,1)S(1)}, u32[]{:S(2)}, u32[]{:S(2)}) collective-permute-start(bf16[6,4096]{1,0:T(8,128)(2,1)} %param.16), channel_id=1, source_target_pairs={{0,16},{1,17},{2,18},{3,19},{4,20},{5,21},{6,22},{7,23},{8,24},{9,... | collective-permute-start | bytes 147464 | tf_op jit(solution)/shard_map/ppermute | solution.py:77
  17.1 7.7 %collective-permute-start.2 = (bf16[6,4096]{1,0:T(8,128)(2,1)}, bf16[6,4096]{1,0:T(8,128)(2,1)S(1)}, u32[]{:S(2)}, u32[]{:S(2)}) collective-permute-start(bf16[6,4096]{1,0:T(8,128)(2,1)} %param.16), channel_id=1, source_target_pairs={{0,24},{1,25},{2,26},{3,27},{4,28},{5,29},{6,30},{7,31},{8,0},{9,1... | collective-permute-start | bytes 147464 | tf_op jit(solution)/shard_map/ppermute | solution.py:77
  26.4 10.1 %collective-permute-start.5 = (bf16[4,6,4096]{2,1,0:T(8,128)(2,1)S(1)}, bf16[4,6,4096]{2,1,0:T(8,128)(2,1)S(1)}, u32[]{:S(2)}, u32[]{:S(2)}) collective-permute-start(bf16[4,6,4096]{2,1,0:T(8,128)(2,1)S(1)} %broadcast_select_fusion.2), channel_id=1, source_target_pairs={{0,6},{1,7},{2,0},{3,1},{4,2},{5,3},{6,4},{7,5},{8,14},{9,15},{10,... | collective-permute-start | bytes 589832 | tf_op jit(solution)/shard_map/ppermute | solution.py:77
  30.8 10.0 %collective-permute-start.3 = (bf16[4,6,4096]{2,1,0:T(8,128)(2,1)S(1)}, bf16[4,6,4096]{2,1,0:T(8,128)(2,1)S(1)}, u32[]{:S(2)}, u32[]{:S(2)}) collective-permute-start(bf16[4,6,4096]{2,1,0:T(8,128)(2,1)S(1)} %broadcast_select_fusion.2), channel_id=1, source_target_pairs={{0,2},{1,3},{2,4},{3,5},{4,6},{5,7},{6,0},{7,1},{8,10},{9,11},{10,... | collective-permute-start | bytes 589832 | tf_op jit(solution)/shard_map/ppermute | solution.py:77
  32.8 11.9 %collective-permute-start.4 = (bf16[4,6,4096]{2,1,0:T(8,128)(2,1)S(1)}, bf16[4,6,4096]{2,1,0:T(8,128)(2,1)S(1)}, u32[]{:S(2)}, u32[]{:S(2)}) collective-permute-start(bf16[4,6,4096]{2,1,0:T(8,128)(2,1)S(1)} %broadcast_select_fusion.2), channel_id=1, source_target_pairs={{0,4},{1,5},{2,6},{3,7},{4,0},{5,1},{6,2},{7,3},{8,12},{9,13},{10,... | collective-permute-start | bytes 589832 | tf_op jit(solution)/shard_map/ppermute | solution.py:77
  47.2 7.4 %collective-permute-start.6 = (bf16[4,4,6,4096]{3,1,2,0:T(4,128)(2,1)S(1)}, bf16[4,4,6,4096]{3,1,2,0:T(4,128)(2,1)S(1)}, u32[]{:S(2)}, u32[]{:S(2)}) collective-permute-start(bf16[4,4,6,4096]{3,1,2,0:T(4,128)(2,1)S(1)} %broadcast_select_fusion.1), channel_id=1, source_target_pairs={{0,1},{1,0},{2,3},{3,2},{4,5},{5,4},{6,7},{7,6},{8,9},{9,8},{10,11... | collective-permute-start | bytes 2359304 | tf_op jit(solution)/shard_map/ppermute | solution.py:77
  58.7 4.4 %copy-start.4 = (f32[4096]{0:T(1024)S(1)}, f32[4096]{0:T(1024)}, u32[]{:S(2)}) copy-start(f32[4096]{0:T(1024)} %param.18) | copy-start | bytes 49156
  58.7 4.4 %copy-start.5 = (f32[4096]{0:T(1024)S(1)}, f32[4096]{0:T(1024)}, u32[]{:S(2)}) copy-start(f32[4096]{0:T(1024)} %param.17) | copy-start | bytes 49156
  58.7 4.4 %copy-start.6 = (f32[4096]{0:T(1024)S(1)}, f32[4096]{0:T(1024)}, u32[]{:S(2)}) copy-start(f32[4096]{0:T(1024)} %param.20) | copy-start | bytes 49156
  58.8 4.4 %copy-start.7 = (f32[4096]{0:T(1024)S(1)}, f32[4096]{0:T(1024)}, u32[]{:S(2)}) copy-start(f32[4096]{0:T(1024)} %param.19) | copy-start | bytes 49156
  112.4 2.8 %copy-start.1 = (bf16[192,4096]{1,0:T(8,128)(2,1)S(1)}, bf16[192,4096]{1,0:T(8,128)(2,1)}, u32[]{:S(2)}) copy-start(bf16[192,4096]{1,0:T(8,128)(2,1)} %convert_element_type.70) | copy-start | bytes 4718596
  112.5 2.8 %copy-start.10 = (f32[384]{0:T(512)S(1)}, f32[384]{0:T(512)}, u32[]{:S(2)}) copy-start(f32[384]{0:T(512)} %param.22) | copy-start | bytes 4612
  119.8 1.4 copy-start.2
  121.2 0.9 copy-start.11
  192.3 43.0 %copy-start.3 = (bf16[6,4096]{1,0:T(8,128)(2,1)S(1)}, bf16[6,4096]{1,0:T(8,128)(2,1)}, u32[]{:S(2)}) copy-start(bf16[6,4096]{1,0:T(8,128)(2,1)} %param.16) | copy-start | bytes 147460
  192.3 43.0 %copy-start.8 = (f32[4096]{0:T(1024)S(1)}, f32[4096]{0:T(1024)}, u32[]{:S(2)}) copy-start(f32[4096]{0:T(1024)} %param.28) | copy-start | bytes 49156
  192.3 43.0 %copy-start.9 = (f32[4096]{0:T(1024)S(1)}, f32[4096]{0:T(1024)}, u32[]{:S(2)}) copy-start(f32[4096]{0:T(1024)} %param.24) | copy-start | bytes 49156
Sparse Core Ops, SparseCore 0:
  9.4 100.7 all-gather.4
  112.3 72.5 all-gather.6

commit v7 on v6

--- a/solution.py
+++ b/solution.py
@@ -1,4 +1,5 @@
 import jax
+import numpy as np
 import jax.numpy as jnp
 from jax import lax
 from jax.sharding import PartitionSpec as P
@@ -84,7 +85,7 @@
     by_y = gather_stage(block, 4, 8)
     by_x = gather_stage(by_y, 4, 2)
     by_core = gather_stage(by_x, 2, 1)
-    ordered = by_core.transpose((2, 1, 0) + tuple(range(3, by_core.ndim)))
+    ordered = by_core.transpose((0, 2, 1) + tuple(range(3, by_core.ndim)))
     return ordered.reshape((-1,) + block.shape[1:])
 
 
@@ -143,6 +144,9 @@
     upward = jnp.dot(normed_two, up_full, preferred_element_type=jnp.float32)
     lengths_row = cache_lengths[0]
     query_owner, query_place = token_layout(lengths_row, rows_total)
+    source = np.arange(rows_total).reshape(4, 4, 2, -1).transpose(2, 0, 1, 3).reshape(-1)
+    query_owner = jnp.take(query_owner, source)
+    query_place = jnp.take(query_place, source)
     queries = rotate(projected[:, :HD], query_place).astype(jnp.bfloat16)
     new_keys = rotate(projected[:, HD : 2 * HD], query_place).astype(jnp.bfloat16)
     new_values = projected[:, 2 * HD :].astype(jnp.bfloat16)
@@ -170,8 +174,16 @@
     partial = lax.dot_general(mixed_in, second, contract, preferred_element_type=jnp.float32)
     partial = partial.reshape(rows_total, -1)
     heads = lax.axis_size("head")
-    blocks = partial.astype(jnp.bfloat16).reshape(heads, tokens.shape[0], -1)
-    exchanged = lax.all_to_all(blocks, "head", 0, 0, tiled=True)
+    blocks = partial.reshape(2, heads // 2, tokens.shape[0], -1)
+    core = lax.axis_index("head") % 2
+    mine = lax.dynamic_index_in_dim(blocks, core, 0, keepdims=False)
+    theirs = lax.dynamic_index_in_dim(blocks, 1 - core, 0, keepdims=False)
+    swapped = lax.ppermute(
+        theirs.astype(jnp.bfloat16), "head", [(index, index ^ 1) for index in range(heads)]
+    )
+    chip_sum = (mine + swapped.astype(jnp.float32)).astype(jnp.bfloat16)
+    groups = [list(range(side, heads, 2)) for side in range(2)]
+    exchanged = lax.all_to_all(chip_sum, "head", 0, 0, axis_index_groups=groups, tiled=True)
     partial_value = jnp.sum(exchanged.astype(jnp.float32), axis=0)
     mixed = tokens.astype(jnp.float32) + partial_value + b_dense + b_down
     return mixed.astype(jnp.bfloat16)

time: 244 us -> 243 us (level)
  blocking collectives: 42.5 us -> 22.8 us
  local copies, waits for them, and re-layouts: 25.2 us -> 37.7 us
  starting transfers between devices: 27.2 us -> 36.1 us
  waiting for transfers between devices: 104 us -> 101 us
    all_to_all x1, blocking collectives: 42.5 us -> 22.8 us  [body(): lax.all_to_all(chip_sum, 'head', 0, 0, axis_index_groups=groups, tiled=True)]
    ppermute x0 -> x1, starting transfers between devices: none -> 8.9 us  [body(): lax.ppermute(theirs.astype(jnp.bfloat16), 'head', [(index, index ^ 1) for...]
    another operation x0 -> x1, local copies, waits for them, and re-layouts: none -> 4.92 us  [body(): blocks = partial.reshape(2, heads // 2, tokens.shape[0], -1)]
    dot_general x0 -> x1, local copies, waits for them, and re-layouts: none -> 3.51 us  [body(): lax.dot_general(mixed_in, second, contract, preferred_element_type=jnp.fl...]
    gather x0 -> x2, local copies, waits for them, and re-layouts: none -> 3.22 us  [the longest x1 1.61 us: body(): query_place = jnp.take(query_place, source)]
    all_gather x1, waiting for transfers between devices: 34 us -> 30.9 us  [body(): lax.all_gather(jnp.concatenate([w_qkv, w_up], axis=1), 'tok', axis=0, til...]
  transfers between devices with their start and end apart: 9 -> 10, of which waited for: 5 -> 6; matrix products, arithmetic and copies ran while one was open for 18% -> 20% of each run, Pallas kernels for 0% -> 0%
where the time goes in v7:
time: 243 us; the launch traced here: 242 us
  waiting for transfers between devices  101 us (42%)
  local copies, waits for them, and re-layouts  37.7 us (16%)
  starting transfers between devices  36.1 us (15%)
  blocking collectives  22.8 us (9%)
  other arithmetic  18.9 us (8%)
  between operations  14 us (6%)
  matrix products  11.2 us (5%)
    all_gather x1, waiting for transfers between devices, body(): lax.all_gather(jnp.concatenate([w_dense, w_down], axis=0), 'tok', axis=0,...  60.9 us
    all_gather x1, waiting for transfers between devices, body(): lax.all_gather(jnp.concatenate([w_qkv, w_up], axis=1), 'tok', axis=0, til...  30.9 us
    ppermute x7, starting transfers between devices, gather_stage(): lax.ppermute(stacked, 'head', stage_pairs(size, stride, shift, total))  27.2 us
    all_to_all x1, blocking collectives, body(): lax.all_to_all(chip_sum, 'head', 0, 0, axis_index_groups=groups, tiled=True)  22.8 us
    ppermute x7, waiting for transfers between devices, gather_stage(): lax.ppermute(stacked, 'head', stage_pairs(size, stride, shift, total))  9.45 us
    ppermute x1, starting transfers between devices, body(): lax.ppermute(theirs.astype(jnp.bfloat16), 'head', [(index, index ^ 1) for...  8.9 us
    convert_element_type x2, local copies, waits for them, and re-layouts, body(): normed_one = layer_norm(whole, ln1_gain, ln1_bias).astype(jnp.bfloat16)  5.94 us
    convert_element_type x2, local copies, waits for them, and re-layouts, body(): normed_two = layer_norm(whole, ln2_gain, ln2_bias).astype(jnp.bfloat16)  5.02 us
  transfers between devices with their start and end apart: 10, of which 6 were waited for; matrix products, arithmetic and copies ran while one was open for 20% of the time, Pallas kernels for 0%

profile of v7, /device:TPU:1, one launch (start us, length us, event | category | flops | bytes accessed | tf_op | source)
XLA Modules:
  0.0 242.1 jit_solution(18016439119373889386)
XLA Ops:
  6.5 2.0 pad_maximum_fusion.2
  8.6 4.0 %collective-permute-start = (bf16[6,4096]{1,0:T(8,128)(2,1)}, bf16[6,4096]{1,0:T(8,128)(2,1)S(1)}, u32[]{:S(2)}, u32[]{:S(2)}) collective-permute-start(bf16[6,4096]{1,0:T(8,128)(2,1)} %param.19), channel_id=1, source_target_pairs={{0,8},{1,9},{2,10},{3,11},{4,12},{5,13},{6,14},{7,15},{8,16},{9,17... | collective-permute-start | bytes 147464 | tf_op jit(solution)/shard_map/ppermute | solution.py:78
  12.6 4.5 %collective-permute-start.1 = (bf16[6,4096]{1,0:T(8,128)(2,1)}, bf16[6,4096]{1,0:T(8,128)(2,1)S(1)}, u32[]{:S(2)}, u32[]{:S(2)}) collective-permute-start(bf16[6,4096]{1,0:T(8,128)(2,1)} %param.19), channel_id=1, source_target_pairs={{0,16},{1,17},{2,18},{3,19},{4,20},{5,21},{6,22},{7,23},{8,24},{9,... | collective-permute-start | bytes 147464 | tf_op jit(solution)/shard_map/ppermute | solution.py:78
  17.2 3.0 %collective-permute-start.2 = (bf16[6,4096]{1,0:T(8,128)(2,1)}, bf16[6,4096]{1,0:T(8,128)(2,1)S(1)}, u32[]{:S(2)}, u32[]{:S(2)}) collective-permute-start(bf16[6,4096]{1,0:T(8,128)(2,1)} %param.19), channel_id=1, source_target_pairs={{0,24},{1,25},{2,26},{3,27},{4,28},{5,29},{6,30},{7,31},{8,0},{9,1... | collective-permute-start | bytes 147464 | tf_op jit(solution)/shard_map/ppermute | solution.py:78
  20.2 1.7 pad_maximum_fusion.3
  25.5 1.6 gather_fusion.4
  29.5 4.4 %collective-permute-start.5 = (bf16[4,6,4096]{2,1,0:T(8,128)(2,1)S(1)}, bf16[4,6,4096]{2,1,0:T(8,128)(2,1)S(1)}, u32[]{:S(2)}, u32[]{:S(2)}) collective-permute-start(bf16[4,6,4096]{2,1,0:T(8,128)(2,1)S(1)} %broadcast_select_fusion.2), channel_id=1, source_target_pairs={{0,6},{1,7},{2,0},{3,1},{4,2},{5,3},{6,4},{7,5},{8,14},{9,15},{10,... | collective-permute-start | bytes 589832 | tf_op jit(solution)/shard_map/ppermute | solution.py:78
  33.9 1.9 collective-permute-start.3
  35.9 3.6 %collective-permute-start.4 = (bf16[4,6,4096]{2,1,0:T(8,128)(2,1)S(1)}, bf16[4,6,4096]{2,1,0:T(8,128)(2,1)S(1)}, u32[]{:S(2)}, u32[]{:S(2)}) collective-permute-start(bf16[4,6,4096]{2,1,0:T(8,128)(2,1)S(1)} %broadcast_select_fusion.2), channel_id=1, source_target_pairs={{0,4},{1,5},{2,6},{3,7},{4,0},{5,1},{6,2},{7,3},{8,12},{9,13},{10,... | collective-permute-start | bytes 589832 | tf_op jit(solution)/shard_map/ppermute | solution.py:78
  39.6 4.4 %collective-permute-done.3 = bf16[4,6,4096]{2,1,0:T(8,128)(2,1)S(1)} collective-permute-done((bf16[4,6,4096]{2,1,0:T(8,128)(2,1)S(1)}, bf16[4,6,4096]{2,1,0:T(8,128)(2,1)S(1)}, u32[]{:S(2)}, u32[]{:S(2)}) %collective-permute-start.3) | collective-permute-done | bytes 196640 | tf_op jit(solution)/shard_map/ppermute | solution.py:78
  44.0 3.8 %collective-permute-done.4 = bf16[4,6,4096]{2,1,0:T(8,128)(2,1)S(1)} collective-permute-done((bf16[4,6,4096]{2,1,0:T(8,128)(2,1)S(1)}, bf16[4,6,4096]{2,1,0:T(8,128)(2,1)S(1)}, u32[]{:S(2)}, u32[]{:S(2)}) %collective-permute-start.4) | collective-permute-done | bytes 196640 | tf_op jit(solution)/shard_map/ppermute | solution.py:78
  50.3 5.7 %collective-permute-start.6 = (bf16[4,4,6,4096]{3,1,2,0:T(4,128)(2,1)S(1)}, bf16[4,4,6,4096]{3,1,2,0:T(4,128)(2,1)S(1)}, u32[]{:S(2)}, u32[]{:S(2)}) collective-permute-start(bf16[4,4,6,4096]{3,1,2,0:T(4,128)(2,1)S(1)} %broadcast_select_fusion.1), channel_id=1, source_target_pairs={{0,1},{1,0},{2,3},{3,2},{4,5},{5,4},{6,7},{7,6},{8,9},{9,8},{10,11... | collective-permute-start | bytes 2359304 | tf_op jit(solution)/shard_map/ppermute | solution.py:78
  58.8 3.0 %gather_fusion.2 = bf16[2,4,4,6,4096]{4,2,3,1,0:T(4,128)(2,1)} fusion(bf16[2,4,4,6,4096]{4,2,3,1,0:T(4,128)(2,1)S(1)} %pad_maximum_fusion, s32[1024]{0:T(1024)S(1)} %pad_clamp_fusion), kind=kCustom, calls=%fused_computation.4 | custom fusion | bytes 3145736 | tf_op jit(solution)/shard_map/jit(_take)/gather | solution.py:81
  61.8 3.2 %bitcast_reduce_fusion = (f32[2,4,4,6]{1,3,2,0:T(8,128)S(1)}, bf16[2,4,4,6,4096]{4,2,3,1,0:T(4,128)(2,1)S(1)}) fusion(bf16[2,4,4,6,4096]{4,2,3,1,0:T(4,128)(2,1)} %gather_fusion.2, pred[2]{0:T(512)(128)(4,1)S(1)} %compare_and_fusion.2), kind=kLoop, calls=%fused_computation.14 | loop fusion | flops 2359104 | bytes 3146498 | tf_op jit(solution)/shard_map/reduce_sum | solution.py:18
  66.3 2.1 fusion.10
  68.4 2.2 copy.51
  70.6 3.7 %convert_element_type.71 = bf16[192,4096]{1,0:T(8,128)(2,1)} reshape(bf16[2,4,4,6,4096]{4,3,2,1,0:T(8,128)(2,1)} %copy.51) | data formatting | bytes 3145728 | tf_op jit(solution)/shard_map/convert_element_type | solution.py:140
  74.3 2.2 copy.53
  76.5 2.8 %convert_element_type.77 = bf16[192,4096]{1,0:T(8,128)(2,1)S(1)} reshape(bf16[2,4,4,6,4096]{4,3,2,1,0:T(8,128)(2,1)} %copy.53) | data formatting | bytes 3145728 | tf_op jit(solution)/shard_map/convert_element_type | solution.py:141
  79.3 30.9 %all-gather.5.cloned.1.call-done = bf16[4096,896]{1,0:T(8,128)(2,1)} async-done(((bf16[256,896]{1,0:T(8,128)(2,1)}), bf16[4096,896]{1,0:T(8,128)(2,1)}) %all-gather.5.cloned.1.call-update) | async-done | bytes 7340048 | tf_op jit(solution)/shard_map/all_gather | solution.py:132
  110.2 2.3 slice.57
  112.5 2.7 %slice.65 = bf16[16,256,512]{2,1,0:T(8,128)(2,1)S(1)} slice(bf16[16,256,896]{2,1,0:T(8,128)(2,1)} %bitcast.63), slice={[0:16], [0:256], [384:896]} | slice | bytes 8388608 | tf_op jit(solution)/shard_map/slice | solution.py:138
  117.1 2.7 %fusion.86 = (f32[192]{0:T(256)S(1)}, f32[192,6144]{1,0:T(8,128)S(1)}) fusion(bf16[6144,128]{1,0:T(8,128)(2,1)S(1)} %copy-done, bf16[192,96]{0,1:T(8,128)(2,1)S(1)} %get-tuple-element.16, bf16[192,16]{0,1:T(8,128)(2,1)S(1)} %get-tuple-element.15, bf16[192,16]{0,1:T(8,128)(2,1)S(1)} %get-tuple-element.12, pred[6144]{0:T(1024)(128)(4,1)S(1)} %broadcast_compare_fusion, ...), kind=kOutput, calls=%fused_computation.167 | convolution fusion | flops 313933632 | bytes 6398208 | tf_op jit(solution)/shard_map/dot_general | solution.py:156
  122.2 1.8 fusion.31
  123.9 60.9 %all-gather.7.cloned.1.call-done = bf16[10240,256]{1,0:T(8,128)(2,1)} async-done(((bf16[640,256]{1,0:T(8,128)(2,1)}), bf16[10240,256]{1,0:T(8,128)(2,1)}) %all-gather.7.cloned.1.call-update) | async-done | bytes 5242896 | tf_op jit(solution)/shard_map/all_gather | solution.py:133
  184.8 3.9 %fusion.39 = f32[192,16,256]{2,0,1:T(8,128)S(1)} fusion(bf16[16,640,256]{2,1,0:T(8,128)(2,1)} %bitcast.64, bf16[192,512]{1,0:T(8,128)(2,1)S(1)} %fusion.31, bf16[192,128]{1,0:T(8,128)(2,1)S(1)} %fusion.25), kind=kOutput, calls=%fused_computation.71 | convolution fusion | flops 1007124480 | bytes 8634368 | tf_op jit(solution)/shard_map/dot_general | solution.py:174
  188.7 3.5 %copy.54 = f32[192,16,256]{2,1,0:T(8,128)} copy(f32[192,16,256]{2,0,1:T(8,128)S(1)} %fusion.39) | data formatting | bytes 6291456 | tf_op jit(solution)/shard_map/dot_general | solution.py:174
  192.2 4.9 %reshape_reshape.3 = f32[2,16,6,4096]{3,2,1,0:T(8,128)} reshape(f32[192,16,256]{2,1,0:T(8,128)} %copy.54) | data formatting | bytes 6291456 | tf_op jit(solution)/shard_map/reshape;reshape | solution.py:177
  197.2 1.7 fusion.28
  199.3 8.9 %collective-permute-start.7 = (bf16[16,6,4096]{2,0,1:T(8,128)(2,1)S(1)}, bf16[16,6,4096]{2,0,1:T(8,128)(2,1)S(1)}, u32[]{:S(2)}, u32[]{:S(2)}) collective-permute-start(bf16[16,6,4096]{2,0,1:T(8,128)(2,1)S(1)} %copy.56), channel_id=1, source_target_pairs={{0,1},{1,0},{2,3},{3,2},{4,5},{5,4},{6,7},{7,6},{8,9},{9,8},{10,11... | collective-permute-start | bytes 2359304 | tf_op jit(solution)/shard_map/ppermute | solution.py:181
  208.2 1.7 constant_dynamic-slice_fusion
  211.5 22.8 %all_to_all.5 = bf16[16,6,4096]{2,1,0:T(8,128)(2,1)S(1)} all-to-all(bf16[16,6,4096]{2,1,0:T(8,128)(2,1)S(1)} %copy.57), channel_id=1, replica_groups={{0,2,4,6,8,10,12,14,16,18,20,22,24,26,28,30},{1,3,5,7,9,11,13,15,17,19,..., dimensions={0} | all-to-all | bytes 1572864 | tf_op jit(solution)/shard_map/all_to_all | solution.py:186
  (85 shorter events, 19.6 us)
Async XLA Ops:
  6.5 110.5 %copy-start = (bf16[6144,128]{1,0:T(8,128)(2,1)S(1)}, bf16[6144,128]{1,0:T(8,128)(2,1)}, u32[]{:S(2)}) copy-start(bf16[6144,128]{1,0:T(8,128)(2,1)} %param.32) | copy-start | bytes 4718596
  6.5 22.2 %copy-start.4 = (bf16[6,4096]{1,0:T(8,128)(2,1)S(1)}, bf16[6,4096]{1,0:T(8,128)(2,1)}, u32[]{:S(2)}) copy-start(bf16[6,4096]{1,0:T(8,128)(2,1)} %param.19) | copy-start | bytes 147460
  6.5 103.6 %all-gather.5.cloned.1.call-start = ((), (), s32[]{:S(2)}) async-start(), calls=%async_computation.1 | async-start | bytes 7798784 | tf_op jit(solution)/shard_map/all_gather | solution.py:132
  8.5 176.3 %all-gather.7.cloned.1.call-start = ((), (), s32[]{:S(2)}) async-start(), calls=%async_computation.2 | async-start | bytes 5570560 | tf_op jit(solution)/shard_map/all_gather | solution.py:133
  8.6 20.2 %collective-permute-start = (bf16[6,4096]{1,0:T(8,128)(2,1)}, bf16[6,4096]{1,0:T(8,128)(2,1)S(1)}, u32[]{:S(2)}, u32[]{:S(2)}) collective-permute-start(bf16[6,4096]{1,0:T(8,128)(2,1)} %param.19), channel_id=1, source_target_pairs={{0,8},{1,9},{2,10},{3,11},{4,12},{5,13},{6,14},{7,15},{8,16},{9,17... | collective-permute-start | bytes 147464 | tf_op jit(solution)/shard_map/ppermute | solution.py:78
  12.6 16.1 %collective-permute-start.1 = (bf16[6,4096]{1,0:T(8,128)(2,1)}, bf16[6,4096]{1,0:T(8,128)(2,1)S(1)}, u32[]{:S(2)}, u32[]{:S(2)}) collective-permute-start(bf16[6,4096]{1,0:T(8,128)(2,1)} %param.19), channel_id=1, source_target_pairs={{0,16},{1,17},{2,18},{3,19},{4,20},{5,21},{6,22},{7,23},{8,24},{9,... | collective-permute-start | bytes 147464 | tf_op jit(solution)/shard_map/ppermute | solution.py:78
  17.2 11.6 %collective-permute-start.2 = (bf16[6,4096]{1,0:T(8,128)(2,1)}, bf16[6,4096]{1,0:T(8,128)(2,1)S(1)}, u32[]{:S(2)}, u32[]{:S(2)}) collective-permute-start(bf16[6,4096]{1,0:T(8,128)(2,1)} %param.19), channel_id=1, source_target_pairs={{0,24},{1,25},{2,26},{3,27},{4,28},{5,29},{6,30},{7,31},{8,0},{9,1... | collective-permute-start | bytes 147464 | tf_op jit(solution)/shard_map/ppermute | solution.py:78
  29.5 10.1 %collective-permute-start.5 = (bf16[4,6,4096]{2,1,0:T(8,128)(2,1)S(1)}, bf16[4,6,4096]{2,1,0:T(8,128)(2,1)S(1)}, u32[]{:S(2)}, u32[]{:S(2)}) collective-permute-start(bf16[4,6,4096]{2,1,0:T(8,128)(2,1)S(1)} %broadcast_select_fusion.2), channel_id=1, source_target_pairs={{0,6},{1,7},{2,0},{3,1},{4,2},{5,3},{6,4},{7,5},{8,14},{9,15},{10,... | collective-permute-start | bytes 589832 | tf_op jit(solution)/shard_map/ppermute | solution.py:78
  33.9 10.0 %collective-permute-start.3 = (bf16[4,6,4096]{2,1,0:T(8,128)(2,1)S(1)}, bf16[4,6,4096]{2,1,0:T(8,128)(2,1)S(1)}, u32[]{:S(2)}, u32[]{:S(2)}) collective-permute-start(bf16[4,6,4096]{2,1,0:T(8,128)(2,1)S(1)} %broadcast_select_fusion.2), channel_id=1, source_target_pairs={{0,2},{1,3},{2,4},{3,5},{4,6},{5,7},{6,0},{7,1},{8,10},{9,11},{10,... | collective-permute-start | bytes 589832 | tf_op jit(solution)/shard_map/ppermute | solution.py:78
  35.9 11.9 %collective-permute-start.4 = (bf16[4,6,4096]{2,1,0:T(8,128)(2,1)S(1)}, bf16[4,6,4096]{2,1,0:T(8,128)(2,1)S(1)}, u32[]{:S(2)}, u32[]{:S(2)}) collective-permute-start(bf16[4,6,4096]{2,1,0:T(8,128)(2,1)S(1)} %broadcast_select_fusion.2), channel_id=1, source_target_pairs={{0,4},{1,5},{2,6},{3,7},{4,0},{5,1},{6,2},{7,3},{8,12},{9,13},{10,... | collective-permute-start | bytes 589832 | tf_op jit(solution)/shard_map/ppermute | solution.py:78
  50.3 7.4 %collective-permute-start.6 = (bf16[4,4,6,4096]{3,1,2,0:T(4,128)(2,1)S(1)}, bf16[4,4,6,4096]{3,1,2,0:T(4,128)(2,1)S(1)}, u32[]{:S(2)}, u32[]{:S(2)}) collective-permute-start(bf16[4,4,6,4096]{3,1,2,0:T(4,128)(2,1)S(1)} %broadcast_select_fusion.1), channel_id=1, source_target_pairs={{0,1},{1,0},{2,3},{3,2},{4,5},{5,4},{6,7},{7,6},{8,9},{9,8},{10,11... | collective-permute-start | bytes 2359304 | tf_op jit(solution)/shard_map/ppermute | solution.py:78
  61.8 4.4 %copy-start.5 = (f32[4096]{0:T(1024)S(1)}, f32[4096]{0:T(1024)}, u32[]{:S(2)}) copy-start(f32[4096]{0:T(1024)} %param.21) | copy-start | bytes 49156
  61.8 4.4 %copy-start.6 = (f32[4096]{0:T(1024)S(1)}, f32[4096]{0:T(1024)}, u32[]{:S(2)}) copy-start(f32[4096]{0:T(1024)} %param.20) | copy-start | bytes 49156
  61.8 4.4 %copy-start.7 = (f32[4096]{0:T(1024)S(1)}, f32[4096]{0:T(1024)}, u32[]{:S(2)}) copy-start(f32[4096]{0:T(1024)} %param.23) | copy-start | bytes 49156
  61.8 4.4 %copy-start.8 = (f32[4096]{0:T(1024)S(1)}, f32[4096]{0:T(1024)}, u32[]{:S(2)}) copy-start(f32[4096]{0:T(1024)} %param.22) | copy-start | bytes 49156
  112.4 2.8 %copy-start.2 = (bf16[192,4096]{1,0:T(8,128)(2,1)S(1)}, bf16[192,4096]{1,0:T(8,128)(2,1)}, u32[]{:S(2)}) copy-start(bf16[192,4096]{1,0:T(8,128)(2,1)} %convert_element_type.71) | copy-start | bytes 4718596
  112.5 2.8 %copy-start.11 = (f32[384]{0:T(512)S(1)}, f32[384]{0:T(512)}, u32[]{:S(2)}) copy-start(f32[384]{0:T(512)} %param.25) | copy-start | bytes 4612
  119.8 1.4 copy-start.3
  121.2 1.0 copy-start.12
  199.3 10.8 %collective-permute-start.7 = (bf16[16,6,4096]{2,0,1:T(8,128)(2,1)S(1)}, bf16[16,6,4096]{2,0,1:T(8,128)(2,1)S(1)}, u32[]{:S(2)}, u32[]{:S(2)}) collective-permute-start(bf16[16,6,4096]{2,0,1:T(8,128)(2,1)S(1)} %copy.56), channel_id=1, source_target_pairs={{0,1},{1,0},{2,3},{3,2},{4,5},{5,4},{6,7},{7,6},{8,9},{9,8},{10,11... | collective-permute-start | bytes 2359304 | tf_op jit(solution)/shard_map/ppermute | solution.py:181
  210.1 25.1 %copy-start.1 = (bf16[6144,128]{1,0:T(8,128)(2,1)S(1)}, bf16[6144,128]{1,0:T(8,128)(2,1)}, u32[]{:S(2)}) copy-start(bf16[6144,128]{1,0:T(8,128)(2,1)} %param.32) | copy-start | bytes 4718596
  211.1 23.5 %copy-start.9 = (f32[4096]{0:T(1024)S(1)}, f32[4096]{0:T(1024)}, u32[]{:S(2)}) copy-start(f32[4096]{0:T(1024)} %param.31) | copy-start | bytes 49156
  211.1 23.5 %copy-start.10 = (f32[4096]{0:T(1024)S(1)}, f32[4096]{0:T(1024)}, u32[]{:S(2)}) copy-start(f32[4096]{0:T(1024)} %param.27) | copy-start | bytes 49156
Sparse Core Ops, SparseCore 0:
  9.4 100.7 all-gather.4
  112.3 72.5 all-gather.6

commit v8 on v7

--- a/solution.py
+++ b/solution.py
@@ -174,14 +174,14 @@
     partial = lax.dot_general(mixed_in, second, contract, preferred_element_type=jnp.float32)
     partial = partial.reshape(rows_total, -1)
     heads = lax.axis_size("head")
-    blocks = partial.reshape(2, heads // 2, tokens.shape[0], -1)
+    blocks = partial.astype(jnp.bfloat16).reshape(2, heads // 2, tokens.shape[0], -1)
     core = lax.axis_index("head") % 2
     mine = lax.dynamic_index_in_dim(blocks, core, 0, keepdims=False)
     theirs = lax.dynamic_index_in_dim(blocks, 1 - core, 0, keepdims=False)
     swapped = lax.ppermute(
-        theirs.astype(jnp.bfloat16), "head", [(index, index ^ 1) for index in range(heads)]
-    )
-    chip_sum = (mine + swapped.astype(jnp.float32)).astype(jnp.bfloat16)
+        theirs, "head", [(index, index ^ 1) for index in range(heads)]
+    )
+    chip_sum = (mine.astype(jnp.float32) + swapped.astype(jnp.float32)).astype(jnp.bfloat16)
     groups = [list(range(side, heads, 2)) for side in range(2)]
     exchanged = lax.all_to_all(chip_sum, "head", 0, 0, axis_index_groups=groups, tiled=True)
     partial_value = jnp.sum(exchanged.astype(jnp.float32), axis=0)

time: 243 us -> 238 us (0.979)
  local copies, waits for them, and re-layouts: 37.7 us -> 30.3 us
  waiting for transfers between devices: 101 us -> 106 us
    another operation x1 -> x0, local copies, waits for them, and re-layouts: 4.92 us -> none  [body(): blocks = partial.reshape(2, heads // 2, tokens.shape[0], -1)]
    dot_general x1 -> x0, local copies, waits for them, and re-layouts: 3.51 us -> none  [body(): lax.dot_general(mixed_in, second, contract, preferred_element_type=jnp.fl...]
    all_gather x1, waiting for transfers between devices: 30.9 us -> 33.5 us  [body(): lax.all_gather(jnp.concatenate([w_qkv, w_up], axis=1), 'tok', axis=0, til...]
  transfers between devices with their start and end apart: 10 -> 10, of which waited for: 6 -> 6; matrix products, arithmetic and copies ran while one was open for 20% -> 19% of each run, Pallas kernels for 0% -> 0%
where the time goes in v8:
time: 238 us; the launch traced here: 237 us
  waiting for transfers between devices  106 us (45%)
  starting transfers between devices  36.2 us (15%)
  local copies, waits for them, and re-layouts  30.3 us (13%)
  blocking collectives  22.8 us (10%)
  other arithmetic  17.1 us (7%)
  between operations  14 us (6%)
  matrix products  11.2 us (5%)
    all_gather x1, waiting for transfers between devices, body(): lax.all_gather(jnp.concatenate([w_dense, w_down], axis=0), 'tok', axis=0,...  60.8 us
    all_gather x1, waiting for transfers between devices, body(): lax.all_gather(jnp.concatenate([w_qkv, w_up], axis=1), 'tok', axis=0, til...  33.5 us
    ppermute x7, starting transfers between devices, gather_stage(): lax.ppermute(stacked, 'head', stage_pairs(size, stride, shift, total))  27.2 us
    all_to_all x1, blocking collectives, body(): lax.all_to_all(chip_sum, 'head', 0, 0, axis_index_groups=groups, tiled=True)  22.8 us
    ppermute x7, waiting for transfers between devices, gather_stage(): lax.ppermute(stacked, 'head', stage_pairs(size, stride, shift, total))  9.45 us
    ppermute x1, starting transfers between devices, body(): lax.ppermute(theirs, 'head', [(index, index ^ 1) for index in range(heads)])  8.9 us
    convert_element_type x2, local copies, waits for them, and re-layouts, body(): normed_one = layer_norm(whole, ln1_gain, ln1_bias).astype(jnp.bfloat16)  5.93 us
    convert_element_type x2, local copies, waits for them, and re-layouts, body(): normed_two = layer_norm(whole, ln2_gain, ln2_bias).astype(jnp.bfloat16)  5.01 us
  transfers between devices with their start and end apart: 10, of which 6 were waited for; matrix products, arithmetic and copies ran while one was open for 19% of the time, Pallas kernels for 0%

profile of v8, /device:TPU:1, one launch (start us, length us, event | category | flops | bytes accessed | tf_op | source)
XLA Modules:
  0.0 237.2 jit_solution(3458557559253510708)
XLA Ops:
  6.6 1.9 pad_maximum_fusion.2
  8.6 4.0 %collective-permute-start = (bf16[6,4096]{1,0:T(8,128)(2,1)}, bf16[6,4096]{1,0:T(8,128)(2,1)S(1)}, u32[]{:S(2)}, u32[]{:S(2)}) collective-permute-start(bf16[6,4096]{1,0:T(8,128)(2,1)} %param.19), channel_id=1, source_target_pairs={{0,8},{1,9},{2,10},{3,11},{4,12},{5,13},{6,14},{7,15},{8,16},{9,17... | collective-permute-start | bytes 147464 | tf_op jit(solution)/shard_map/ppermute | solution.py:78
  12.7 4.5 %collective-permute-start.1 = (bf16[6,4096]{1,0:T(8,128)(2,1)}, bf16[6,4096]{1,0:T(8,128)(2,1)S(1)}, u32[]{:S(2)}, u32[]{:S(2)}) collective-permute-start(bf16[6,4096]{1,0:T(8,128)(2,1)} %param.19), channel_id=1, source_target_pairs={{0,16},{1,17},{2,18},{3,19},{4,20},{5,21},{6,22},{7,23},{8,24},{9,... | collective-permute-start | bytes 147464 | tf_op jit(solution)/shard_map/ppermute | solution.py:78
  17.2 3.0 %collective-permute-start.2 = (bf16[6,4096]{1,0:T(8,128)(2,1)}, bf16[6,4096]{1,0:T(8,128)(2,1)S(1)}, u32[]{:S(2)}, u32[]{:S(2)}) collective-permute-start(bf16[6,4096]{1,0:T(8,128)(2,1)} %param.19), channel_id=1, source_target_pairs={{0,24},{1,25},{2,26},{3,27},{4,28},{5,29},{6,30},{7,31},{8,0},{9,1... | collective-permute-start | bytes 147464 | tf_op jit(solution)/shard_map/ppermute | solution.py:78
  20.2 1.7 pad_maximum_fusion.3
  22.9 1.6 gather_fusion.4
  24.5 1.6 gather_fusion.3
  27.0 4.4 %collective-permute-start.5 = (bf16[4,6,4096]{2,1,0:T(8,128)(2,1)S(1)}, bf16[4,6,4096]{2,1,0:T(8,128)(2,1)S(1)}, u32[]{:S(2)}, u32[]{:S(2)}) collective-permute-start(bf16[4,6,4096]{2,1,0:T(8,128)(2,1)S(1)} %broadcast_select_fusion.2), channel_id=1, source_target_pairs={{0,6},{1,7},{2,0},{3,1},{4,2},{5,3},{6,4},{7,5},{8,14},{9,15},{10,... | collective-permute-start | bytes 589832 | tf_op jit(solution)/shard_map/ppermute | solution.py:78
  31.4 1.9 collective-permute-start.3
  33.3 3.6 %collective-permute-start.4 = (bf16[4,6,4096]{2,1,0:T(8,128)(2,1)S(1)}, bf16[4,6,4096]{2,1,0:T(8,128)(2,1)S(1)}, u32[]{:S(2)}, u32[]{:S(2)}) collective-permute-start(bf16[4,6,4096]{2,1,0:T(8,128)(2,1)S(1)} %broadcast_select_fusion.2), channel_id=1, source_target_pairs={{0,4},{1,5},{2,6},{3,7},{4,0},{5,1},{6,2},{7,3},{8,12},{9,13},{10,... | collective-permute-start | bytes 589832 | tf_op jit(solution)/shard_map/ppermute | solution.py:78
  37.0 4.4 %collective-permute-done.3 = bf16[4,6,4096]{2,1,0:T(8,128)(2,1)S(1)} collective-permute-done((bf16[4,6,4096]{2,1,0:T(8,128)(2,1)S(1)}, bf16[4,6,4096]{2,1,0:T(8,128)(2,1)S(1)}, u32[]{:S(2)}, u32[]{:S(2)}) %collective-permute-start.3) | collective-permute-done | bytes 196640 | tf_op jit(solution)/shard_map/ppermute | solution.py:78
  41.4 3.8 %collective-permute-done.4 = bf16[4,6,4096]{2,1,0:T(8,128)(2,1)S(1)} collective-permute-done((bf16[4,6,4096]{2,1,0:T(8,128)(2,1)S(1)}, bf16[4,6,4096]{2,1,0:T(8,128)(2,1)S(1)}, u32[]{:S(2)}, u32[]{:S(2)}) %collective-permute-start.4) | collective-permute-done | bytes 196640 | tf_op jit(solution)/shard_map/ppermute | solution.py:78
  47.7 5.7 %collective-permute-start.6 = (bf16[4,4,6,4096]{3,1,2,0:T(4,128)(2,1)S(1)}, bf16[4,4,6,4096]{3,1,2,0:T(4,128)(2,1)S(1)}, u32[]{:S(2)}, u32[]{:S(2)}) collective-permute-start(bf16[4,4,6,4096]{3,1,2,0:T(4,128)(2,1)S(1)} %broadcast_select_fusion.1), channel_id=1, source_target_pairs={{0,1},{1,0},{2,3},{3,2},{4,5},{5,4},{6,7},{7,6},{8,9},{9,8},{10,11... | collective-permute-start | bytes 2359304 | tf_op jit(solution)/shard_map/ppermute | solution.py:78
  56.3 3.0 %gather_fusion.2 = bf16[2,4,4,6,4096]{4,2,3,1,0:T(4,128)(2,1)} fusion(bf16[2,4,4,6,4096]{4,2,3,1,0:T(4,128)(2,1)S(1)} %pad_maximum_fusion, s32[1024]{0:T(1024)S(1)} %pad_clamp_fusion), kind=kCustom, calls=%fused_computation.4 | custom fusion | bytes 3145736 | tf_op jit(solution)/shard_map/jit(_take)/gather | solution.py:81
  59.3 3.2 %bitcast_reduce_fusion = (f32[2,4,4,6]{1,3,2,0:T(8,128)S(1)}, bf16[2,4,4,6,4096]{4,2,3,1,0:T(4,128)(2,1)S(1)}) fusion(bf16[2,4,4,6,4096]{4,2,3,1,0:T(4,128)(2,1)} %gather_fusion.2, pred[2]{0:T(512)(128)(4,1)S(1)} %compare_and_fusion.2), kind=kLoop, calls=%fused_computation.14 | loop fusion | flops 2359104 | bytes 3146498 | tf_op jit(solution)/shard_map/reduce_sum | solution.py:18
  63.7 2.1 fusion.10
  65.8 2.2 copy.43
  68.0 3.7 %convert_element_type.78 = bf16[192,4096]{1,0:T(8,128)(2,1)} reshape(bf16[2,4,4,6,4096]{4,3,2,1,0:T(8,128)(2,1)} %copy.43) | data formatting | bytes 3145728 | tf_op jit(solution)/shard_map/convert_element_type | solution.py:140
  71.7 2.2 copy.45
  73.9 2.8 %convert_element_type.84 = bf16[192,4096]{1,0:T(8,128)(2,1)S(1)} reshape(bf16[2,4,4,6,4096]{4,3,2,1,0:T(8,128)(2,1)} %copy.45) | data formatting | bytes 3145728 | tf_op jit(solution)/shard_map/convert_element_type | solution.py:141
  76.7 33.5 %all-gather.5.cloned.1.call-done = bf16[4096,896]{1,0:T(8,128)(2,1)} async-done(((bf16[256,896]{1,0:T(8,128)(2,1)}), bf16[4096,896]{1,0:T(8,128)(2,1)}) %all-gather.5.cloned.1.call-update) | async-done | bytes 7340048 | tf_op jit(solution)/shard_map/all_gather | solution.py:132
  110.2 2.3 slice.57
  112.5 2.7 %slice.65 = bf16[16,256,512]{2,1,0:T(8,128)(2,1)S(1)} slice(bf16[16,256,896]{2,1,0:T(8,128)(2,1)} %bitcast.63), slice={[0:16], [0:256], [384:896]} | slice | bytes 8388608 | tf_op jit(solution)/shard_map/slice | solution.py:138
  117.1 2.7 %fusion.84 = (f32[192]{0:T(256)S(1)}, f32[192,6144]{1,0:T(8,128)S(1)}) fusion(bf16[6144,128]{1,0:T(8,128)(2,1)S(1)} %copy-done, bf16[192,96]{0,1:T(8,128)(2,1)S(1)} %get-tuple-element.16, bf16[192,16]{0,1:T(8,128)(2,1)S(1)} %get-tuple-element.15, bf16[192,16]{0,1:T(8,128)(2,1)S(1)} %get-tuple-element.12, pred[6144]{0:T(1024)(128)(4,1)S(1)} %broadcast_compare_fusion, ...), kind=kOutput, calls=%fused_computation.166 | convolution fusion | flops 313933632 | bytes 6398208 | tf_op jit(solution)/shard_map/dot_general | solution.py:156
  122.2 1.8 fusion.30
  124.0 60.8 %all-gather.7.cloned.1.call-done = bf16[10240,256]{1,0:T(8,128)(2,1)} async-done(((bf16[640,256]{1,0:T(8,128)(2,1)}), bf16[10240,256]{1,0:T(8,128)(2,1)}) %all-gather.7.cloned.1.call-update) | async-done | bytes 5242896 | tf_op jit(solution)/shard_map/all_gather | solution.py:133
  184.9 3.9 %convolution_convert_fusion = bf16[192,16,256]{2,0,1:T(8,128)(2,1)S(1)} fusion(bf16[16,640,256]{2,1,0:T(8,128)(2,1)} %bitcast.64, bf16[192,512]{1,0:T(8,128)(2,1)S(1)} %fusion.30, bf16[192,128]{1,0:T(8,128)(2,1)S(1)} %fusion.25), kind=kOutput, calls=%fused_computation.29 | convolution fusion | flops 1007910912 | bytes 7061504 | tf_op jit(solution)/shard_map/dot_general | solution.py:174
  189.6 2.7 %convert_element_type.87 = bf16[2,16,6,4096]{3,2,1,0:T(8,128)(2,1)} reshape(bf16[192,16,256]{2,1,0:T(8,128)(2,1)S(1)} %copy.46) | data formatting | bytes 3145728 | tf_op jit(solution)/shard_map/convert_element_type | solution.py:177
  194.1 8.9 %collective-permute-start.7 = (bf16[16,6,4096]{2,0,1:T(8,128)(2,1)S(1)}, bf16[16,6,4096]{2,0,1:T(8,128)(2,1)S(1)}, u32[]{:S(2)}, u32[]{:S(2)}) collective-permute-start(bf16[16,6,4096]{2,0,1:T(8,128)(2,1)S(1)} %bitcast.67), channel_id=1, source_target_pairs={{0,1},{1,0},{2,3},{3,2},{4,5},{5,4},{6,7},{7,6},{8,9},{9,8},{10,11... | collective-permute-start | bytes 2359304 | tf_op jit(solution)/shard_map/ppermute | solution.py:181
  203.0 1.9 collective-permute-done.7
  204.9 1.8 fusion.17
  206.7 22.8 %all_to_all.5 = bf16[16,6,4096]{2,1,0:T(8,128)(2,1)S(1)} all-to-all(bf16[16,6,4096]{2,1,0:T(8,128)(2,1)S(1)} %fusion.17), channel_id=1, replica_groups={{0,2,4,6,8,10,12,14,16,18,20,22,24,26,28,30},{1,3,5,7,9,11,13,15,17,19,..., dimensions={0} | all-to-all | bytes 1572864 | tf_op jit(solution)/shard_map/all_to_all | solution.py:186
  (85 shorter events, 16.1 us)
Async XLA Ops:
  6.5 110.6 %copy-start = (bf16[6144,128]{1,0:T(8,128)(2,1)S(1)}, bf16[6144,128]{1,0:T(8,128)(2,1)}, u32[]{:S(2)}) copy-start(bf16[6144,128]{1,0:T(8,128)(2,1)} %param.32) | copy-start | bytes 4718596
  6.5 15.6 %copy-start.10 = (s32[192]{0:T(256)S(1)}, s32[192]{0:T(256)}, u32[]{:S(2)}) copy-start(s32[192]{0:T(256)} %constant.262) | copy-start | bytes 2308
  6.5 19.7 %copy-start.3 = (bf16[6,4096]{1,0:T(8,128)(2,1)S(1)}, bf16[6,4096]{1,0:T(8,128)(2,1)}, u32[]{:S(2)}) copy-start(bf16[6,4096]{1,0:T(8,128)(2,1)} %param.19) | copy-start | bytes 147460
  6.5 15.6 %copy-start.11 = (s32[1,33]{1,0:T(1,128)S(1)}, s32[1,33]{1,0:T(1,128)}, u32[]{:S(2)}) copy-start(s32[1,33]{1,0:T(1,128)} %param.34) | copy-start | bytes 400
  6.5 103.7 %all-gather.5.cloned.1.call-start = ((), (), s32[]{:S(2)}) async-start(), calls=%async_computation.1 | async-start | bytes 7798784 | tf_op jit(solution)/shard_map/all_gather | solution.py:132
  8.6 176.3 %all-gather.7.cloned.1.call-start = ((), (), s32[]{:S(2)}) async-start(), calls=%async_computation.2 | async-start | bytes 5570560 | tf_op jit(solution)/shard_map/all_gather | solution.py:133
  8.6 17.6 %collective-permute-start = (bf16[6,4096]{1,0:T(8,128)(2,1)}, bf16[6,4096]{1,0:T(8,128)(2,1)S(1)}, u32[]{:S(2)}, u32[]{:S(2)}) collective-permute-start(bf16[6,4096]{1,0:T(8,128)(2,1)} %param.19), channel_id=1, source_target_pairs={{0,8},{1,9},{2,10},{3,11},{4,12},{5,13},{6,14},{7,15},{8,16},{9,17... | collective-permute-start | bytes 147464 | tf_op jit(solution)/shard_map/ppermute | solution.py:78
  12.7 13.5 %collective-permute-start.1 = (bf16[6,4096]{1,0:T(8,128)(2,1)}, bf16[6,4096]{1,0:T(8,128)(2,1)S(1)}, u32[]{:S(2)}, u32[]{:S(2)}) collective-permute-start(bf16[6,4096]{1,0:T(8,128)(2,1)} %param.19), channel_id=1, source_target_pairs={{0,16},{1,17},{2,18},{3,19},{4,20},{5,21},{6,22},{7,23},{8,24},{9,... | collective-permute-start | bytes 147464 | tf_op jit(solution)/shard_map/ppermute | solution.py:78
  17.2 9.0 %collective-permute-start.2 = (bf16[6,4096]{1,0:T(8,128)(2,1)}, bf16[6,4096]{1,0:T(8,128)(2,1)S(1)}, u32[]{:S(2)}, u32[]{:S(2)}) collective-permute-start(bf16[6,4096]{1,0:T(8,128)(2,1)} %param.19), channel_id=1, source_target_pairs={{0,24},{1,25},{2,26},{3,27},{4,28},{5,29},{6,30},{7,31},{8,0},{9,1... | collective-permute-start | bytes 147464 | tf_op jit(solution)/shard_map/ppermute | solution.py:78
  27.0 10.1 %collective-permute-start.5 = (bf16[4,6,4096]{2,1,0:T(8,128)(2,1)S(1)}, bf16[4,6,4096]{2,1,0:T(8,128)(2,1)S(1)}, u32[]{:S(2)}, u32[]{:S(2)}) collective-permute-start(bf16[4,6,4096]{2,1,0:T(8,128)(2,1)S(1)} %broadcast_select_fusion.2), channel_id=1, source_target_pairs={{0,6},{1,7},{2,0},{3,1},{4,2},{5,3},{6,4},{7,5},{8,14},{9,15},{10,... | collective-permute-start | bytes 589832 | tf_op jit(solution)/shard_map/ppermute | solution.py:78
  31.4 10.0 %collective-permute-start.3 = (bf16[4,6,4096]{2,1,0:T(8,128)(2,1)S(1)}, bf16[4,6,4096]{2,1,0:T(8,128)(2,1)S(1)}, u32[]{:S(2)}, u32[]{:S(2)}) collective-permute-start(bf16[4,6,4096]{2,1,0:T(8,128)(2,1)S(1)} %broadcast_select_fusion.2), channel_id=1, source_target_pairs={{0,2},{1,3},{2,4},{3,5},{4,6},{5,7},{6,0},{7,1},{8,10},{9,11},{10,... | collective-permute-start | bytes 589832 | tf_op jit(solution)/shard_map/ppermute | solution.py:78
  33.3 11.9 %collective-permute-start.4 = (bf16[4,6,4096]{2,1,0:T(8,128)(2,1)S(1)}, bf16[4,6,4096]{2,1,0:T(8,128)(2,1)S(1)}, u32[]{:S(2)}, u32[]{:S(2)}) collective-permute-start(bf16[4,6,4096]{2,1,0:T(8,128)(2,1)S(1)} %broadcast_select_fusion.2), channel_id=1, source_target_pairs={{0,4},{1,5},{2,6},{3,7},{4,0},{5,1},{6,2},{7,3},{8,12},{9,13},{10,... | collective-permute-start | bytes 589832 | tf_op jit(solution)/shard_map/ppermute | solution.py:78
  47.7 7.4 %collective-permute-start.6 = (bf16[4,4,6,4096]{3,1,2,0:T(4,128)(2,1)S(1)}, bf16[4,4,6,4096]{3,1,2,0:T(4,128)(2,1)S(1)}, u32[]{:S(2)}, u32[]{:S(2)}) collective-permute-start(bf16[4,4,6,4096]{3,1,2,0:T(4,128)(2,1)S(1)} %broadcast_select_fusion.1), channel_id=1, source_target_pairs={{0,1},{1,0},{2,3},{3,2},{4,5},{5,4},{6,7},{7,6},{8,9},{9,8},{10,11... | collective-permute-start | bytes 2359304 | tf_op jit(solution)/shard_map/ppermute | solution.py:78
  59.3 4.4 %copy-start.4 = (f32[4096]{0:T(1024)S(1)}, f32[4096]{0:T(1024)}, u32[]{:S(2)}) copy-start(f32[4096]{0:T(1024)} %param.21) | copy-start | bytes 49156
  59.3 4.4 %copy-start.5 = (f32[4096]{0:T(1024)S(1)}, f32[4096]{0:T(1024)}, u32[]{:S(2)}) copy-start(f32[4096]{0:T(1024)} %param.20) | copy-start | bytes 49156
  59.3 4.4 %copy-start.6 = (f32[4096]{0:T(1024)S(1)}, f32[4096]{0:T(1024)}, u32[]{:S(2)}) copy-start(f32[4096]{0:T(1024)} %param.23) | copy-start | bytes 49156
  59.3 4.4 %copy-start.7 = (f32[4096]{0:T(1024)S(1)}, f32[4096]{0:T(1024)}, u32[]{:S(2)}) copy-start(f32[4096]{0:T(1024)} %param.22) | copy-start | bytes 49156
  112.5 2.8 %copy-start.1 = (bf16[192,4096]{1,0:T(8,128)(2,1)S(1)}, bf16[192,4096]{1,0:T(8,128)(2,1)}, u32[]{:S(2)}) copy-start(bf16[192,4096]{1,0:T(8,128)(2,1)} %convert_element_type.78) | copy-start | bytes 4718596
  112.5 2.8 %copy-start.12 = (f32[384]{0:T(512)S(1)}, f32[384]{0:T(512)}, u32[]{:S(2)}) copy-start(f32[384]{0:T(512)} %param.25) | copy-start | bytes 4612
  119.8 1.4 copy-start.2
  121.3 0.9 copy-start.13
  194.1 10.8 %collective-permute-start.7 = (bf16[16,6,4096]{2,0,1:T(8,128)(2,1)S(1)}, bf16[16,6,4096]{2,0,1:T(8,128)(2,1)S(1)}, u32[]{:S(2)}, u32[]{:S(2)}) collective-permute-start(bf16[16,6,4096]{2,0,1:T(8,128)(2,1)S(1)} %bitcast.67), channel_id=1, source_target_pairs={{0,1},{1,0},{2,3},{3,2},{4,5},{5,4},{6,7},{7,6},{8,9},{9,8},{10,11... | collective-permute-start | bytes 2359304 | tf_op jit(solution)/shard_map/ppermute | solution.py:181
  206.6 23.1 %copy-start.8 = (f32[4096]{0:T(1024)S(1)}, f32[4096]{0:T(1024)}, u32[]{:S(2)}) copy-start(f32[4096]{0:T(1024)} %param.31) | copy-start | bytes 49156
  206.7 23.1 %copy-start.9 = (f32[4096]{0:T(1024)S(1)}, f32[4096]{0:T(1024)}, u32[]{:S(2)}) copy-start(f32[4096]{0:T(1024)} %param.27) | copy-start | bytes 49156
Sparse Core Ops, SparseCore 0:
  9.5 100.7 all-gather.4
  112.3 72.5 all-gather.6

commit v9 on v8

--- a/solution.py
+++ b/solution.py
@@ -171,20 +171,21 @@
     attention = (summed / total[:, None]).astype(jnp.bfloat16)
     contract = (((1,), (1,)), ((), ()))
     mixed_in = jnp.concatenate([attention, hidden], axis=1)
-    partial = lax.dot_general(mixed_in, second, contract, preferred_element_type=jnp.float32)
-    partial = partial.reshape(rows_total, -1)
     heads = lax.axis_size("head")
-    blocks = partial.astype(jnp.bfloat16).reshape(2, heads // 2, tokens.shape[0], -1)
     core = lax.axis_index("head") % 2
-    mine = lax.dynamic_index_in_dim(blocks, core, 0, keepdims=False)
-    theirs = lax.dynamic_index_in_dim(blocks, 1 - core, 0, keepdims=False)
-    swapped = lax.ppermute(
-        theirs, "head", [(index, index ^ 1) for index in range(heads)]
-    )
-    chip_sum = (mine.astype(jnp.float32) + swapped.astype(jnp.float32)).astype(jnp.bfloat16)
     groups = [list(range(side, heads, 2)) for side in range(2)]
-    exchanged = lax.all_to_all(chip_sum, "head", 0, 0, axis_index_groups=groups, tiled=True)
-    partial_value = jnp.sum(exchanged.astype(jnp.float32), axis=0)
+    split = second.shape[0] // 2
+    halves = []
+    for pieces in (second[:split], second[split:]):
+        partial = lax.dot_general(mixed_in, pieces, contract, preferred_element_type=jnp.float32)
+        blocks = partial.astype(jnp.bfloat16).reshape(2, heads // 2, tokens.shape[0], -1)
+        mine = lax.dynamic_index_in_dim(blocks, core, 0, keepdims=False)
+        theirs = lax.dynamic_index_in_dim(blocks, 1 - core, 0, keepdims=False)
+        swapped = lax.ppermute(theirs, "head", [(index, index ^ 1) for index in range(heads)])
+        chip_sum = (mine.astype(jnp.float32) + swapped.astype(jnp.float32)).astype(jnp.bfloat16)
+        exchanged = lax.all_to_all(chip_sum, "head", 0, 0, axis_index_groups=groups, tiled=True)
+        halves.append(jnp.sum(exchanged.astype(jnp.float32), axis=0))
+    partial_value = jnp.concatenate(halves, axis=1)
     mixed = tokens.astype(jnp.float32) + partial_value + b_dense + b_down
     return mixed.astype(jnp.bfloat16)
 

time: 238 us -> 258 us (1.084)
  waiting for transfers between devices: 106 us -> 131 us
  blocking collectives: 22.8 us -> 0 us
  other arithmetic: 17.1 us -> 23.6 us
  starting transfers between devices: 36.2 us -> 42.2 us
  local copies, waits for them, and re-layouts: 30.3 us -> 36.1 us
    all_gather x1, waiting for transfers between devices: 33.5 us -> 94.7 us  [body(): lax.all_gather(jnp.concatenate([w_qkv, w_up], axis=1), 'tok', axis=0, til...]
    all_gather x1, waiting for transfers between devices: 60.8 us -> 8.27 us  [body(): lax.all_gather(jnp.concatenate([w_dense, w_down], axis=0), 'tok', axis=0,...]
    all_to_all x1 -> x0, blocking collectives: 22.8 us -> none  [body(): lax.all_to_all(chip_sum, 'head', 0, 0, axis_index_groups=groups, tiled=True)]
    all_to_all x0 -> x2, waiting for transfers between devices: none -> 18.2 us  [body(): lax.all_to_all(chip_sum, 'head', 0, 0, axis_index_groups=groups, tiled=True)]
    all_to_all x0 -> x2, starting transfers between devices: none -> 10.2 us  [body(): lax.all_to_all(chip_sum, 'head', 0, 0, axis_index_groups=groups, tiled=True)]
    slice x0 -> x1, local copies, waits for them, and re-layouts: none -> 5.22 us  [body(): second[:split]]
    ppermute x1 -> x2, starting transfers between devices: 8.9 us -> 4.74 us  [body(): lax.ppermute(theirs, 'head', [(index, index ^ 1) for index in range(heads)])]
    convert_element_type x2, local copies, waits for them, and re-layouts: 3.6 us -> 0.87 us  [body(): partial.astype(jnp.bfloat16).reshape(2, heads // 2, tokens.shape[0], -1)]
  transfers between devices with their start and end apart: 10 -> 13, of which waited for: 6 -> 7; matrix products, arithmetic and copies ran while one was open for 19% -> 19% of each run, Pallas kernels for 0% -> 0%
where the time goes in v9:
time: 258 us; the launch traced here: 256 us
  waiting for transfers between devices  131 us (51%)
  starting transfers between devices  42.2 us (16%)
  local copies, waits for them, and re-layouts  36.1 us (14%)
  other arithmetic  23.6 us (9%)
  between operations  14.2 us (6%)
  matrix products  9.69 us (4%)
    all_gather x1, waiting for transfers between devices, body(): lax.all_gather(jnp.concatenate([w_qkv, w_up], axis=1), 'tok', axis=0, til...  94.7 us
    ppermute x7, starting transfers between devices, gather_stage(): lax.ppermute(stacked, 'head', stage_pairs(size, stride, shift, total))  27.2 us
    all_to_all x2, waiting for transfers between devices, body(): lax.all_to_all(chip_sum, 'head', 0, 0, axis_index_groups=groups, tiled=True)  18.2 us
    all_to_all x2, starting transfers between devices, body(): lax.all_to_all(chip_sum, 'head', 0, 0, axis_index_groups=groups, tiled=True)  10.2 us
    ppermute x7, waiting for transfers between devices, gather_stage(): lax.ppermute(stacked, 'head', stage_pairs(size, stride, shift, total))  9.45 us
    all_gather x1, waiting for transfers between devices, body(): lax.all_gather(jnp.concatenate([w_dense, w_down], axis=0), 'tok', axis=0,...  8.27 us
    convert_element_type x2, local copies, waits for them, and re-layouts, body(): normed_one = layer_norm(whole, ln1_gain, ln1_bias).astype(jnp.bfloat16)  5.9 us
    slice x1, local copies, waits for them, and re-layouts, body(): second[:split]  5.22 us
  transfers between devices with their start and end apart: 13, of which 7 were waited for; matrix products, arithmetic and copies ran while one was open for 19% of the time, Pallas kernels for 0%

profile of v9, /device:TPU:1, one launch (start us, length us, event | category | flops | bytes accessed | tf_op | source)
XLA Modules:
  0.0 256.4 jit_solution(5111725670475157188)
XLA Ops:
  8.4 1.8 pad_maximum_fusion.2
  10.3 4.0 %collective-permute-start = (bf16[6,4096]{1,0:T(8,128)(2,1)}, bf16[6,4096]{1,0:T(8,128)(2,1)S(1)}, u32[]{:S(2)}, u32[]{:S(2)}) collective-permute-start(bf16[6,4096]{1,0:T(8,128)(2,1)} %param.19), channel_id=1, source_target_pairs={{0,8},{1,9},{2,10},{3,11},{4,12},{5,13},{6,14},{7,15},{8,16},{9,17... | collective-permute-start | bytes 147464 | tf_op jit(solution)/shard_map/ppermute | solution.py:78
  14.3 4.5 %collective-permute-start.1 = (bf16[6,4096]{1,0:T(8,128)(2,1)}, bf16[6,4096]{1,0:T(8,128)(2,1)S(1)}, u32[]{:S(2)}, u32[]{:S(2)}) collective-permute-start(bf16[6,4096]{1,0:T(8,128)(2,1)} %param.19), channel_id=1, source_target_pairs={{0,16},{1,17},{2,18},{3,19},{4,20},{5,21},{6,22},{7,23},{8,24},{9,... | collective-permute-start | bytes 147464 | tf_op jit(solution)/shard_map/ppermute | solution.py:78
  18.9 3.0 %collective-permute-start.2 = (bf16[6,4096]{1,0:T(8,128)(2,1)}, bf16[6,4096]{1,0:T(8,128)(2,1)S(1)}, u32[]{:S(2)}, u32[]{:S(2)}) collective-permute-start(bf16[6,4096]{1,0:T(8,128)(2,1)} %param.19), channel_id=1, source_target_pairs={{0,24},{1,25},{2,26},{3,27},{4,28},{5,29},{6,30},{7,31},{8,0},{9,1... | collective-permute-start | bytes 147464 | tf_op jit(solution)/shard_map/ppermute | solution.py:78
  28.7 2.2 gather_fusion.3
  31.6 4.4 %collective-permute-start.5 = (bf16[4,6,4096]{2,1,0:T(8,128)(2,1)S(1)}, bf16[4,6,4096]{2,1,0:T(8,128)(2,1)S(1)}, u32[]{:S(2)}, u32[]{:S(2)}) collective-permute-start(bf16[4,6,4096]{2,1,0:T(8,128)(2,1)S(1)} %broadcast_select_fusion.2), channel_id=1, source_target_pairs={{0,6},{1,7},{2,0},{3,1},{4,2},{5,3},{6,4},{7,5},{8,14},{9,15},{10,... | collective-permute-start | bytes 589832 | tf_op jit(solution)/shard_map/ppermute | solution.py:78
  36.0 1.9 collective-permute-start.3
  37.9 3.6 %collective-permute-start.4 = (bf16[4,6,4096]{2,1,0:T(8,128)(2,1)S(1)}, bf16[4,6,4096]{2,1,0:T(8,128)(2,1)S(1)}, u32[]{:S(2)}, u32[]{:S(2)}) collective-permute-start(bf16[4,6,4096]{2,1,0:T(8,128)(2,1)S(1)} %broadcast_select_fusion.2), channel_id=1, source_target_pairs={{0,4},{1,5},{2,6},{3,7},{4,0},{5,1},{6,2},{7,3},{8,12},{9,13},{10,... | collective-permute-start | bytes 589832 | tf_op jit(solution)/shard_map/ppermute | solution.py:78
  41.7 4.3 %collective-permute-done.3 = bf16[4,6,4096]{2,1,0:T(8,128)(2,1)S(1)} collective-permute-done((bf16[4,6,4096]{2,1,0:T(8,128)(2,1)S(1)}, bf16[4,6,4096]{2,1,0:T(8,128)(2,1)S(1)}, u32[]{:S(2)}, u32[]{:S(2)}) %collective-permute-start.3) | collective-permute-done | bytes 196640 | tf_op jit(solution)/shard_map/ppermute | solution.py:78
  46.0 3.8 %collective-permute-done.4 = bf16[4,6,4096]{2,1,0:T(8,128)(2,1)S(1)} collective-permute-done((bf16[4,6,4096]{2,1,0:T(8,128)(2,1)S(1)}, bf16[4,6,4096]{2,1,0:T(8,128)(2,1)S(1)}, u32[]{:S(2)}, u32[]{:S(2)}) %collective-permute-start.4) | collective-permute-done | bytes 196640 | tf_op jit(solution)/shard_map/ppermute | solution.py:78
  52.4 5.7 %collective-permute-start.6 = (bf16[4,4,6,4096]{3,1,2,0:T(4,128)(2,1)S(1)}, bf16[4,4,6,4096]{3,1,2,0:T(4,128)(2,1)S(1)}, u32[]{:S(2)}, u32[]{:S(2)}) collective-permute-start(bf16[4,4,6,4096]{3,1,2,0:T(4,128)(2,1)S(1)} %broadcast_select_fusion.1), channel_id=1, source_target_pairs={{0,1},{1,0},{2,3},{3,2},{4,5},{5,4},{6,7},{7,6},{8,9},{9,8},{10,11... | collective-permute-start | bytes 2359304 | tf_op jit(solution)/shard_map/ppermute | solution.py:78
  60.9 3.0 %gather_fusion.2 = bf16[2,4,4,6,4096]{4,2,3,1,0:T(4,128)(2,1)} fusion(bf16[2,4,4,6,4096]{4,2,3,1,0:T(4,128)(2,1)S(1)} %pad_maximum_fusion, s32[1024]{0:T(1024)S(1)} %pad_clamp_fusion), kind=kCustom, calls=%fused_computation.4 | custom fusion | bytes 3145736 | tf_op jit(solution)/shard_map/jit(_take)/gather | solution.py:81
  63.9 3.2 %bitcast_reduce_fusion = (f32[2,4,4,6]{1,3,2,0:T(8,128)S(1)}, bf16[2,4,4,6,4096]{4,2,3,1,0:T(4,128)(2,1)S(1)}) fusion(bf16[2,4,4,6,4096]{4,2,3,1,0:T(4,128)(2,1)} %gather_fusion.2, pred[2]{0:T(512)(128)(4,1)S(1)} %compare_and_fusion.2), kind=kLoop, calls=%fused_computation.14 | loop fusion | flops 2359104 | bytes 3146498 | tf_op jit(solution)/shard_map/reduce_sum | solution.py:18
  68.3 2.1 fusion.10
  70.4 2.2 copy.41
  72.6 3.7 %convert_element_type.92 = bf16[192,4096]{1,0:T(8,128)(2,1)} reshape(bf16[2,4,4,6,4096]{4,3,2,1,0:T(8,128)(2,1)} %copy.41) | data formatting | bytes 3145728 | tf_op jit(solution)/shard_map/convert_element_type | solution.py:140
  76.3 2.2 copy.43
  78.5 2.8 %convert_element_type.98 = bf16[192,4096]{1,0:T(8,128)(2,1)S(1)} reshape(bf16[2,4,4,6,4096]{4,3,2,1,0:T(8,128)(2,1)} %copy.43) | data formatting | bytes 3145728 | tf_op jit(solution)/shard_map/convert_element_type | solution.py:141
  81.3 8.3 %all-gather.7.cloned.1.call-done = bf16[10240,256]{1,0:T(8,128)(2,1)} async-done(((bf16[640,256]{1,0:T(8,128)(2,1)}), bf16[10240,256]{1,0:T(8,128)(2,1)}) %all-gather.7.cloned.1.call-update) | async-done | bytes 5242896 | tf_op jit(solution)/shard_map/all_gather | solution.py:133
  89.6 5.2 %fusion.85 = (bf16[5120,256]{1,0:T(8,128)(2,1)}, bf16[5120,256]{1,0:T(8,128)(2,1)}) fusion(bf16[10240,256]{1,0:T(8,128)(2,1)} %all-gather.7.cloned.1.call-done), kind=kLoop, calls=%fused_computation.170 | loop fusion | bytes 10485760 | tf_op jit(solution)/shard_map/slice | solution.py:179
  94.8 94.7 %all-gather.5.cloned.1.call-done = bf16[4096,896]{1,0:T(8,128)(2,1)} async-done(((bf16[256,896]{1,0:T(8,128)(2,1)}), bf16[4096,896]{1,0:T(8,128)(2,1)}) %all-gather.5.cloned.1.call-update) | async-done | bytes 7340048 | tf_op jit(solution)/shard_map/all_gather | solution.py:132
  189.5 2.4 slice.67
  193.6 2.7 %fusion.88 = (f32[192]{0:T(256)S(1)}, f32[192,6144]{1,0:T(8,128)S(1)}) fusion(bf16[6144,128]{1,0:T(8,128)(2,1)S(1)} %copy-done, bf16[192,96]{0,1:T(8,128)(2,1)S(1)} %get-tuple-element.18, bf16[192,16]{0,1:T(8,128)(2,1)S(1)} %get-tuple-element.17, bf16[192,16]{0,1:T(8,128)(2,1)S(1)} %get-tuple-element.14, pred[6144]{0:T(1024)(128)(4,1)S(1)} %broadcast_compare_fusion, ...), kind=kOutput, calls=%fused_computation.173 | convolution fusion | flops 313933632 | bytes 6398208 | tf_op jit(solution)/shard_map/dot_general | solution.py:156
  204.6 1.9 dynamic-slice_bitcast_fusion.1
  206.5 2.8 %collective-permute-start.7 = (bf16[16,6,2048]{2,1,0:T(8,128)(2,1)}, bf16[16,6,2048]{2,1,0:T(8,128)(2,1)}, u32[]{:S(2)}, u32[]{:S(2)}) collective-permute-start(bf16[16,6,2048]{2,1,0:T(8,128)(2,1)} %dynamic-slice_bitcast_fusion.1), channel_id=1, source_target_pairs={{0,1},{1,0},{2,3},{3,2},{4,5},{5,4},{6,7},{7,6},{8,9},{9,8},{10,11... | collective-permute-start | bytes 1179656 | tf_op jit(solution)/shard_map/ppermute | solution.py:184
  214.2 1.9 collective-permute-start.8
  216.1 2.1 fusion.28
  218.2 6.7 %all-to-all-start = ((bf16[16,6,2048]{2,1,0:T(8,128)(2,1)}), bf16[16,6,2048]{2,1,0:T(8,128)(2,1)S(1)}, u32[]{:S(2)}, u32[]{:S(2)}) async-start(bf16[16,6,2048]{2,1,0:T(8,128)(2,1)} %fusion.28), calls=%async_computation | async-start | bytes 1048576 | tf_op jit(solution)/shard_map/all_to_all | solution.py:186
  224.9 2.0 fusion.27
  226.9 8.6 %all-to-all-done = bf16[16,6,2048]{2,1,0:T(8,128)(2,1)S(1)} async-done(((bf16[16,6,2048]{2,1,0:T(8,128)(2,1)}), bf16[16,6,2048]{2,1,0:T(8,128)(2,1)S(1)}, u32[]{:S(2)}, u32[]{:S(2)}) %all-to-all-start) | async-done | bytes 393248 | tf_op jit(solution)/shard_map/all_to_all | solution.py:186
  235.4 3.6 %all-to-all-start.1 = ((bf16[16,6,2048]{2,1,0:T(8,128)(2,1)}), bf16[16,6,2048]{2,1,0:T(8,128)(2,1)S(1)}, u32[]{:S(2)}, u32[]{:S(2)}) async-start(bf16[16,6,2048]{2,1,0:T(8,128)(2,1)} %fusion.27), calls=%async_computation.1 | async-start | bytes 1048576 | tf_op jit(solution)/shard_map/all_to_all | solution.py:186
  239.1 9.6 %all-to-all-done.1 = bf16[16,6,2048]{2,1,0:T(8,128)(2,1)S(1)} async-done(((bf16[16,6,2048]{2,1,0:T(8,128)(2,1)}), bf16[16,6,2048]{2,1,0:T(8,128)(2,1)S(1)}, u32[]{:S(2)}, u32[]{:S(2)}) %all-to-all-start.1) | async-done | bytes 393248 | tf_op jit(solution)/shard_map/all_to_all | solution.py:186
  (125 shorter events, 31.4 us)
Async XLA Ops:
  6.5 187.0 %copy-start = (bf16[6144,128]{1,0:T(8,128)(2,1)S(1)}, bf16[6144,128]{1,0:T(8,128)(2,1)}, u32[]{:S(2)}) copy-start(bf16[6144,128]{1,0:T(8,128)(2,1)} %param.32) | copy-start | bytes 4718596
  6.5 24.3 %copy-start.9 = (bf16[6,4096]{1,0:T(8,128)(2,1)S(1)}, bf16[6,4096]{1,0:T(8,128)(2,1)}, u32[]{:S(2)}) copy-start(bf16[6,4096]{1,0:T(8,128)(2,1)} %param.19) | copy-start | bytes 147460
  6.5 19.4 %copy-start.22 = (s32[1,33]{1,0:T(1,128)S(1)}, s32[1,33]{1,0:T(1,128)}, u32[]{:S(2)}) copy-start(s32[1,33]{1,0:T(1,128)} %param.34) | copy-start | bytes 400
  6.5 83.0 %all-gather.7.cloned.1.call-start = ((), (), s32[]{:S(2)}) async-start(), calls=%async_computation.3 | async-start | bytes 5570560 | tf_op jit(solution)/shard_map/all_gather | solution.py:133
  8.4 181.1 %all-gather.5.cloned.1.call-start = ((), (), s32[]{:S(2)}) async-start(), calls=%async_computation.2 | async-start | bytes 7798784 | tf_op jit(solution)/shard_map/all_gather | solution.py:132
  10.3 20.6 %collective-permute-start = (bf16[6,4096]{1,0:T(8,128)(2,1)}, bf16[6,4096]{1,0:T(8,128)(2,1)S(1)}, u32[]{:S(2)}, u32[]{:S(2)}) collective-permute-start(bf16[6,4096]{1,0:T(8,128)(2,1)} %param.19), channel_id=1, source_target_pairs={{0,8},{1,9},{2,10},{3,11},{4,12},{5,13},{6,14},{7,15},{8,16},{9,17... | collective-permute-start | bytes 147464 | tf_op jit(solution)/shard_map/ppermute | solution.py:78
  14.3 16.5 %collective-permute-start.1 = (bf16[6,4096]{1,0:T(8,128)(2,1)}, bf16[6,4096]{1,0:T(8,128)(2,1)S(1)}, u32[]{:S(2)}, u32[]{:S(2)}) collective-permute-start(bf16[6,4096]{1,0:T(8,128)(2,1)} %param.19), channel_id=1, source_target_pairs={{0,16},{1,17},{2,18},{3,19},{4,20},{5,21},{6,22},{7,23},{8,24},{9,... | collective-permute-start | bytes 147464 | tf_op jit(solution)/shard_map/ppermute | solution.py:78
  18.9 12.0 %collective-permute-start.2 = (bf16[6,4096]{1,0:T(8,128)(2,1)}, bf16[6,4096]{1,0:T(8,128)(2,1)S(1)}, u32[]{:S(2)}, u32[]{:S(2)}) collective-permute-start(bf16[6,4096]{1,0:T(8,128)(2,1)} %param.19), channel_id=1, source_target_pairs={{0,24},{1,25},{2,26},{3,27},{4,28},{5,29},{6,30},{7,31},{8,0},{9,1... | collective-permute-start | bytes 147464 | tf_op jit(solution)/shard_map/ppermute | solution.py:78
  25.8 24.3 %copy-start.18 = (s32[192]{0:T(256)}, s32[192]{0:T(256)S(1)}, u32[]{:S(2)}) copy-start(s32[192]{0:T(256)S(1)} %gather_fusion.4) | copy-start | bytes 2308
  31.6 10.1 %collective-permute-start.5 = (bf16[4,6,4096]{2,1,0:T(8,128)(2,1)S(1)}, bf16[4,6,4096]{2,1,0:T(8,128)(2,1)S(1)}, u32[]{:S(2)}, u32[]{:S(2)}) collective-permute-start(bf16[4,6,4096]{2,1,0:T(8,128)(2,1)S(1)} %broadcast_select_fusion.2), channel_id=1, source_target_pairs={{0,6},{1,7},{2,0},{3,1},{4,2},{5,3},{6,4},{7,5},{8,14},{9,15},{10,... | collective-permute-start | bytes 589832 | tf_op jit(solution)/shard_map/ppermute | solution.py:78
  36.0 10.0 %collective-permute-start.3 = (bf16[4,6,4096]{2,1,0:T(8,128)(2,1)S(1)}, bf16[4,6,4096]{2,1,0:T(8,128)(2,1)S(1)}, u32[]{:S(2)}, u32[]{:S(2)}) collective-permute-start(bf16[4,6,4096]{2,1,0:T(8,128)(2,1)S(1)} %broadcast_select_fusion.2), channel_id=1, source_target_pairs={{0,2},{1,3},{2,4},{3,5},{4,6},{5,7},{6,0},{7,1},{8,10},{9,11},{10,... | collective-permute-start | bytes 589832 | tf_op jit(solution)/shard_map/ppermute | solution.py:78
  37.9 11.9 %collective-permute-start.4 = (bf16[4,6,4096]{2,1,0:T(8,128)(2,1)S(1)}, bf16[4,6,4096]{2,1,0:T(8,128)(2,1)S(1)}, u32[]{:S(2)}, u32[]{:S(2)}) collective-permute-start(bf16[4,6,4096]{2,1,0:T(8,128)(2,1)S(1)} %broadcast_select_fusion.2), channel_id=1, source_target_pairs={{0,4},{1,5},{2,6},{3,7},{4,0},{5,1},{6,2},{7,3},{8,12},{9,13},{10,... | collective-permute-start | bytes 589832 | tf_op jit(solution)/shard_map/ppermute | solution.py:78
  52.4 7.4 %collective-permute-start.6 = (bf16[4,4,6,4096]{3,1,2,0:T(4,128)(2,1)S(1)}, bf16[4,4,6,4096]{3,1,2,0:T(4,128)(2,1)S(1)}, u32[]{:S(2)}, u32[]{:S(2)}) collective-permute-start(bf16[4,4,6,4096]{3,1,2,0:T(4,128)(2,1)S(1)} %broadcast_select_fusion.1), channel_id=1, source_target_pairs={{0,1},{1,0},{2,3},{3,2},{4,5},{5,4},{6,7},{7,6},{8,9},{9,8},{10,11... | collective-permute-start | bytes 2359304 | tf_op jit(solution)/shard_map/ppermute | solution.py:78
  63.9 4.4 %copy-start.11 = (f32[4096]{0:T(1024)S(1)}, f32[4096]{0:T(1024)}, u32[]{:S(2)}) copy-start(f32[4096]{0:T(1024)} %param.21) | copy-start | bytes 49156
  63.9 4.4 %copy-start.12 = (f32[4096]{0:T(1024)S(1)}, f32[4096]{0:T(1024)}, u32[]{:S(2)}) copy-start(f32[4096]{0:T(1024)} %param.20) | copy-start | bytes 49156
  63.9 4.4 %copy-start.13 = (f32[4096]{0:T(1024)S(1)}, f32[4096]{0:T(1024)}, u32[]{:S(2)}) copy-start(f32[4096]{0:T(1024)} %param.23) | copy-start | bytes 49156
  63.9 4.4 %copy-start.14 = (f32[4096]{0:T(1024)S(1)}, f32[4096]{0:T(1024)}, u32[]{:S(2)}) copy-start(f32[4096]{0:T(1024)} %param.22) | copy-start | bytes 49156
  189.5 2.4 copy-start.6
  189.5 2.4 copy-start.23
  193.5 3.3 %slice-start = ((s8[7340032]{0:T(1024)(128)(4,1)}), s8[4194304]{0:T(1024)(128)(4,1)S(1)}, s32[]{:S(2)}) async-start(s8[7340032]{0:T(1024)(128)(4,1)} %bitcast.72), calls=%async_computation.4 | async-start | bytes 8388608
  193.6 2.7 %copy-start.25 = (pred[192]{0:T(512)(128)(4,1)S(1)}, pred[192]{0:T(512)(128)(4,1)}, u32[]{:S(2)}) copy-start(pred[192]{0:T(512)(128)(4,1)} %broadcast_compare_fusion.1) | copy-start | bytes 580
  193.6 3.2 %slice-start.1 = ((s8[7340032]{0:T(1024)(128)(4,1)}), s8[3145728]{0:T(1024)(128)(4,1)S(1)}, s32[]{:S(2)}) async-start(s8[7340032]{0:T(1024)(128)(4,1)} %bitcast.72), calls=%async_computation.5 | async-start | bytes 6291456
  199.7 1.8 copy-start.3
  202.3 7.0 %copy-start.2 = (bf16[5120,256]{1,0:T(8,128)(2,1)S(1)}, bf16[5120,256]{1,0:T(8,128)(2,1)}, u32[]{:S(2)}) copy-start(bf16[5120,256]{1,0:T(8,128)(2,1)} %get-tuple-element.11) | copy-start | bytes 7864324
  206.5 9.6 %collective-permute-start.7 = (bf16[16,6,2048]{2,1,0:T(8,128)(2,1)}, bf16[16,6,2048]{2,1,0:T(8,128)(2,1)}, u32[]{:S(2)}, u32[]{:S(2)}) collective-permute-start(bf16[16,6,2048]{2,1,0:T(8,128)(2,1)} %dynamic-slice_bitcast_fusion.1), channel_id=1, source_target_pairs={{0,1},{1,0},{2,3},{3,2},{4,5},{5,4},{6,7},{7,6},{8,9},{9,8},{10,11... | collective-permute-start | bytes 1179656 | tf_op jit(solution)/shard_map/ppermute | solution.py:184
  211.0 5.0 %copy-start.4 = (bf16[2,16,6,2048]{3,2,1,0:T(8,128)(2,1)S(1)}, bf16[2,16,6,2048]{3,2,1,0:T(8,128)(2,1)}, u32[]{:S(2)}) copy-start(bf16[2,16,6,2048]{3,2,1,0:T(8,128)(2,1)} %reshape.324) | copy-start | bytes 2359300
  214.2 10.7 %collective-permute-start.8 = (bf16[16,6,2048]{2,1,0:T(8,128)(2,1)}, bf16[16,6,2048]{2,1,0:T(8,128)(2,1)S(1)}, u32[]{:S(2)}, u32[]{:S(2)}) collective-permute-start(bf16[16,6,2048]{2,1,0:T(8,128)(2,1)} %dynamic-slice_bitcast_fusion), channel_id=1, source_target_pairs={{0,1},{1,0},{2,3},{3,2},{4,5},{5,4},{6,7},{7,6},{8,9},{9,8},{10,11... | collective-permute-start | bytes 1179656 | tf_op jit(solution)/shard_map/ppermute | solution.py:184
  216.1 33.5 %copy-start.1 = (bf16[6144,128]{1,0:T(8,128)(2,1)S(1)}, bf16[6144,128]{1,0:T(8,128)(2,1)}, u32[]{:S(2)}) copy-start(bf16[6144,128]{1,0:T(8,128)(2,1)} %param.32) | copy-start | bytes 4718596
  218.2 30.7 %copy-start.15 = (f32[4096]{0:T(1024)S(1)}, f32[4096]{0:T(1024)}, u32[]{:S(2)}) copy-start(f32[4096]{0:T(1024)} %param.31) | copy-start | bytes 49156
  218.2 30.7 %copy-start.16 = (f32[4096]{0:T(1024)S(1)}, f32[4096]{0:T(1024)}, u32[]{:S(2)}) copy-start(f32[4096]{0:T(1024)} %param.27) | copy-start | bytes 49156
  218.2 17.2 %all-to-all-start = ((bf16[16,6,2048]{2,1,0:T(8,128)(2,1)}), bf16[16,6,2048]{2,1,0:T(8,128)(2,1)S(1)}, u32[]{:S(2)}, u32[]{:S(2)}) async-start(bf16[16,6,2048]{2,1,0:T(8,128)(2,1)} %fusion.28), calls=%async_computation | async-start | bytes 1048576 | tf_op jit(solution)/shard_map/all_to_all | solution.py:186
  235.4 13.3 %all-to-all-start.1 = ((bf16[16,6,2048]{2,1,0:T(8,128)(2,1)}), bf16[16,6,2048]{2,1,0:T(8,128)(2,1)S(1)}, u32[]{:S(2)}, u32[]{:S(2)}) async-start(bf16[16,6,2048]{2,1,0:T(8,128)(2,1)} %fusion.27), calls=%async_computation.1 | async-start | bytes 1048576 | tf_op jit(solution)/shard_map/all_to_all | solution.py:186
  (9 other events, 11.9 us)
Sparse Core Ops, SparseCore 0:
  9.4 80.0 all-gather.6
  91.6 97.7 all-gather.4

commit v10 on v8

--- a/solution.py
+++ b/solution.py
@@ -171,16 +171,19 @@
     attention = (summed / total[:, None]).astype(jnp.bfloat16)
     contract = (((1,), (1,)), ((), ()))
     mixed_in = jnp.concatenate([attention, hidden], axis=1)
-    partial = lax.dot_general(mixed_in, second, contract, preferred_element_type=jnp.float32)
-    partial = partial.reshape(rows_total, -1)
     heads = lax.axis_size("head")
-    blocks = partial.astype(jnp.bfloat16).reshape(2, heads // 2, tokens.shape[0], -1)
     core = lax.axis_index("head") % 2
-    mine = lax.dynamic_index_in_dim(blocks, core, 0, keepdims=False)
-    theirs = lax.dynamic_index_in_dim(blocks, 1 - core, 0, keepdims=False)
+    share = mixed_in.shape[0] // 2
+
+    def output_rows(side):
+        rows = lax.dynamic_slice_in_dim(mixed_in, side * share, share, 0)
+        partial = lax.dot_general(rows, second, contract, preferred_element_type=jnp.float32)
+        return partial.astype(jnp.bfloat16).reshape(heads // 2, tokens.shape[0], -1)
+
     swapped = lax.ppermute(
-        theirs, "head", [(index, index ^ 1) for index in range(heads)]
-    )
+        output_rows(1 - core), "head", [(index, index ^ 1) for index in range(heads)]
+    )
+    mine = output_rows(core)
     chip_sum = (mine.astype(jnp.float32) + swapped.astype(jnp.float32)).astype(jnp.bfloat16)
     groups = [list(range(side, heads, 2)) for side in range(2)]
     exchanged = lax.all_to_all(chip_sum, "head", 0, 0, axis_index_groups=groups, tiled=True)

time: 238 us -> 241 us (1.013)
  waiting for transfers between devices: 106 us -> 101 us
  matrix products: 11.2 us -> 14.4 us
  other arithmetic: 17.1 us -> 19.9 us
    dot_general x1 -> x2, matrix products: 3.88 us -> 7.1 us  [output_rows(): lax.dot_general(rows, second, contract, preferred_element_type=jnp.float32)]
    all_gather x1, waiting for transfers between devices: 33.5 us -> 30.7 us  [body(): lax.all_gather(jnp.concatenate([w_qkv, w_up], axis=1), 'tok', axis=0, til...]
  transfers between devices with their start and end apart: 10 -> 10, of which waited for: 6 -> 5; matrix products, arithmetic and copies ran while one was open for 19% -> 22% of each run, Pallas kernels for 0% -> 0%
where the time goes in v10:
time: 241 us; the launch traced here: 240 us
  waiting for transfers between devices  101 us (42%)
  starting transfers between devices  36.4 us (15%)
  local copies, waits for them, and re-layouts  30.9 us (13%)
  blocking collectives  23.2 us (10%)
  other arithmetic  19.9 us (8%)
  matrix products  14.4 us (6%)
  between operations  14.1 us (6%)
    all_gather x1, waiting for transfers between devices, body(): lax.all_gather(jnp.concatenate([w_dense, w_down], axis=0), 'tok', axis=0,...  60.7 us
    all_gather x1, waiting for transfers between devices, body(): lax.all_gather(jnp.concatenate([w_qkv, w_up], axis=1), 'tok', axis=0, til...  30.7 us
    ppermute x7, starting transfers between devices, gather_stage(): lax.ppermute(stacked, 'head', stage_pairs(size, stride, shift, total))  27.2 us
    all_to_all x1, blocking collectives, body(): lax.all_to_all(chip_sum, 'head', 0, 0, axis_index_groups=groups, tiled=True)  23.2 us
    ppermute x7, waiting for transfers between devices, gather_stage(): lax.ppermute(stacked, 'head', stage_pairs(size, stride, shift, total))  9.45 us
    ppermute x1, starting transfers between devices, body(): lax.ppermute(output_rows(1 - core), 'head', [(index, index ^ 1) for index...  9.14 us
    dot_general x2, matrix products, output_rows(): lax.dot_general(rows, second, contract, preferred_element_type=jnp.float32)  7.1 us
    convert_element_type x2, local copies, waits for them, and re-layouts, body(): normed_one = layer_norm(whole, ln1_gain, ln1_bias).astype(jnp.bfloat16)  5.92 us
  transfers between devices with their start and end apart: 10, of which 5 were waited for; matrix products, arithmetic and copies ran while one was open for 22% of the time, Pallas kernels for 0%

profile of v10, /device:TPU:1, one launch (start us, length us, event | category | flops | bytes accessed | tf_op | source)
XLA Modules:
  0.0 239.8 jit_solution(12721192860464098700)
XLA Ops:
  6.6 2.0 pad_maximum_fusion.2
  8.6 4.0 %collective-permute-start = (bf16[6,4096]{1,0:T(8,128)(2,1)}, bf16[6,4096]{1,0:T(8,128)(2,1)S(1)}, u32[]{:S(2)}, u32[]{:S(2)}) collective-permute-start(bf16[6,4096]{1,0:T(8,128)(2,1)} %param.19), channel_id=1, source_target_pairs={{0,8},{1,9},{2,10},{3,11},{4,12},{5,13},{6,14},{7,15},{8,16},{9,17... | collective-permute-start | bytes 147464 | tf_op jit(solution)/shard_map/ppermute | solution.py:78
  12.7 4.5 %collective-permute-start.1 = (bf16[6,4096]{1,0:T(8,128)(2,1)}, bf16[6,4096]{1,0:T(8,128)(2,1)S(1)}, u32[]{:S(2)}, u32[]{:S(2)}) collective-permute-start(bf16[6,4096]{1,0:T(8,128)(2,1)} %param.19), channel_id=1, source_target_pairs={{0,16},{1,17},{2,18},{3,19},{4,20},{5,21},{6,22},{7,23},{8,24},{9,... | collective-permute-start | bytes 147464 | tf_op jit(solution)/shard_map/ppermute | solution.py:78
  17.2 3.0 %collective-permute-start.2 = (bf16[6,4096]{1,0:T(8,128)(2,1)}, bf16[6,4096]{1,0:T(8,128)(2,1)S(1)}, u32[]{:S(2)}, u32[]{:S(2)}) collective-permute-start(bf16[6,4096]{1,0:T(8,128)(2,1)} %param.19), channel_id=1, source_target_pairs={{0,24},{1,25},{2,26},{3,27},{4,28},{5,29},{6,30},{7,31},{8,0},{9,1... | collective-permute-start | bytes 147464 | tf_op jit(solution)/shard_map/ppermute | solution.py:78
  20.2 1.7 pad_maximum_fusion.3
  23.5 1.6 gather_fusion.4
  26.9 2.2 gather_fusion.3
  29.8 4.4 %collective-permute-start.5 = (bf16[4,6,4096]{2,1,0:T(8,128)(2,1)S(1)}, bf16[4,6,4096]{2,1,0:T(8,128)(2,1)S(1)}, u32[]{:S(2)}, u32[]{:S(2)}) collective-permute-start(bf16[4,6,4096]{2,1,0:T(8,128)(2,1)S(1)} %broadcast_select_fusion.2), channel_id=1, source_target_pairs={{0,6},{1,7},{2,0},{3,1},{4,2},{5,3},{6,4},{7,5},{8,14},{9,15},{10,... | collective-permute-start | bytes 589832 | tf_op jit(solution)/shard_map/ppermute | solution.py:78
  34.2 1.9 collective-permute-start.3
  36.1 3.6 %collective-permute-start.4 = (bf16[4,6,4096]{2,1,0:T(8,128)(2,1)S(1)}, bf16[4,6,4096]{2,1,0:T(8,128)(2,1)S(1)}, u32[]{:S(2)}, u32[]{:S(2)}) collective-permute-start(bf16[4,6,4096]{2,1,0:T(8,128)(2,1)S(1)} %broadcast_select_fusion.2), channel_id=1, source_target_pairs={{0,4},{1,5},{2,6},{3,7},{4,0},{5,1},{6,2},{7,3},{8,12},{9,13},{10,... | collective-permute-start | bytes 589832 | tf_op jit(solution)/shard_map/ppermute | solution.py:78
  39.9 4.4 %collective-permute-done.3 = bf16[4,6,4096]{2,1,0:T(8,128)(2,1)S(1)} collective-permute-done((bf16[4,6,4096]{2,1,0:T(8,128)(2,1)S(1)}, bf16[4,6,4096]{2,1,0:T(8,128)(2,1)S(1)}, u32[]{:S(2)}, u32[]{:S(2)}) %collective-permute-start.3) | collective-permute-done | bytes 196640 | tf_op jit(solution)/shard_map/ppermute | solution.py:78
  44.2 3.8 %collective-permute-done.4 = bf16[4,6,4096]{2,1,0:T(8,128)(2,1)S(1)} collective-permute-done((bf16[4,6,4096]{2,1,0:T(8,128)(2,1)S(1)}, bf16[4,6,4096]{2,1,0:T(8,128)(2,1)S(1)}, u32[]{:S(2)}, u32[]{:S(2)}) %collective-permute-start.4) | collective-permute-done | bytes 196640 | tf_op jit(solution)/shard_map/ppermute | solution.py:78
  50.6 5.7 %collective-permute-start.6 = (bf16[4,4,6,4096]{3,1,2,0:T(4,128)(2,1)S(1)}, bf16[4,4,6,4096]{3,1,2,0:T(4,128)(2,1)S(1)}, u32[]{:S(2)}, u32[]{:S(2)}) collective-permute-start(bf16[4,4,6,4096]{3,1,2,0:T(4,128)(2,1)S(1)} %broadcast_select_fusion.1), channel_id=1, source_target_pairs={{0,1},{1,0},{2,3},{3,2},{4,5},{5,4},{6,7},{7,6},{8,9},{9,8},{10,11... | collective-permute-start | bytes 2359304 | tf_op jit(solution)/shard_map/ppermute | solution.py:78
  59.1 3.0 %gather_fusion.2 = bf16[2,4,4,6,4096]{4,2,3,1,0:T(4,128)(2,1)} fusion(bf16[2,4,4,6,4096]{4,2,3,1,0:T(4,128)(2,1)S(1)} %pad_maximum_fusion, s32[1024]{0:T(1024)S(1)} %pad_clamp_fusion), kind=kCustom, calls=%fused_computation.4 | custom fusion | bytes 3145736 | tf_op jit(solution)/shard_map/jit(_take)/gather | solution.py:81
  62.1 3.2 %bitcast_reduce_fusion = (f32[2,4,4,6]{1,3,2,0:T(8,128)S(1)}, bf16[2,4,4,6,4096]{4,2,3,1,0:T(4,128)(2,1)S(1)}) fusion(bf16[2,4,4,6,4096]{4,2,3,1,0:T(4,128)(2,1)} %gather_fusion.2, pred[2]{0:T(512)(128)(4,1)S(1)} %compare_and_fusion.2), kind=kLoop, calls=%fused_computation.14 | loop fusion | flops 2359104 | bytes 3146498 | tf_op jit(solution)/shard_map/reduce_sum | solution.py:18
  66.5 2.1 fusion.10
  68.6 2.2 copy.49
  70.8 3.7 %convert_element_type.77 = bf16[192,4096]{1,0:T(8,128)(2,1)} reshape(bf16[2,4,4,6,4096]{4,3,2,1,0:T(8,128)(2,1)} %copy.49) | data formatting | bytes 3145728 | tf_op jit(solution)/shard_map/convert_element_type | solution.py:140
  74.5 2.2 copy.51
  76.7 2.8 %convert_element_type.83 = bf16[192,4096]{1,0:T(8,128)(2,1)S(1)} reshape(bf16[2,4,4,6,4096]{4,3,2,1,0:T(8,128)(2,1)} %copy.51) | data formatting | bytes 3145728 | tf_op jit(solution)/shard_map/convert_element_type | solution.py:141
  79.5 30.7 %all-gather.5.cloned.1.call-done = bf16[4096,896]{1,0:T(8,128)(2,1)} async-done(((bf16[256,896]{1,0:T(8,128)(2,1)}), bf16[4096,896]{1,0:T(8,128)(2,1)}) %all-gather.5.cloned.1.call-update) | async-done | bytes 7340048 | tf_op jit(solution)/shard_map/all_gather | solution.py:132
  110.2 2.3 slice.57
  112.5 2.7 %slice.65 = bf16[16,256,512]{2,1,0:T(8,128)(2,1)S(1)} slice(bf16[16,256,896]{2,1,0:T(8,128)(2,1)} %bitcast.63), slice={[0:16], [0:256], [384:896]} | slice | bytes 8388608 | tf_op jit(solution)/shard_map/slice | solution.py:138
  117.2 2.7 %fusion.91 = (f32[192]{0:T(256)S(1)}, f32[192,6144]{1,0:T(8,128)S(1)}) fusion(bf16[6144,128]{1,0:T(8,128)(2,1)S(1)} %copy-done, bf16[192,96]{0,1:T(8,128)(2,1)S(1)} %get-tuple-element.16, bf16[192,16]{0,1:T(8,128)(2,1)S(1)} %get-tuple-element.15, bf16[192,16]{0,1:T(8,128)(2,1)S(1)} %get-tuple-element.12, pred[6144]{0:T(1024)(128)(4,1)S(1)} %broadcast_compare_fusion, ...), kind=kOutput, calls=%fused_computation.173 | convolution fusion | flops 313933632 | bytes 6398208 | tf_op jit(solution)/shard_map/dot_general | solution.py:156
  122.3 1.8 fusion.30
  124.1 60.7 %all-gather.7.cloned.1.call-done = bf16[10240,256]{1,0:T(8,128)(2,1)} async-done(((bf16[640,256]{1,0:T(8,128)(2,1)}), bf16[10240,256]{1,0:T(8,128)(2,1)}) %all-gather.7.cloned.1.call-update) | async-done | bytes 5242896 | tf_op jit(solution)/shard_map/all_gather | solution.py:133
  184.9 3.5 %convolution_convert_fusion = bf16[96,16,256]{2,0,1:T(8,128)(2,1)S(1)} fusion(bf16[16,640,256]{2,1,0:T(8,128)(2,1)} %bitcast.60, s32[]{:T(128)S(6)} %select_n.214, bf16[192,512]{1,0:T(8,128)(2,1)S(1)} %fusion.30, bf16[192,128]{1,0:T(8,128)(2,1)S(1)} %fusion.25), kind=kOutput, calls=%fused_computation.30 | convolution fusion | flops 503955456 | bytes 6275076 | tf_op jit(solution)/shard_map/dot_general | solution.py:180
  191.0 9.1 %collective-permute-start.7 = (bf16[16,6,4096]{2,0,1:T(8,128)(2,1)}, bf16[16,6,4096]{2,0,1:T(8,128)(2,1)}, u32[]{:S(2)}, u32[]{:S(2)}) collective-permute-start(bf16[16,6,4096]{2,0,1:T(8,128)(2,1)} %copy.54), channel_id=1, source_target_pairs={{0,1},{1,0},{2,3},{3,2},{4,5},{5,4},{6,7},{7,6},{8,9},{9,8},{10,11... | collective-permute-start | bytes 2359304 | tf_op jit(solution)/shard_map/ppermute | solution.py:183
  200.1 3.6 %fusion.17 = f32[96,16,256]{2,0,1:T(8,128)S(1)} fusion(bf16[16,640,256]{2,1,0:T(8,128)(2,1)} %bitcast.61, s32[]{:T(128)S(6)} %select_n.213, bf16[192,512]{1,0:T(8,128)(2,1)} %copy-done.3, bf16[192,128]{1,0:T(8,128)(2,1)S(1)} %fusion.25), kind=kOutput, calls=%fused_computation.32 | convolution fusion | flops 504348672 | bytes 7061508 | tf_op jit(solution)/shard_map/dot_general | solution.py:180
  204.7 1.8 reshape.321
  206.5 2.3 add_convert_fusion
  208.8 23.2 %all_to_all.5 = bf16[16,6,4096]{2,1,0:T(8,128)(2,1)S(1)} all-to-all(bf16[16,6,4096]{2,1,0:T(8,128)(2,1)S(1)} %add_convert_fusion), channel_id=1, replica_groups={{0,2,4,6,8,10,12,14,16,18,20,22,24,26,28,30},{1,3,5,7,9,11,13,15,17,19,..., dimensions={0} | all-to-all | bytes 1572864 | tf_op jit(solution)/shard_map/all_to_all | solution.py:189
  (103 shorter events, 19.3 us)
Async XLA Ops:
  6.5 110.7 %copy-start = (bf16[6144,128]{1,0:T(8,128)(2,1)S(1)}, bf16[6144,128]{1,0:T(8,128)(2,1)}, u32[]{:S(2)}) copy-start(bf16[6144,128]{1,0:T(8,128)(2,1)} %param.32) | copy-start | bytes 4718596
  6.5 15.6 %copy-start.15 = (s32[192]{0:T(256)S(1)}, s32[192]{0:T(256)}, u32[]{:S(2)}) copy-start(s32[192]{0:T(256)} %constant.259) | copy-start | bytes 2308
  6.5 22.5 %copy-start.4 = (bf16[6,4096]{1,0:T(8,128)(2,1)S(1)}, bf16[6,4096]{1,0:T(8,128)(2,1)}, u32[]{:S(2)}) copy-start(bf16[6,4096]{1,0:T(8,128)(2,1)} %param.19) | copy-start | bytes 147460
  6.5 15.6 %copy-start.18 = (s32[1,33]{1,0:T(1,128)S(1)}, s32[1,33]{1,0:T(1,128)}, u32[]{:S(2)}) copy-start(s32[1,33]{1,0:T(1,128)} %param.34) | copy-start | bytes 400
  6.5 103.7 %all-gather.5.cloned.1.call-start = ((), (), s32[]{:S(2)}) async-start(), calls=%async_computation.1 | async-start | bytes 7798784 | tf_op jit(solution)/shard_map/all_gather | solution.py:132
  8.6 176.3 %all-gather.7.cloned.1.call-start = ((), (), s32[]{:S(2)}) async-start(), calls=%async_computation.2 | async-start | bytes 5570560 | tf_op jit(solution)/shard_map/all_gather | solution.py:133
  8.6 20.4 %collective-permute-start = (bf16[6,4096]{1,0:T(8,128)(2,1)}, bf16[6,4096]{1,0:T(8,128)(2,1)S(1)}, u32[]{:S(2)}, u32[]{:S(2)}) collective-permute-start(bf16[6,4096]{1,0:T(8,128)(2,1)} %param.19), channel_id=1, source_target_pairs={{0,8},{1,9},{2,10},{3,11},{4,12},{5,13},{6,14},{7,15},{8,16},{9,17... | collective-permute-start | bytes 147464 | tf_op jit(solution)/shard_map/ppermute | solution.py:78
  12.7 16.4 %collective-permute-start.1 = (bf16[6,4096]{1,0:T(8,128)(2,1)}, bf16[6,4096]{1,0:T(8,128)(2,1)S(1)}, u32[]{:S(2)}, u32[]{:S(2)}) collective-permute-start(bf16[6,4096]{1,0:T(8,128)(2,1)} %param.19), channel_id=1, source_target_pairs={{0,16},{1,17},{2,18},{3,19},{4,20},{5,21},{6,22},{7,23},{8,24},{9,... | collective-permute-start | bytes 147464 | tf_op jit(solution)/shard_map/ppermute | solution.py:78
  17.2 11.8 %collective-permute-start.2 = (bf16[6,4096]{1,0:T(8,128)(2,1)}, bf16[6,4096]{1,0:T(8,128)(2,1)S(1)}, u32[]{:S(2)}, u32[]{:S(2)}) collective-permute-start(bf16[6,4096]{1,0:T(8,128)(2,1)} %param.19), channel_id=1, source_target_pairs={{0,24},{1,25},{2,26},{3,27},{4,28},{5,29},{6,30},{7,31},{8,0},{9,1... | collective-permute-start | bytes 147464 | tf_op jit(solution)/shard_map/ppermute | solution.py:78
  25.1 3.9 %copy-start.13 = (s32[192]{0:T(256)}, s32[192]{0:T(256)S(1)}, u32[]{:S(2)}) copy-start(s32[192]{0:T(256)S(1)} %gather_fusion.4) | copy-start | bytes 2308
  29.8 10.1 %collective-permute-start.5 = (bf16[4,6,4096]{2,1,0:T(8,128)(2,1)S(1)}, bf16[4,6,4096]{2,1,0:T(8,128)(2,1)S(1)}, u32[]{:S(2)}, u32[]{:S(2)}) collective-permute-start(bf16[4,6,4096]{2,1,0:T(8,128)(2,1)S(1)} %broadcast_select_fusion.2), channel_id=1, source_target_pairs={{0,6},{1,7},{2,0},{3,1},{4,2},{5,3},{6,4},{7,5},{8,14},{9,15},{10,... | collective-permute-start | bytes 589832 | tf_op jit(solution)/shard_map/ppermute | solution.py:78
  34.2 10.0 %collective-permute-start.3 = (bf16[4,6,4096]{2,1,0:T(8,128)(2,1)S(1)}, bf16[4,6,4096]{2,1,0:T(8,128)(2,1)S(1)}, u32[]{:S(2)}, u32[]{:S(2)}) collective-permute-start(bf16[4,6,4096]{2,1,0:T(8,128)(2,1)S(1)} %broadcast_select_fusion.2), channel_id=1, source_target_pairs={{0,2},{1,3},{2,4},{3,5},{4,6},{5,7},{6,0},{7,1},{8,10},{9,11},{10,... | collective-permute-start | bytes 589832 | tf_op jit(solution)/shard_map/ppermute | solution.py:78
  36.1 11.9 %collective-permute-start.4 = (bf16[4,6,4096]{2,1,0:T(8,128)(2,1)S(1)}, bf16[4,6,4096]{2,1,0:T(8,128)(2,1)S(1)}, u32[]{:S(2)}, u32[]{:S(2)}) collective-permute-start(bf16[4,6,4096]{2,1,0:T(8,128)(2,1)S(1)} %broadcast_select_fusion.2), channel_id=1, source_target_pairs={{0,4},{1,5},{2,6},{3,7},{4,0},{5,1},{6,2},{7,3},{8,12},{9,13},{10,... | collective-permute-start | bytes 589832 | tf_op jit(solution)/shard_map/ppermute | solution.py:78
  50.6 7.4 %collective-permute-start.6 = (bf16[4,4,6,4096]{3,1,2,0:T(4,128)(2,1)S(1)}, bf16[4,4,6,4096]{3,1,2,0:T(4,128)(2,1)S(1)}, u32[]{:S(2)}, u32[]{:S(2)}) collective-permute-start(bf16[4,4,6,4096]{3,1,2,0:T(4,128)(2,1)S(1)} %broadcast_select_fusion.1), channel_id=1, source_target_pairs={{0,1},{1,0},{2,3},{3,2},{4,5},{5,4},{6,7},{7,6},{8,9},{9,8},{10,11... | collective-permute-start | bytes 2359304 | tf_op jit(solution)/shard_map/ppermute | solution.py:78
  62.1 4.4 %copy-start.6 = (f32[4096]{0:T(1024)S(1)}, f32[4096]{0:T(1024)}, u32[]{:S(2)}) copy-start(f32[4096]{0:T(1024)} %param.21) | copy-start | bytes 49156
  62.1 4.4 %copy-start.7 = (f32[4096]{0:T(1024)S(1)}, f32[4096]{0:T(1024)}, u32[]{:S(2)}) copy-start(f32[4096]{0:T(1024)} %param.20) | copy-start | bytes 49156
  62.1 4.4 %copy-start.8 = (f32[4096]{0:T(1024)S(1)}, f32[4096]{0:T(1024)}, u32[]{:S(2)}) copy-start(f32[4096]{0:T(1024)} %param.23) | copy-start | bytes 49156
  62.1 4.4 %copy-start.9 = (f32[4096]{0:T(1024)S(1)}, f32[4096]{0:T(1024)}, u32[]{:S(2)}) copy-start(f32[4096]{0:T(1024)} %param.22) | copy-start | bytes 49156
  112.5 2.8 %copy-start.1 = (bf16[192,4096]{1,0:T(8,128)(2,1)S(1)}, bf16[192,4096]{1,0:T(8,128)(2,1)}, u32[]{:S(2)}) copy-start(bf16[192,4096]{1,0:T(8,128)(2,1)} %convert_element_type.77) | copy-start | bytes 4718596
  112.5 2.8 %copy-start.19 = (f32[384]{0:T(512)S(1)}, f32[384]{0:T(512)}, u32[]{:S(2)}) copy-start(f32[384]{0:T(512)} %param.25) | copy-start | bytes 4612
  115.2 1.5 copy-start.12
  115.2 1.5 copy-start.17
  115.3 1.7 copy-start.14
  115.3 1.7 copy-start.16
  115.3 1.7 copy-start.21
  115.3 1.9 copy-start.5
  120.0 1.4 copy-start.2
  121.4 0.9 copy-start.20
  124.1 60.7 %copy-start.3 = (bf16[192,512]{1,0:T(8,128)(2,1)}, bf16[192,512]{1,0:T(8,128)(2,1)S(1)}, u32[]{:S(2)}) copy-start(bf16[192,512]{1,0:T(8,128)(2,1)S(1)} %fusion.30) | copy-start | bytes 589828
  191.0 15.5 %collective-permute-start.7 = (bf16[16,6,4096]{2,0,1:T(8,128)(2,1)}, bf16[16,6,4096]{2,0,1:T(8,128)(2,1)}, u32[]{:S(2)}, u32[]{:S(2)}) collective-permute-start(bf16[16,6,4096]{2,0,1:T(8,128)(2,1)} %copy.54), channel_id=1, source_target_pairs={{0,1},{1,0},{2,3},{3,2},{4,5},{5,4},{6,7},{7,6},{8,9},{9,8},{10,11... | collective-permute-start | bytes 2359304 | tf_op jit(solution)/shard_map/ppermute | solution.py:183
  208.8 23.5 %copy-start.10 = (f32[4096]{0:T(1024)S(1)}, f32[4096]{0:T(1024)}, u32[]{:S(2)}) copy-start(f32[4096]{0:T(1024)} %param.31) | copy-start | bytes 49156
  208.8 23.5 %copy-start.11 = (f32[4096]{0:T(1024)S(1)}, f32[4096]{0:T(1024)}, u32[]{:S(2)}) copy-start(f32[4096]{0:T(1024)} %param.27) | copy-start | bytes 49156
Sparse Core Ops, SparseCore 0:
  9.5 100.7 all-gather.4
  112.3 72.5 all-gather.6

commit v11 on v8

--- a/solution.py
+++ b/solution.py
@@ -84,7 +84,8 @@
 def head_gather(block):
     by_y = gather_stage(block, 4, 8)
     by_x = gather_stage(by_y, 4, 2)
-    by_core = gather_stage(by_x, 2, 1)
+    partner = lax.ppermute(by_x, "head", stage_pairs(2, 1, 1, lax.axis_size("head")))
+    by_core = jnp.stack([by_x, partner])
     ordered = by_core.transpose((0, 2, 1) + tuple(range(3, by_core.ndim)))
     return ordered.reshape((-1,) + block.shape[1:])
 
@@ -144,7 +145,9 @@
     upward = jnp.dot(normed_two, up_full, preferred_element_type=jnp.float32)
     lengths_row = cache_lengths[0]
     query_owner, query_place = token_layout(lengths_row, rows_total)
-    source = np.arange(rows_total).reshape(4, 4, 2, -1).transpose(2, 0, 1, 3).reshape(-1)
+    source = np.arange(rows_total).reshape(4, 4, 2, -1).transpose(2, 0, 1, 3)
+    core = lax.axis_index("head") % 2
+    source = jnp.where(core == 0, source.reshape(-1), source[::-1].reshape(-1))
     query_owner = jnp.take(query_owner, source)
     query_place = jnp.take(query_place, source)
     queries = rotate(projected[:, :HD], query_place).astype(jnp.bfloat16)
@@ -175,9 +178,8 @@
     partial = partial.reshape(rows_total, -1)
     heads = lax.axis_size("head")
     blocks = partial.astype(jnp.bfloat16).reshape(2, heads // 2, tokens.shape[0], -1)
-    core = lax.axis_index("head") % 2
-    mine = lax.dynamic_index_in_dim(blocks, core, 0, keepdims=False)
-    theirs = lax.dynamic_index_in_dim(blocks, 1 - core, 0, keepdims=False)
+    mine = blocks[0]
+    theirs = blocks[1]
     swapped = lax.ppermute(
         theirs, "head", [(index, index ^ 1) for index in range(heads)]
     )

time: 238 us -> 240 us (level)
    ppermute x7 -> x6, starting transfers between devices: 27.2 us -> 21.5 us  [gather_stage(): lax.ppermute(stacked, 'head', stage_pairs(size, stride, shift, total))]
    ppermute x0 -> x1, starting transfers between devices: none -> 5.53 us  [head_gather(): lax.ppermute(by_x, 'head', stage_pairs(2, 1, 1, lax.axis_size('head')))]
    all_gather x1, waiting for transfers between devices: 33.5 us -> 37.6 us  [body(): lax.all_gather(jnp.concatenate([w_qkv, w_up], axis=1), 'tok', axis=0, til...]
    gather x3 -> x2, local copies, waits for them, and re-layouts: 4.78 us -> 1.78 us  [gather_stage(): jnp.take(jnp.stack(received), (sub - jnp.arange(size)) % size, axis=0)]
    ppermute x7 -> x6, waiting for transfers between devices: 9.45 us -> 8.16 us  [gather_stage(): lax.ppermute(stacked, 'head', stage_pairs(size, stride, shift, total))]
  transfers between devices with their start and end apart: 10 -> 10, of which waited for: 6 -> 5; matrix products, arithmetic and copies ran while one was open for 19% -> 18% of each run, Pallas kernels for 0% -> 0%
where the time goes in v11:
time: 240 us; the launch traced here: 239 us
  waiting for transfers between devices  108 us (45%)
  starting transfers between devices  36.2 us (15%)
  local copies, waits for them, and re-layouts  28.6 us (12%)
  blocking collectives  23.2 us (10%)
  other arithmetic  17.9 us (7%)
  between operations  14 us (6%)
  matrix products  11.2 us (5%)
    all_gather x1, waiting for transfers between devices, body(): lax.all_gather(jnp.concatenate([w_dense, w_down], axis=0), 'tok', axis=0,...  60.9 us
    all_gather x1, waiting for transfers between devices, body(): lax.all_gather(jnp.concatenate([w_qkv, w_up], axis=1), 'tok', axis=0, til...  37.6 us
    all_to_all x1, blocking collectives, body(): lax.all_to_all(chip_sum, 'head', 0, 0, axis_index_groups=groups, tiled=True)  23.2 us
    ppermute x6, starting transfers between devices, gather_stage(): lax.ppermute(stacked, 'head', stage_pairs(size, stride, shift, total))  21.5 us
    ppermute x1, starting transfers between devices, body(): lax.ppermute(theirs, 'head', [(index, index ^ 1) for index in range(heads)])  9.11 us
    ppermute x6, waiting for transfers between devices, gather_stage(): lax.ppermute(stacked, 'head', stage_pairs(size, stride, shift, total))  8.16 us
    convert_element_type x2, local copies, waits for them, and re-layouts, body(): normed_one = layer_norm(whole, ln1_gain, ln1_bias).astype(jnp.bfloat16)  5.9 us
    ppermute x1, starting transfers between devices, head_gather(): lax.ppermute(by_x, 'head', stage_pairs(2, 1, 1, lax.axis_size('head')))  5.53 us
  transfers between devices with their start and end apart: 10, of which 5 were waited for; matrix products, arithmetic and copies ran while one was open for 18% of the time, Pallas kernels for 0%

profile of v11, /device:TPU:1, one launch (start us, length us, event | category | flops | bytes accessed | tf_op | source)
XLA Modules:
  0.0 239.3 jit_solution(12400566450064290654)
XLA Ops:
  6.6 2.0 pad_maximum_fusion.2
  8.6 4.0 %collective-permute-start = (bf16[6,4096]{1,0:T(8,128)(2,1)}, bf16[6,4096]{1,0:T(8,128)(2,1)S(1)}, u32[]{:S(2)}, u32[]{:S(2)}) collective-permute-start(bf16[6,4096]{1,0:T(8,128)(2,1)} %param.20), channel_id=1, source_target_pairs={{0,8},{1,9},{2,10},{3,11},{4,12},{5,13},{6,14},{7,15},{8,16},{9,17... | collective-permute-start | bytes 147464 | tf_op jit(solution)/shard_map/ppermute | solution.py:78
  12.7 4.5 %collective-permute-start.1 = (bf16[6,4096]{1,0:T(8,128)(2,1)}, bf16[6,4096]{1,0:T(8,128)(2,1)S(1)}, u32[]{:S(2)}, u32[]{:S(2)}) collective-permute-start(bf16[6,4096]{1,0:T(8,128)(2,1)} %param.20), channel_id=1, source_target_pairs={{0,16},{1,17},{2,18},{3,19},{4,20},{5,21},{6,22},{7,23},{8,24},{9,... | collective-permute-start | bytes 147464 | tf_op jit(solution)/shard_map/ppermute | solution.py:78
  17.2 3.0 %collective-permute-start.2 = (bf16[6,4096]{1,0:T(8,128)(2,1)}, bf16[6,4096]{1,0:T(8,128)(2,1)S(1)}, u32[]{:S(2)}, u32[]{:S(2)}) collective-permute-start(bf16[6,4096]{1,0:T(8,128)(2,1)} %param.20), channel_id=1, source_target_pairs={{0,24},{1,25},{2,26},{3,27},{4,28},{5,29},{6,30},{7,31},{8,0},{9,1... | collective-permute-start | bytes 147464 | tf_op jit(solution)/shard_map/ppermute | solution.py:78
  20.2 1.7 pad_maximum_fusion.3
  24.4 1.6 gather_fusion.2
  26.1 1.6 gather_fusion.3
  29.0 4.4 %collective-permute-start.5 = (bf16[4,6,4096]{2,1,0:T(8,128)(2,1)S(1)}, bf16[4,6,4096]{2,1,0:T(8,128)(2,1)S(1)}, u32[]{:S(2)}, u32[]{:S(2)}) collective-permute-start(bf16[4,6,4096]{2,1,0:T(8,128)(2,1)S(1)} %broadcast_select_fusion.1), channel_id=1, source_target_pairs={{0,6},{1,7},{2,0},{3,1},{4,2},{5,3},{6,4},{7,5},{8,14},{9,15},{10,... | collective-permute-start | bytes 589832 | tf_op jit(solution)/shard_map/ppermute | solution.py:78
  33.4 1.9 collective-permute-start.3
  35.3 3.6 %collective-permute-start.4 = (bf16[4,6,4096]{2,1,0:T(8,128)(2,1)S(1)}, bf16[4,6,4096]{2,1,0:T(8,128)(2,1)S(1)}, u32[]{:S(2)}, u32[]{:S(2)}) collective-permute-start(bf16[4,6,4096]{2,1,0:T(8,128)(2,1)S(1)} %broadcast_select_fusion.1), channel_id=1, source_target_pairs={{0,4},{1,5},{2,6},{3,7},{4,0},{5,1},{6,2},{7,3},{8,12},{9,13},{10,... | collective-permute-start | bytes 589832 | tf_op jit(solution)/shard_map/ppermute | solution.py:78
  39.0 4.4 %collective-permute-done.3 = bf16[4,6,4096]{2,1,0:T(8,128)(2,1)S(1)} collective-permute-done((bf16[4,6,4096]{2,1,0:T(8,128)(2,1)S(1)}, bf16[4,6,4096]{2,1,0:T(8,128)(2,1)S(1)}, u32[]{:S(2)}, u32[]{:S(2)}) %collective-permute-start.3) | collective-permute-done | bytes 196640 | tf_op jit(solution)/shard_map/ppermute | solution.py:78
  43.4 3.8 %collective-permute-done.4 = bf16[4,6,4096]{2,1,0:T(8,128)(2,1)S(1)} collective-permute-done((bf16[4,6,4096]{2,1,0:T(8,128)(2,1)S(1)}, bf16[4,6,4096]{2,1,0:T(8,128)(2,1)S(1)}, u32[]{:S(2)}, u32[]{:S(2)}) %collective-permute-start.4) | collective-permute-done | bytes 196640 | tf_op jit(solution)/shard_map/ppermute | solution.py:78
  49.8 5.5 %collective-permute-start.6 = (bf16[4,4,6,4096]{3,1,2,0:T(4,128)(2,1)S(1)}, bf16[4,4,6,4096]{3,1,2,0:T(4,128)(2,1)S(1)}, u32[]{:S(2)}, u32[]{:S(2)}) collective-permute-start(bf16[4,4,6,4096]{3,1,2,0:T(4,128)(2,1)S(1)} %broadcast_select_fusion), channel_id=1, source_target_pairs={{0,1},{1,0},{2,3},{3,2},{4,5},{5,4},{6,7},{7,6},{8,9},{9,8},{10,11... | collective-permute-start | bytes 2359304 | tf_op jit(solution)/shard_map/ppermute | solution.py:87
  55.7 1.5 collective-permute-done.6
  59.5 2.2 fusion.10
  61.7 2.2 copy.50
  64.0 3.7 %convert_element_type.76 = bf16[192,4096]{1,0:T(8,128)(2,1)} reshape(bf16[2,4,4,6,4096]{4,3,2,1,0:T(8,128)(2,1)} %copy.50) | data formatting | bytes 3145728 | tf_op jit(solution)/shard_map/convert_element_type | solution.py:141
  67.6 2.2 copy.52
  69.9 2.7 %convert_element_type.82 = bf16[192,4096]{1,0:T(8,128)(2,1)S(1)} reshape(bf16[2,4,4,6,4096]{4,3,2,1,0:T(8,128)(2,1)} %copy.52) | data formatting | bytes 3145728 | tf_op jit(solution)/shard_map/convert_element_type | solution.py:142
  72.6 37.6 %all-gather.5.cloned.1.call-done = bf16[4096,896]{1,0:T(8,128)(2,1)} async-done(((bf16[256,896]{1,0:T(8,128)(2,1)}), bf16[4096,896]{1,0:T(8,128)(2,1)}) %all-gather.5.cloned.1.call-update) | async-done | bytes 7340048 | tf_op jit(solution)/shard_map/all_gather | solution.py:133
  110.2 2.3 slice.67
  112.5 2.7 %slice.75 = bf16[16,256,512]{2,1,0:T(8,128)(2,1)S(1)} slice(bf16[16,256,896]{2,1,0:T(8,128)(2,1)} %bitcast.55), slice={[0:16], [0:256], [384:896]} | slice | bytes 8388608 | tf_op jit(solution)/shard_map/slice | solution.py:139
  115.2 1.4 fusion.81
  117.1 2.7 %fusion.82 = (f32[192]{0:T(256)S(1)}, f32[192,6144]{1,0:T(8,128)S(1)}) fusion(bf16[6144,128]{1,0:T(8,128)(2,1)S(1)} %copy-done, bf16[192,96]{0,1:T(8,128)(2,1)S(1)} %get-tuple-element.18, bf16[192,16]{0,1:T(8,128)(2,1)S(1)} %get-tuple-element.17, bf16[192,16]{0,1:T(8,128)(2,1)S(1)} %get-tuple-element.14, pred[6144]{0:T(1024)(128)(4,1)S(1)} %broadcast_compare_fusion, ...), kind=kOutput, calls=%fused_computation.155 | convolution fusion | flops 313933632 | bytes 6398208 | tf_op jit(solution)/shard_map/dot_general | solution.py:159
  122.2 1.8 fusion.29
  123.9 60.9 %all-gather.7.cloned.1.call-done = bf16[10240,256]{1,0:T(8,128)(2,1)} async-done(((bf16[640,256]{1,0:T(8,128)(2,1)}), bf16[10240,256]{1,0:T(8,128)(2,1)}) %all-gather.7.cloned.1.call-update) | async-done | bytes 5242896 | tf_op jit(solution)/shard_map/all_gather | solution.py:134
  184.9 3.9 %convolution_convert_fusion = bf16[192,16,256]{2,0,1:T(8,128)(2,1)S(1)} fusion(bf16[16,640,256]{2,1,0:T(8,128)(2,1)} %bitcast.59, bf16[192,512]{1,0:T(8,128)(2,1)S(1)} %fusion.29, bf16[192,128]{1,0:T(8,128)(2,1)S(1)} %fusion.24), kind=kOutput, calls=%fused_computation.27 | convolution fusion | flops 1007910912 | bytes 7061504 | tf_op jit(solution)/shard_map/dot_general | solution.py:177
  192.7 9.1 %collective-permute-start.7 = (bf16[16,6,4096]{2,0,1:T(8,128)(2,1)}, bf16[16,6,4096]{2,0,1:T(8,128)(2,1)}, u32[]{:S(2)}, u32[]{:S(2)}) collective-permute-start(bf16[16,6,4096]{2,0,1:T(8,128)(2,1)} %copy.55), channel_id=1, source_target_pairs={{0,1},{1,0},{2,3},{3,2},{4,5},{5,4},{6,7},{7,6},{8,9},{9,8},{10,11... | collective-permute-start | bytes 2359304 | tf_op jit(solution)/shard_map/ppermute | solution.py:183
  201.9 2.3 copy.53
  204.2 1.8 reshape.274
  206.0 2.3 add_convert_fusion
  208.4 23.2 %all_to_all.5 = bf16[16,6,4096]{2,1,0:T(8,128)(2,1)S(1)} all-to-all(bf16[16,6,4096]{2,1,0:T(8,128)(2,1)S(1)} %add_convert_fusion), channel_id=1, replica_groups={{0,2,4,6,8,10,12,14,16,18,20,22,24,26,28,30},{1,3,5,7,9,11,13,15,17,19,..., dimensions={0} | all-to-all | bytes 1572864 | tf_op jit(solution)/shard_map/all_to_all | solution.py:188
  (86 shorter events, 16.6 us)
Async XLA Ops:
  6.5 110.6 %copy-start = (bf16[6144,128]{1,0:T(8,128)(2,1)S(1)}, bf16[6144,128]{1,0:T(8,128)(2,1)}, u32[]{:S(2)}) copy-start(bf16[6144,128]{1,0:T(8,128)(2,1)} %param.33) | copy-start | bytes 4718596
  6.5 21.6 %copy-start.10 = (s32[192]{0:T(256)S(1)}, s32[192]{0:T(256)}, u32[]{:S(2)}) copy-start(s32[192]{0:T(256)} %constant.201.clone) | copy-start | bytes 2308
  6.5 21.6 %copy-start.11 = (s32[192]{0:T(256)S(1)}, s32[192]{0:T(256)}, u32[]{:S(2)}) copy-start(s32[192]{0:T(256)} %constant.202.clone) | copy-start | bytes 2308
  6.5 21.7 %copy-start.3 = (bf16[6,4096]{1,0:T(8,128)(2,1)S(1)}, bf16[6,4096]{1,0:T(8,128)(2,1)}, u32[]{:S(2)}) copy-start(bf16[6,4096]{1,0:T(8,128)(2,1)} %param.20) | copy-start | bytes 147460
  6.5 21.1 %copy-start.12 = (s32[1,33]{1,0:T(1,128)S(1)}, s32[1,33]{1,0:T(1,128)}, u32[]{:S(2)}) copy-start(s32[1,33]{1,0:T(1,128)} %param.35) | copy-start | bytes 400
  6.6 103.7 %all-gather.5.cloned.1.call-start = ((), (), s32[]{:S(2)}) async-start(), calls=%async_computation.1 | async-start | bytes 7798784 | tf_op jit(solution)/shard_map/all_gather | solution.py:133
  8.6 176.3 %all-gather.7.cloned.1.call-start = ((), (), s32[]{:S(2)}) async-start(), calls=%async_computation.2 | async-start | bytes 5570560 | tf_op jit(solution)/shard_map/all_gather | solution.py:134
  8.6 19.5 %collective-permute-start = (bf16[6,4096]{1,0:T(8,128)(2,1)}, bf16[6,4096]{1,0:T(8,128)(2,1)S(1)}, u32[]{:S(2)}, u32[]{:S(2)}) collective-permute-start(bf16[6,4096]{1,0:T(8,128)(2,1)} %param.20), channel_id=1, source_target_pairs={{0,8},{1,9},{2,10},{3,11},{4,12},{5,13},{6,14},{7,15},{8,16},{9,17... | collective-permute-start | bytes 147464 | tf_op jit(solution)/shard_map/ppermute | solution.py:78
  12.7 15.5 %collective-permute-start.1 = (bf16[6,4096]{1,0:T(8,128)(2,1)}, bf16[6,4096]{1,0:T(8,128)(2,1)S(1)}, u32[]{:S(2)}, u32[]{:S(2)}) collective-permute-start(bf16[6,4096]{1,0:T(8,128)(2,1)} %param.20), channel_id=1, source_target_pairs={{0,16},{1,17},{2,18},{3,19},{4,20},{5,21},{6,22},{7,23},{8,24},{9,... | collective-permute-start | bytes 147464 | tf_op jit(solution)/shard_map/ppermute | solution.py:78
  17.2 11.0 %collective-permute-start.2 = (bf16[6,4096]{1,0:T(8,128)(2,1)}, bf16[6,4096]{1,0:T(8,128)(2,1)S(1)}, u32[]{:S(2)}, u32[]{:S(2)}) collective-permute-start(bf16[6,4096]{1,0:T(8,128)(2,1)} %param.20), channel_id=1, source_target_pairs={{0,24},{1,25},{2,26},{3,27},{4,28},{5,29},{6,30},{7,31},{8,0},{9,1... | collective-permute-start | bytes 147464 | tf_op jit(solution)/shard_map/ppermute | solution.py:78
  29.0 10.1 %collective-permute-start.5 = (bf16[4,6,4096]{2,1,0:T(8,128)(2,1)S(1)}, bf16[4,6,4096]{2,1,0:T(8,128)(2,1)S(1)}, u32[]{:S(2)}, u32[]{:S(2)}) collective-permute-start(bf16[4,6,4096]{2,1,0:T(8,128)(2,1)S(1)} %broadcast_select_fusion.1), channel_id=1, source_target_pairs={{0,6},{1,7},{2,0},{3,1},{4,2},{5,3},{6,4},{7,5},{8,14},{9,15},{10,... | collective-permute-start | bytes 589832 | tf_op jit(solution)/shard_map/ppermute | solution.py:78
  33.4 10.1 %collective-permute-start.3 = (bf16[4,6,4096]{2,1,0:T(8,128)(2,1)S(1)}, bf16[4,6,4096]{2,1,0:T(8,128)(2,1)S(1)}, u32[]{:S(2)}, u32[]{:S(2)}) collective-permute-start(bf16[4,6,4096]{2,1,0:T(8,128)(2,1)S(1)} %broadcast_select_fusion.1), channel_id=1, source_target_pairs={{0,2},{1,3},{2,4},{3,5},{4,6},{5,7},{6,0},{7,1},{8,10},{9,11},{10,... | collective-permute-start | bytes 589832 | tf_op jit(solution)/shard_map/ppermute | solution.py:78
  35.3 11.9 %collective-permute-start.4 = (bf16[4,6,4096]{2,1,0:T(8,128)(2,1)S(1)}, bf16[4,6,4096]{2,1,0:T(8,128)(2,1)S(1)}, u32[]{:S(2)}, u32[]{:S(2)}) collective-permute-start(bf16[4,6,4096]{2,1,0:T(8,128)(2,1)S(1)} %broadcast_select_fusion.1), channel_id=1, source_target_pairs={{0,4},{1,5},{2,6},{3,7},{4,0},{5,1},{6,2},{7,3},{8,12},{9,13},{10,... | collective-permute-start | bytes 589832 | tf_op jit(solution)/shard_map/ppermute | solution.py:78
  49.3 10.1 %copy-start.4 = (f32[4096]{0:T(1024)S(1)}, f32[4096]{0:T(1024)}, u32[]{:S(2)}) copy-start(f32[4096]{0:T(1024)} %param.22) | copy-start | bytes 49156
  49.3 10.1 %copy-start.5 = (f32[4096]{0:T(1024)S(1)}, f32[4096]{0:T(1024)}, u32[]{:S(2)}) copy-start(f32[4096]{0:T(1024)} %param.21) | copy-start | bytes 49156
  49.3 10.1 %copy-start.6 = (f32[4096]{0:T(1024)S(1)}, f32[4096]{0:T(1024)}, u32[]{:S(2)}) copy-start(f32[4096]{0:T(1024)} %param.24) | copy-start | bytes 49156
  49.3 10.1 %copy-start.7 = (f32[4096]{0:T(1024)S(1)}, f32[4096]{0:T(1024)}, u32[]{:S(2)}) copy-start(f32[4096]{0:T(1024)} %param.23) | copy-start | bytes 49156
  49.8 7.4 %collective-permute-start.6 = (bf16[4,4,6,4096]{3,1,2,0:T(4,128)(2,1)S(1)}, bf16[4,4,6,4096]{3,1,2,0:T(4,128)(2,1)S(1)}, u32[]{:S(2)}, u32[]{:S(2)}) collective-permute-start(bf16[4,4,6,4096]{3,1,2,0:T(4,128)(2,1)S(1)} %broadcast_select_fusion), channel_id=1, source_target_pairs={{0,1},{1,0},{2,3},{3,2},{4,5},{5,4},{6,7},{7,6},{8,9},{9,8},{10,11... | collective-permute-start | bytes 2359304 | tf_op jit(solution)/shard_map/ppermute | solution.py:87
  112.5 2.8 %copy-start.1 = (bf16[192,4096]{1,0:T(8,128)(2,1)S(1)}, bf16[192,4096]{1,0:T(8,128)(2,1)}, u32[]{:S(2)}) copy-start(bf16[192,4096]{1,0:T(8,128)(2,1)} %convert_element_type.76) | copy-start | bytes 4718596
  112.5 2.8 %copy-start.13 = (f32[384]{0:T(512)S(1)}, f32[384]{0:T(512)}, u32[]{:S(2)}) copy-start(f32[384]{0:T(512)} %param.26) | copy-start | bytes 4612
  119.8 1.4 copy-start.2
  121.2 0.9 copy-start.14
  192.7 13.3 %collective-permute-start.7 = (bf16[16,6,4096]{2,0,1:T(8,128)(2,1)}, bf16[16,6,4096]{2,0,1:T(8,128)(2,1)}, u32[]{:S(2)}, u32[]{:S(2)}) collective-permute-start(bf16[16,6,4096]{2,0,1:T(8,128)(2,1)} %copy.55), channel_id=1, source_target_pairs={{0,1},{1,0},{2,3},{3,2},{4,5},{5,4},{6,7},{7,6},{8,9},{9,8},{10,11... | collective-permute-start | bytes 2359304 | tf_op jit(solution)/shard_map/ppermute | solution.py:183
  206.0 25.8 %copy-start.8 = (f32[4096]{0:T(1024)S(1)}, f32[4096]{0:T(1024)}, u32[]{:S(2)}) copy-start(f32[4096]{0:T(1024)} %param.32) | copy-start | bytes 49156
  206.0 25.8 %copy-start.9 = (f32[4096]{0:T(1024)S(1)}, f32[4096]{0:T(1024)}, u32[]{:S(2)}) copy-start(f32[4096]{0:T(1024)} %param.28) | copy-start | bytes 49156
Sparse Core Ops, SparseCore 0:
  9.5 100.7 all-gather.4
  112.3 72.5 all-gather.6
